TPU v7x, 512 devices: a whole 4x4x16 slice. The times are simulated.
512 devices in a mesh: pair: 32 (over z_lo, y), loop: 16 (over x, z_hi, core).
Axes of the slice: x: 4, y: 4, z: 16 (z_hi: 2, z_lo: 8; z = z_hi * 8 + z_lo), core: 2. Of those that a mesh axis runs over, the one named last changes fastest.
Arguments:
- amplitudes: float32 [8192, 8192], P('pair', 'loop'), may hold values from -6 to 6
- integrals: float32 [2048, 8192], P(None, 'loop'), may hold values from -0.0625 to 0.0625
- pair_partner: int32 [8192], P('pair'), may hold values from 0 to 8191, as said below
- virtual_swap: int32 [2048], P('loop'), may hold values from 0 to 2047, as said below
Outputs:
- ladder_sym: float32 [2048, 8192], P('loop', 'pair')
Inputs may be any that keep to these rules, and one draw needn't show every extreme that they name: pair_partner[pair_partner[p]] = p, and pair_partner[p] lies in the aligned block of 256 pairs that starts 8192 / 2 pairs further on, counted modulo 8192. virtual_swap[virtual_swap[k]] = k, virtual_swap[k] != k, and virtual_swap[k] lies in the same aligned block of 64 ab pairs as k.
All inputs are finite; a program needn't handle non-finite values.
Results may differ from a plain program's by a relative error of at most 0.000071.
Values sent between devices are 32-bit elements; how exact they have to be, the bound alone decides.
No kernel may reach another device: no remote copies, remote signals or barrier semaphores. Data moves between devices by JAX's collectives and lax.ppermute only.
A program may use at most 64 MiB of HBM per device.

v0:
```python
import jax
import jax.numpy as jnp
from jax import lax
from jax.sharding import PartitionSpec as P


def shifted(x, axis, by):
    count = lax.axis_size(axis)
    return lax.ppermute(x, axis, [(i, (i + by) % count) for i in range(count)])


def local(amplitudes, integrals, pair_partner, virtual_swap):
    loop_count = lax.axis_size("loop")
    pair_count = lax.axis_size("pair")
    ab_local = integrals.shape[0] // loop_count
    ij_local = amplitudes.shape[0]
    slab = lax.all_to_all(integrals, "loop", split_axis=0, concat_axis=1, tiled=True)
    ladder = lax.dot_general(
        slab,
        lax.all_gather(amplitudes, "loop", axis=1, tiled=True),
        (((1,), (1,)), ((), ())),
        precision=lax.Precision.HIGHEST,
        preferred_element_type=jnp.float32,
    )
    mirror = shifted(ladder, "pair", pair_count // 2)
    swap_local = virtual_swap - lax.axis_index("loop") * ab_local
    partner_local = pair_partner % ij_local
    mirror = jnp.take(jnp.take(mirror, swap_local, axis=0), partner_local, axis=1)
    return ladder + mirror


def solution(mesh):
    in_specs = (P("pair", "loop"), P(None, "loop"), P("pair"), P("loop"))
    out_specs = P("loop", "pair")
    return jax.shard_map(local, mesh=mesh, in_specs=in_specs, out_specs=out_specs, check_vma=False)
```

profile of v0, /device:TPU:1, one launch (start us, length us, event | category | flops | bytes accessed | tf_op | source)
XLA Modules:
  0.0 387.8 jit_solution(8886406078017381639)
XLA Ops:
  6.5 0.0 copy-start.1
  6.5 0.0 copy-start
  6.5 19.2 %all-to-all-start = ((f32[16,128,512]{2,1,0:T(8,128)}), f32[16,128,512]{2,1,0:T(8,128)}, u32[]{:S(2)}, u32[]{:S(2)}) async-start(f32[16,128,512]{2,1,0:T(8,128)} %bitcast.8), calls=%async_computation | async-start | bytes 8388608 | tf_op jit(solution)/shard_map/all_to_all | solution.py:17
  25.7 0.0 all-gather.2.cloned.1.call-start
  25.8 0.7 all-gather.2.cloned.1.call-update
  26.5 0.0 copy-done.1
  26.5 0.0 copy-done
  26.5 115.3 %all-to-all-done = f32[16,128,512]{2,1,0:T(8,128)} async-done(((f32[16,128,512]{2,1,0:T(8,128)}), f32[16,128,512]{2,1,0:T(8,128)}, u32[]{:S(2)}, u32[]{:S(2)}) %all-to-all-start) | async-done | bytes 4194336 | tf_op jit(solution)/shard_map/all_to_all | solution.py:17
  141.8 5.3 %copy.9 = f32[128,16,512]{0,2,1:T(8,128)} copy(f32[128,16,512]{2,0,1:T(8,128)} %bitcast.1) | data formatting | bytes 8388608 | tf_op jit(solution)/shard_map/all_to_all | solution.py:17
  147.1 166.5 %all-gather.2.cloned.1.call-done = f32[256,8192]{1,0:T(8,128)} async-done(((f32[256,512]{1,0:T(8,128)}), f32[256,8192]{1,0:T(8,128)}) %all-gather.2.cloned.1.call-update) | async-done | bytes 8388624 | tf_op jit(solution)/shard_map/all_gather | solution.py:20
  313.6 11.4 %fusion.1 = f32[128,256]{1,0:T(8,128)S(1)} fusion(f32[128,8192]{0,1:T(8,128)} %bitcast.7, f32[256,8192]{1,0:T(8,128)} %all-gather.2.cloned.1.call-done), kind=kOutput, calls=%fused_computation.14 | convolution fusion | flops 3221225472 | bytes 12713984 | tf_op jit(solution)/shard_map/dot_general | solution.py:18
  325.0 49.9 %collective-permute-start = (f32[128,256]{1,0:T(8,128)S(1)}, f32[128,256]{1,0:T(8,128)S(1)}, u32[]{:S(2)}, u32[]{:S(2)}) collective-permute-start(f32[128,256]{1,0:T(8,128)S(1)} %fusion.1), channel_id=1, source_target_pairs={{0,256},{16,272},{32,288},{48,304},{64,320},{80,336},{96,352},{112... | collective-permute-start | bytes 393224 | tf_op jit(solution)/shard_map/ppermute | solution.py:9
  374.9 3.5 collective-permute-done
  378.5 0.8 gather_fusion
  379.2 0.1 broadcast_select_fusion
  379.3 0.1 copy.10
  379.4 0.7 gather_fusion.1
  380.2 0.1 copy.11
  380.3 0.7 bitcast_add_fusion
  (4 shorter events, 0.0 us)
Async XLA Ops:
  6.5 19.9 %copy-start.1 = (s32[128]{0:T(128)S(1)}, s32[128]{0:T(128)}, u32[]{:S(2)}) copy-start(s32[128]{0:T(128)} %param.7) | copy-start | bytes 1540
  6.5 20.0 %copy-start = (s32[256]{0:T(256)S(1)}, s32[256]{0:T(256)}, u32[]{:S(2)}) copy-start(s32[256]{0:T(256)} %param.6) | copy-start | bytes 3076
  6.5 135.3 %all-to-all-start = ((f32[16,128,512]{2,1,0:T(8,128)}), f32[16,128,512]{2,1,0:T(8,128)}, u32[]{:S(2)}, u32[]{:S(2)}) async-start(f32[16,128,512]{2,1,0:T(8,128)} %bitcast.8), calls=%async_computation | async-start | bytes 8388608 | tf_op jit(solution)/shard_map/all_to_all | solution.py:17
  25.7 287.9 %all-gather.2.cloned.1.call-start = ((), (), s32[]{:S(2)}) async-start(), calls=%async_computation.1 | async-start | bytes 8912896 | tf_op jit(solution)/shard_map/all_gather | solution.py:20
  325.0 53.5 %collective-permute-start = (f32[128,256]{1,0:T(8,128)S(1)}, f32[128,256]{1,0:T(8,128)S(1)}, u32[]{:S(2)}, u32[]{:S(2)}) collective-permute-start(f32[128,256]{1,0:T(8,128)S(1)} %fusion.1), channel_id=1, source_target_pairs={{0,256},{16,272},{32,288},{48,304},{64,320},{80,336},{96,352},{112... | collective-permute-start | bytes 393224 | tf_op jit(solution)/shard_map/ppermute | solution.py:9
Sparse Core Ops, SparseCore 0:
  29.9 283.7 all-gather.1
where the time goes:
time: 388 us
  waiting for transfers between devices  286 us (74%)
  starting transfers between devices  69.1 us (18%)
  between operations  13.5 us (3%)
  matrix products  11.4 us (3%)
  local copies, waits for them, and re-layouts  6.99 us (2%)
    all_gather x1, waiting for transfers between devices, local(): lax.all_gather(amplitudes, 'loop', axis=1, tiled=True)  167 us
    all_to_all x1, waiting for transfers between devices, local(): lax.all_to_all(integrals, 'loop', split_axis=0, concat_axis=1, tiled=True)  115 us
    ppermute x1, starting transfers between devices, shifted(): return lax.ppermute(x, axis, [(i, (i + by) % count) for i in range(count)])  49.9 us
    all_to_all x1, starting transfers between devices, local(): lax.all_to_all(integrals, 'loop', split_axis=0, concat_axis=1, tiled=True)  19.2 us
    dot_general x1, matrix products, local(): lax.dot_general(slab, lax.all_gather(amplitudes, 'loop', axis=1, tiled=Tr...  11.4 us
  transfers between devices with their start and end apart: 3, of which 3 were waited for; matrix products, arithmetic and copies ran while one was open for 1% of the time, Pallas kernels for 0%

commit v1 on v0

--- a/solution.py
+++ b/solution.py
@@ -14,14 +14,14 @@
     pair_count = lax.axis_size("pair")
     ab_local = integrals.shape[0] // loop_count
     ij_local = amplitudes.shape[0]
-    slab = lax.all_to_all(integrals, "loop", split_axis=0, concat_axis=1, tiled=True)
-    ladder = lax.dot_general(
-        slab,
-        lax.all_gather(amplitudes, "loop", axis=1, tiled=True),
+    partial = lax.dot_general(
+        integrals,
+        amplitudes,
         (((1,), (1,)), ((), ())),
         precision=lax.Precision.HIGHEST,
         preferred_element_type=jnp.float32,
     )
+    ladder = lax.psum_scatter(partial, "loop", scatter_dimension=0, tiled=True)
     mirror = shifted(ladder, "pair", pair_count // 2)
     swap_local = virtual_swap - lax.axis_index("loop") * ab_local
     partner_local = pair_partner % ij_local

time: 388 us -> 167 us (0.43)
  waiting for transfers between devices: 286 us -> 140 us
  starting transfers between devices: 69.1 us -> 1.91 us
  matrix products: 11.4 us -> 7.03 us
  local copies, waits for them, and re-layouts: 6.99 us -> 2.71 us
    all_gather x1 -> x0, waiting for transfers between devices: 167 us -> none  [local(): lax.all_gather(amplitudes, 'loop', axis=1, tiled=True)]
    reduce_scatter x0 -> x1, waiting for transfers between devices: none -> 126 us  [local(): ladder = lax.psum_scatter(partial, 'loop', scatter_dimension=0, tiled=True)]
    all_to_all x1 -> x0, waiting for transfers between devices: 115 us -> none  [local(): lax.all_to_all(integrals, 'loop', split_axis=0, concat_axis=1, tiled=True)]
    ppermute x1, starting transfers between devices: 49.9 us -> 1.91 us  [shifted(): return lax.ppermute(x, axis, [(i, (i + by) % count) for i in range(count)])]
    all_to_all x1 -> x0, starting transfers between devices: 19.2 us -> none  [local(): lax.all_to_all(integrals, 'loop', split_axis=0, concat_axis=1, tiled=True)]
    ppermute x1, waiting for transfers between devices: 3.55 us -> 13.7 us  [shifted(): return lax.ppermute(x, axis, [(i, (i + by) % count) for i in range(count)])]
    all_to_all x1 -> x0, local copies, waits for them, and re-layouts: 5.31 us -> none  [local(): lax.all_to_all(integrals, 'loop', split_axis=0, concat_axis=1, tiled=True)]
    dot_general x1, matrix products: 11.4 us -> 7.03 us  [local(): lax.dot_general(integrals, amplitudes, (((1,), (1,)), ((), ())), precisio...]
  transfers between devices with their start and end apart: 3 -> 2, of which waited for: 3 -> 2; matrix products, arithmetic and copies ran while one was open for 1% -> 0% of each run, Pallas kernels for 0% -> 0%
where the time goes in v1:
time: 167 us
  waiting for transfers between devices  140 us (84%)
  between operations  13.5 us (8%)
  matrix products  7.03 us (4%)
  local copies, waits for them, and re-layouts  2.71 us (2%)
  starting transfers between devices  1.91 us (1%)
  other arithmetic  1.7 us (1%)
    reduce_scatter x1, waiting for transfers between devices, local(): ladder = lax.psum_scatter(partial, 'loop', scatter_dimension=0, tiled=True)  126 us
    ppermute x1, waiting for transfers between devices, shifted(): return lax.ppermute(x, axis, [(i, (i + by) % count) for i in range(count)])  13.7 us
    dot_general x1, matrix products, local(): lax.dot_general(integrals, amplitudes, (((1,), (1,)), ((), ())), precisio...  7.03 us
  transfers between devices with their start and end apart: 2, of which 2 were waited for; matrix products, arithmetic and copies ran while one was open for 0% of the time, Pallas kernels for 0%

profile of v1, /device:TPU:1, one launch (start us, length us, event | category | flops | bytes accessed | tf_op | source)
XLA Modules:
  0.0 167.0 jit_solution(8803851358384577752)
XLA Ops:
  6.5 0.0 copy-start
  6.5 0.0 copy-start.2
  6.5 0.0 copy-start.1
  6.5 0.0 reduce-scatter.2.cloned.1.call-start
  6.5 1.0 copy-done
  7.6 7.0 %fusion.1 = f32[2048,256]{1,0:T(8,128)} fusion(f32[2048,512]{1,0:T(8,128)} %param.5, f32[256,512]{1,0:T(8,128)S(1)} %copy-done), kind=kOutput, calls=%fused_computation.14 | convolution fusion | flops 3221225472 | bytes 6815744 | tf_op jit(solution)/shard_map/dot_general | solution.py:17
  14.6 0.0 reduce-scatter.2.cloned.1.call-update
  14.6 0.0 copy-done.2
  14.7 0.0 copy-done.1
  14.7 126.5 %reduce-scatter.2.cloned.1.call-done = f32[128,256]{1,0:T(8,128)} async-done(((f32[2048,256]{1,0:T(8,128)}), f32[128,256]{1,0:T(8,128)}) %reduce-scatter.2.cloned.1.call-update) | async-done | bytes 131088 | tf_op jit(solution)/shard_map/reduce_scatter | solution.py:24
  141.2 1.9 %collective-permute-start = (f32[128,256]{1,0:T(8,128)}, f32[128,256]{1,0:T(8,128)S(1)}, u32[]{:S(2)}, u32[]{:S(2)}) collective-permute-start(f32[128,256]{1,0:T(8,128)} %reduce-scatter.2.cloned.1.call-done), channel_id=1, source_target_pairs={{0,256},{16,272},{32,288},{48,304},{64,320},{80,336},{96,352},{112... | collective-permute-start | bytes 393224 | tf_op jit(solution)/shard_map/ppermute | solution.py:9
  143.1 13.7 %collective-permute-done = f32[128,256]{1,0:T(8,128)S(1)} collective-permute-done((f32[128,256]{1,0:T(8,128)}, f32[128,256]{1,0:T(8,128)S(1)}, u32[]{:S(2)}, u32[]{:S(2)}) %collective-permute-start) | collective-permute-done | bytes 131104 | tf_op jit(solution)/shard_map/ppermute | solution.py:9
  156.8 0.8 gather_fusion
  157.5 0.1 broadcast_select_fusion
  157.6 0.1 copy.5
  157.7 0.7 gather_fusion.1
  158.5 0.1 copy.6
  158.6 1.6 bitcast_add_fusion
  (4 shorter events, 0.0 us)
Async XLA Ops:
  6.5 1.0 copy-start
  6.5 8.1 %copy-start.2 = (s32[128]{0:T(128)S(1)}, s32[128]{0:T(128)}, u32[]{:S(2)}) copy-start(s32[128]{0:T(128)} %param.7) | copy-start | bytes 1540
  6.5 8.1 %copy-start.1 = (s32[256]{0:T(256)S(1)}, s32[256]{0:T(256)}, u32[]{:S(2)}) copy-start(s32[256]{0:T(256)} %param.6) | copy-start | bytes 3076
  6.5 134.6 %reduce-scatter.2.cloned.1.call-start = ((), (), s32[]{:S(2)}) async-start(), calls=%async_computation.1 | async-start | bytes 2228224 | tf_op jit(solution)/shard_map/reduce_scatter | solution.py:24
  141.2 15.6 %collective-permute-start = (f32[128,256]{1,0:T(8,128)}, f32[128,256]{1,0:T(8,128)S(1)}, u32[]{:S(2)}, u32[]{:S(2)}) collective-permute-start(f32[128,256]{1,0:T(8,128)} %reduce-scatter.2.cloned.1.call-done), channel_id=1, source_target_pairs={{0,256},{16,272},{32,288},{48,304},{64,320},{80,336},{96,352},{112... | collective-permute-start | bytes 393224 | tf_op jit(solution)/shard_map/ppermute | solution.py:9
Sparse Core Ops, SparseCore 0:
  14.8 126.3 reduce-scatter.1

commit v2 on v1

v2 whole, which is shorter than its diff:
```python
import jax
import jax.numpy as jnp
from jax import lax
from jax.sharding import PartitionSpec as P

X, ZH, CORE = 4, 2, 2


def moved(x, axis, target):
    count = lax.axis_size(axis)
    return lax.ppermute(x, axis, [(i, target(i)) for i in range(count)])


def local(amplitudes, integrals, pair_partner, virtual_swap):
    loop_count = lax.axis_size("loop")
    pair_count = lax.axis_size("pair")
    ab_local = integrals.shape[0] // loop_count
    ij_local = amplitudes.shape[0]
    j = lax.axis_index("loop")
    x, zh, c = j // (ZH * CORE), (j // CORE) % ZH, j % CORE
    partial = lax.dot_general(
        integrals,
        amplitudes,
        (((1,), (1,)), ((), ())),
        precision=lax.Precision.HIGHEST,
        preferred_element_type=jnp.float32,
    )
    part = partial.reshape(X, ZH, CORE, ab_local, ij_local)
    keep = lax.dynamic_index_in_dim(part, c, axis=2, keepdims=False)
    give = lax.dynamic_index_in_dim(part, 1 - c, axis=2, keepdims=False)
    s1 = keep + moved(give, "loop", lambda i: i ^ 1)
    s2 = lax.dynamic_index_in_dim(s1, x, axis=0, keepdims=False)
    for shift in range(1, X):
        out = lax.dynamic_index_in_dim(s1, (x + shift) % X, axis=0, keepdims=False)
        s2 = s2 + moved(out, "loop", lambda i, s=shift: (((i // 4) + s) % X) * 4 + i % 4)
    mine = lax.dynamic_index_in_dim(s2, zh, axis=0, keepdims=False)
    other = lax.dynamic_index_in_dim(s2, 1 - zh, axis=0, keepdims=False)
    half = pair_count // 2
    from_zh = moved(other, "loop", lambda i: i ^ 2)
    from_pair = moved(mine, "pair", lambda i: (i + half) % pair_count)
    from_diag = moved(
        other,
        ("pair", "loop"),
        lambda i: ((i // loop_count + half) % pair_count) * loop_count + ((i % loop_count) ^ 2),
    )
    ladder = mine + from_zh
    mirror = from_pair + from_diag
    swap_local = virtual_swap - j * ab_local
    partner_local = pair_partner % ij_local
    mirror = jnp.take(jnp.take(mirror, swap_local, axis=0), partner_local, axis=1)
    return ladder + mirror


def solution(mesh):
    in_specs = (P("pair", "loop"), P(None, "loop"), P("pair"), P("loop"))
    out_specs = P("loop", "pair")
    return jax.shard_map(local, mesh=mesh, in_specs=in_specs, out_specs=out_specs, check_vma=False)
```

time: 167 us -> 78.7 us (0.47)
  the two profiles are of different devices: /device:TPU:1 before, /device:TPU:115 now
where the time goes in v2:
time: 78.7 us; the launch traced here: 78.3 us
  waiting for transfers between devices  33.7 us (43%)
  starting transfers between devices  30.9 us (39%)
  matrix products  5.28 us (7%)
  local copies, waits for them, and re-layouts  4.9 us (6%)
  other arithmetic  3.2 us (4%)
    ppermute x7, waiting for transfers between devices, moved(): return lax.ppermute(x, axis, [(i, target(i)) for i in range(count)])  33.7 us
    ppermute x7, starting transfers between devices, moved(): return lax.ppermute(x, axis, [(i, target(i)) for i in range(count)])  30.9 us
    dot_general x1, matrix products, local(): lax.dot_general(integrals, amplitudes, (((1,), (1,)), ((), ())), precisio...  5.28 us
    unnamed x8, local copies, waits for them, and re-layouts  2.03 us
  transfers between devices with their start and end apart: 7, of which 5 were waited for; matrix products, arithmetic and copies ran while one was open for 2% of the time, Pallas kernels for 0%

profile of v2, /device:TPU:115, one launch (start us, length us, event | category | flops | bytes accessed | tf_op | source)
XLA Modules:
  0.0 78.3 jit_solution(2896977552705066475)
XLA Ops:
  0.0 1.0 %copy-done = f32[256,512]{1,0:T(8,128)S(1)} copy-done((f32[256,512]{1,0:T(8,128)S(1)}, f32[256,512]{1,0:T(8,128)}, u32[]{:S(2)}) %copy-start) | copy-done | bytes 524312
  1.0 5.3 %fusion.3 = f32[2048,256]{1,0:T(8,128)S(1)} fusion(f32[2048,512]{1,0:T(8,128)} %param.5, f32[256,512]{1,0:T(8,128)S(1)} %copy-done), kind=kOutput, calls=%fused_computation.24 | convolution fusion | flops 3221225472 | bytes 6815744 | tf_op jit(solution)/shard_map/dot_general | solution.py:21
  6.4 1.1 %dynamic-slice_bitcast_fusion = f32[4,2,128,256]{3,2,1,0:T(8,128)} fusion(f32[4,2,2,128,256]{4,3,2,1,0:T(8,128)S(1)} %bitcast.25, s32[]{:T(128)S(6)} %select_n.83), kind=kLoop, calls=%fused_computation.3 | loop fusion | bytes 2097156 | tf_op jit(solution)/shard_map/jit(dynamic_index_in_dim)/squeeze | solution.py:30
  7.5 2.6 %collective-permute-start = (f32[4,2,128,256]{3,2,1,0:T(8,128)}, f32[4,2,128,256]{3,2,1,0:T(8,128)}, u32[]{:S(2)}, u32[]{:S(2)}) collective-permute-start(f32[4,2,128,256]{3,2,1,0:T(8,128)} %dynamic-slice_bitcast_fusion), channel_id=1, source_target_pairs={{0,1},{1,0},{2,3},{3,2},{4,5},{5,4},{6,7},{7,6},{8,9},{9,8},{10,11... | collective-permute-start | bytes 3145736 | tf_op jit(solution)/shard_map/ppermute | solution.py:11
  10.1 2.5 %collective-permute-done = f32[4,2,128,256]{3,2,1,0:T(8,128)} collective-permute-done((f32[4,2,128,256]{3,2,1,0:T(8,128)}, f32[4,2,128,256]{3,2,1,0:T(8,128)}, u32[]{:S(2)}, u32[]{:S(2)}) %collective-permute-start) | collective-permute-done | bytes 1048608 | tf_op jit(solution)/shard_map/ppermute | solution.py:11
  12.6 1.4 %bitcast_add_fusion = f32[4,2,128,256]{3,2,1,0:T(8,128)S(1)} fusion(f32[4,2,128,256]{3,2,1,0:T(8,128)} %collective-permute-done, f32[4,2,2,128,256]{4,3,2,1,0:T(8,128)S(1)} %bitcast.26, s32[]{:T(128)S(6)} %select_n.82), kind=kLoop, calls=%fused_computation.2 | loop fusion | flops 262144 | bytes 3145732 | tf_op jit(solution)/shard_map/add | solution.py:31
  14.0 1.0 %copy-done.1 = f32[4,2,128,256]{3,2,1,0:T(8,128)} copy-done((f32[4,2,128,256]{3,2,1,0:T(8,128)}, f32[4,2,128,256]{3,2,1,0:T(8,128)S(1)}, u32[]{:S(2)}) %copy-start.1) | copy-done | bytes 1048600
  15.1 3.1 %collective-permute-start.1 = (f32[2,128,256]{2,1,0:T(8,128)S(1)}, f32[2,128,256]{2,1,0:T(8,128)S(1)}, u32[]{:S(2)}, u32[]{:S(2)}) collective-permute-start(f32[2,128,256]{2,1,0:T(8,128)S(1)} %get-tuple-element.9), channel_id=1, source_target_pairs={{0,4},{1,5},{2,6},{3,7},{4,8},{5,9},{6,10},{7,11},{8,12},{9,13},{1... | collective-permute-start | bytes 786440 | tf_op jit(solution)/shard_map/ppermute | solution.py:11
  18.2 2.7 %collective-permute-start.2 = (f32[2,128,256]{2,1,0:T(8,128)S(1)}, f32[2,128,256]{2,1,0:T(8,128)S(1)}, u32[]{:S(2)}, u32[]{:S(2)}) collective-permute-start(f32[2,128,256]{2,1,0:T(8,128)S(1)} %get-tuple-element.11), channel_id=1, source_target_pairs={{0,8},{1,9},{2,10},{3,11},{4,12},{5,13},{6,14},{7,15},{8,0},{9,1},... | collective-permute-start | bytes 786440 | tf_op jit(solution)/shard_map/ppermute | solution.py:11
  20.9 3.8 %collective-permute-start.3 = (f32[2,128,256]{2,1,0:T(8,128)S(1)}, f32[2,128,256]{2,1,0:T(8,128)S(1)}, u32[]{:S(2)}, u32[]{:S(2)}) collective-permute-start(f32[2,128,256]{2,1,0:T(8,128)S(1)} %get-tuple-element.10), channel_id=1, source_target_pairs={{0,12},{1,13},{2,14},{3,15},{4,0},{5,1},{6,2},{7,3},{8,4},{9,5},{1... | collective-permute-start | bytes 786440 | tf_op jit(solution)/shard_map/ppermute | solution.py:11
  24.8 4.0 %collective-permute-done.2 = f32[2,128,256]{2,1,0:T(8,128)S(1)} collective-permute-done((f32[2,128,256]{2,1,0:T(8,128)S(1)}, f32[2,128,256]{2,1,0:T(8,128)S(1)}, u32[]{:S(2)}, u32[]{:S(2)}) %collective-permute-start.2) | collective-permute-done | bytes 262176 | tf_op jit(solution)/shard_map/ppermute | solution.py:11
  28.8 6.6 %collective-permute-done.3 = f32[2,128,256]{2,1,0:T(8,128)S(1)} collective-permute-done((f32[2,128,256]{2,1,0:T(8,128)S(1)}, f32[2,128,256]{2,1,0:T(8,128)S(1)}, u32[]{:S(2)}, u32[]{:S(2)}) %collective-permute-start.3) | collective-permute-done | bytes 262176 | tf_op jit(solution)/shard_map/ppermute | solution.py:11
  35.4 1.0 %fusion.1 = f32[2,128,256]{2,1,0:T(8,128)S(1)} fusion(f32[2,128,256]{2,1,0:T(8,128)S(1)} %collective-permute-done.3, f32[2,128,256]{2,1,0:T(8,128)S(1)} %collective-permute-done.2, f32[2,128,256]{2,1,0:T(8,128)S(1)} %collective-permute-done.1, f32[4,2,128,256]{3,2,1,0:T(8,128)} %copy-done.1, s32[]{:T(128)S(6)} %select_n.85), kind=kLoop, calls=%fused_computation.6 | loop fusion | flops 196608 | bytes 1310724 | tf_op jit(solution)/shard_map/add | solution.py:35
  36.5 8.8 %collective-permute-start.5 = (f32[128,256]{1,0:T(8,128)S(1)}, f32[128,256]{1,0:T(8,128)S(1)}, u32[]{:S(2)}, u32[]{:S(2)}) collective-permute-start(f32[128,256]{1,0:T(8,128)S(1)} %get-tuple-element.13), channel_id=1, source_target_pairs={{0,256},{16,272},{32,288},{48,304},{64,320},{80,336},{96,352},{112... | collective-permute-start | bytes 393224 | tf_op jit(solution)/shard_map/ppermute | solution.py:11
  45.3 6.1 %collective-permute-start.6 = (f32[128,256]{1,0:T(8,128)S(1)}, f32[128,256]{1,0:T(8,128)S(1)}, u32[]{:S(2)}, u32[]{:S(2)}) collective-permute-start(f32[128,256]{1,0:T(8,128)S(1)} %get-tuple-element.12), channel_id=1, source_target_pairs={{0,258},{1,259},{2,256},{3,257},{4,262},{5,263},{6,260},{7,261},{8... | collective-permute-start | bytes 393224 | tf_op jit(solution)/shard_map/ppermute | solution.py:11
  51.5 3.7 %collective-permute-start.4 = (f32[128,256]{1,0:T(8,128)S(1)}, f32[128,256]{1,0:T(8,128)S(1)}, u32[]{:S(2)}, u32[]{:S(2)}) collective-permute-start(f32[128,256]{1,0:T(8,128)S(1)} %get-tuple-element.12), channel_id=1, source_target_pairs={{0,2},{1,3},{2,0},{3,1},{4,6},{5,7},{6,4},{7,5},{8,10},{9,11},{10,... | collective-permute-start | bytes 393224 | tf_op jit(solution)/shard_map/ppermute | solution.py:11
  55.2 0.4 collective-permute-done.5
  55.7 20.1 %collective-permute-done.6 = f32[128,256]{1,0:T(8,128)S(1)} collective-permute-done((f32[128,256]{1,0:T(8,128)S(1)}, f32[128,256]{1,0:T(8,128)S(1)}, u32[]{:S(2)}, u32[]{:S(2)}) %collective-permute-start.6) | collective-permute-done | bytes 131104 | tf_op jit(solution)/shard_map/ppermute | solution.py:11
  75.8 0.8 gather_fusion
  76.6 0.1 broadcast_select_fusion
  76.7 0.1 copy.5
  76.8 0.7 gather_fusion.1
  77.5 0.1 copy.6
  77.6 0.7 bitcast_add_fusion.2
  (15 shorter events, 0.2 us)
Async XLA Ops:
  0.0 1.0 %copy-start = (f32[256,512]{1,0:T(8,128)S(1)}, f32[256,512]{1,0:T(8,128)}, u32[]{:S(2)}) copy-start(f32[256,512]{1,0:T(8,128)} %param.4) | copy-start | bytes 1572868
  6.3 18.4 %copy-start.3 = (s32[128]{0:T(128)S(1)}, s32[128]{0:T(128)}, u32[]{:S(2)}) copy-start(s32[128]{0:T(128)} %param.7) | copy-start | bytes 1540
  6.3 18.5 %copy-start.2 = (s32[256]{0:T(256)S(1)}, s32[256]{0:T(256)}, u32[]{:S(2)}) copy-start(s32[256]{0:T(256)} %param.6) | copy-start | bytes 3076
  7.5 5.2 %collective-permute-start = (f32[4,2,128,256]{3,2,1,0:T(8,128)}, f32[4,2,128,256]{3,2,1,0:T(8,128)}, u32[]{:S(2)}, u32[]{:S(2)}) collective-permute-start(f32[4,2,128,256]{3,2,1,0:T(8,128)} %dynamic-slice_bitcast_fusion), channel_id=1, source_target_pairs={{0,1},{1,0},{2,3},{3,2},{4,5},{5,4},{6,7},{7,6},{8,9},{9,8},{10,11... | collective-permute-start | bytes 3145736 | tf_op jit(solution)/shard_map/ppermute | solution.py:11
  14.0 1.0 %copy-start.1 = (f32[4,2,128,256]{3,2,1,0:T(8,128)}, f32[4,2,128,256]{3,2,1,0:T(8,128)S(1)}, u32[]{:S(2)}) copy-start(f32[4,2,128,256]{3,2,1,0:T(8,128)S(1)} %bitcast_add_fusion) | copy-start | bytes 3145732
  15.1 9.8 %collective-permute-start.1 = (f32[2,128,256]{2,1,0:T(8,128)S(1)}, f32[2,128,256]{2,1,0:T(8,128)S(1)}, u32[]{:S(2)}, u32[]{:S(2)}) collective-permute-start(f32[2,128,256]{2,1,0:T(8,128)S(1)} %get-tuple-element.9), channel_id=1, source_target_pairs={{0,4},{1,5},{2,6},{3,7},{4,8},{5,9},{6,10},{7,11},{8,12},{9,13},{1... | collective-permute-start | bytes 786440 | tf_op jit(solution)/shard_map/ppermute | solution.py:11
  18.2 10.6 %collective-permute-start.2 = (f32[2,128,256]{2,1,0:T(8,128)S(1)}, f32[2,128,256]{2,1,0:T(8,128)S(1)}, u32[]{:S(2)}, u32[]{:S(2)}) collective-permute-start(f32[2,128,256]{2,1,0:T(8,128)S(1)} %get-tuple-element.11), channel_id=1, source_target_pairs={{0,8},{1,9},{2,10},{3,11},{4,12},{5,13},{6,14},{7,15},{8,0},{9,1},... | collective-permute-start | bytes 786440 | tf_op jit(solution)/shard_map/ppermute | solution.py:11
  20.9 14.5 %collective-permute-start.3 = (f32[2,128,256]{2,1,0:T(8,128)S(1)}, f32[2,128,256]{2,1,0:T(8,128)S(1)}, u32[]{:S(2)}, u32[]{:S(2)}) collective-permute-start(f32[2,128,256]{2,1,0:T(8,128)S(1)} %get-tuple-element.10), channel_id=1, source_target_pairs={{0,12},{1,13},{2,14},{3,15},{4,0},{5,1},{6,2},{7,3},{8,4},{9,5},{1... | collective-permute-start | bytes 786440 | tf_op jit(solution)/shard_map/ppermute | solution.py:11
  36.5 19.2 %collective-permute-start.5 = (f32[128,256]{1,0:T(8,128)S(1)}, f32[128,256]{1,0:T(8,128)S(1)}, u32[]{:S(2)}, u32[]{:S(2)}) collective-permute-start(f32[128,256]{1,0:T(8,128)S(1)} %get-tuple-element.13), channel_id=1, source_target_pairs={{0,256},{16,272},{32,288},{48,304},{64,320},{80,336},{96,352},{112... | collective-permute-start | bytes 393224 | tf_op jit(solution)/shard_map/ppermute | solution.py:11
  45.3 30.5 %collective-permute-start.6 = (f32[128,256]{1,0:T(8,128)S(1)}, f32[128,256]{1,0:T(8,128)S(1)}, u32[]{:S(2)}, u32[]{:S(2)}) collective-permute-start(f32[128,256]{1,0:T(8,128)S(1)} %get-tuple-element.12), channel_id=1, source_target_pairs={{0,258},{1,259},{2,256},{3,257},{4,262},{5,263},{6,260},{7,261},{8... | collective-permute-start | bytes 393224 | tf_op jit(solution)/shard_map/ppermute | solution.py:11
  51.5 26.1 %collective-permute-start.4 = (f32[128,256]{1,0:T(8,128)S(1)}, f32[128,256]{1,0:T(8,128)S(1)}, u32[]{:S(2)}, u32[]{:S(2)}) collective-permute-start(f32[128,256]{1,0:T(8,128)S(1)} %get-tuple-element.12), channel_id=1, source_target_pairs={{0,2},{1,3},{2,0},{3,1},{4,6},{5,7},{6,4},{7,5},{8,10},{9,11},{10,... | collective-permute-start | bytes 393224 | tf_op jit(solution)/shard_map/ppermute | solution.py:11

commit v3 on v2

--- a/solution.py
+++ b/solution.py
@@ -36,18 +36,18 @@
     mine = lax.dynamic_index_in_dim(s2, zh, axis=0, keepdims=False)
     other = lax.dynamic_index_in_dim(s2, 1 - zh, axis=0, keepdims=False)
     half = pair_count // 2
-    from_zh = moved(other, "loop", lambda i: i ^ 2)
-    from_pair = moved(mine, "pair", lambda i: (i + half) % pair_count)
     from_diag = moved(
         other,
         ("pair", "loop"),
         lambda i: ((i // loop_count + half) % pair_count) * loop_count + ((i % loop_count) ^ 2),
     )
-    ladder = mine + from_zh
-    mirror = from_pair + from_diag
     swap_local = virtual_swap - j * ab_local
     partner_local = pair_partner % ij_local
-    mirror = jnp.take(jnp.take(mirror, swap_local, axis=0), partner_local, axis=1)
+    inverse = jnp.zeros((ij_local,), jnp.int32).at[partner_local].set(jnp.arange(ij_local, dtype=jnp.int32))
+    to_pair = jnp.take(jnp.take(mine, swap_local, axis=0), inverse, axis=1) + from_diag
+    from_pair = moved(to_pair, "pair", lambda i: (i + half) % pair_count)
+    ladder = mine + from_pair
+    mirror = jnp.take(jnp.take(from_diag, swap_local, axis=0), partner_local, axis=1)
     return ladder + mirror
 
 

time: 78.7 us -> 80.3 us (1.020)
  the two profiles are of different devices: /device:TPU:115 before, /device:TPU:1 now
where the time goes in v3:
time: 80.3 us; the launch traced here: 78.8 us
  waiting for transfers between devices  31.9 us (40%)
  starting transfers between devices  30.1 us (37%)
  local copies, waits for them, and re-layouts  7.94 us (10%)
  matrix products  5.29 us (7%)
  other arithmetic  3.22 us (4%)
    ppermute x6, waiting for transfers between devices, moved(): return lax.ppermute(x, axis, [(i, target(i)) for i in range(count)])  31.9 us
    ppermute x6, starting transfers between devices, moved(): return lax.ppermute(x, axis, [(i, target(i)) for i in range(count)])  30.1 us
    dot_general x1, matrix products, local(): lax.dot_general(integrals, amplitudes, (((1,), (1,)), ((), ())), precisio...  5.29 us
    unnamed x8, local copies, waits for them, and re-layouts  2.02 us
  transfers between devices with their start and end apart: 6, of which 5 were waited for; matrix products, arithmetic and copies ran while one was open for 4% of the time, Pallas kernels for 0%

profile of v3, /device:TPU:1, one launch (start us, length us, event | category | flops | bytes accessed | tf_op | source)
XLA Modules:
  0.0 78.8 jit_solution(6414651099597408830)
XLA Ops:
  0.0 1.0 %copy-done = f32[256,512]{1,0:T(8,128)S(1)} copy-done((f32[256,512]{1,0:T(8,128)S(1)}, f32[256,512]{1,0:T(8,128)}, u32[]{:S(2)}) %copy-start) | copy-done | bytes 524312
  1.0 5.3 %fusion.5 = f32[2048,256]{1,0:T(8,128)S(1)} fusion(f32[2048,512]{1,0:T(8,128)} %param.9, f32[256,512]{1,0:T(8,128)S(1)} %copy-done), kind=kOutput, calls=%fused_computation.34 | convolution fusion | flops 3221225472 | bytes 6815744 | tf_op jit(solution)/shard_map/dot_general | solution.py:21
  6.4 1.1 %dynamic-slice_bitcast_fusion = f32[4,2,128,256]{3,2,1,0:T(8,128)} fusion(f32[4,2,2,128,256]{4,3,2,1,0:T(8,128)S(1)} %bitcast.27, s32[]{:T(128)S(6)} %select_n.82), kind=kLoop, calls=%fused_computation.6 | loop fusion | bytes 2097156 | tf_op jit(solution)/shard_map/jit(dynamic_index_in_dim)/squeeze | solution.py:30
  7.4 8.7 %collective-permute-start = (f32[4,2,128,256]{3,2,1,0:T(8,128)}, f32[4,2,128,256]{3,2,1,0:T(8,128)}, u32[]{:S(2)}, u32[]{:S(2)}) collective-permute-start(f32[4,2,128,256]{3,2,1,0:T(8,128)} %dynamic-slice_bitcast_fusion), channel_id=1, source_target_pairs={{0,1},{1,0},{2,3},{3,2},{4,5},{5,4},{6,7},{7,6},{8,9},{9,8},{10,11... | collective-permute-start | bytes 3145736 | tf_op jit(solution)/shard_map/ppermute | solution.py:11
  16.3 1.4 %scatter_custom_fusion = s32[256]{0:T(256)S(1)} fusion(s32[256]{0:T(256)S(1)} %get-tuple-element.8, s32[256]{0:T(256)S(1)} %iota.3, s32[]{:T(128)} %constant.112.clone.1), kind=kCustom, calls=%fused_computation.32 | custom fusion | bytes 1028 | tf_op jit(solution)/shard_map/scatter | solution.py:46
  17.7 1.1 %collective-permute-done = f32[4,2,128,256]{3,2,1,0:T(8,128)} collective-permute-done((f32[4,2,128,256]{3,2,1,0:T(8,128)}, f32[4,2,128,256]{3,2,1,0:T(8,128)}, u32[]{:S(2)}, u32[]{:S(2)}) %collective-permute-start) | collective-permute-done | bytes 1048608 | tf_op jit(solution)/shard_map/ppermute | solution.py:11
  18.8 1.4 %bitcast_add_fusion = f32[4,2,128,256]{3,2,1,0:T(8,128)S(1)} fusion(f32[4,2,128,256]{3,2,1,0:T(8,128)} %collective-permute-done, f32[4,2,2,128,256]{4,3,2,1,0:T(8,128)S(1)} %bitcast.28, s32[]{:T(128)S(6)} %select_n.81), kind=kLoop, calls=%fused_computation.5 | loop fusion | flops 262144 | bytes 3145732 | tf_op jit(solution)/shard_map/add | solution.py:31
  20.2 1.0 %copy-done.1 = f32[4,2,128,256]{3,2,1,0:T(8,128)} copy-done((f32[4,2,128,256]{3,2,1,0:T(8,128)}, f32[4,2,128,256]{3,2,1,0:T(8,128)S(1)}, u32[]{:S(2)}) %copy-start.1) | copy-done | bytes 1048600
  21.2 1.9 %collective-permute-start.1 = (f32[2,128,256]{2,1,0:T(8,128)S(1)}, f32[2,128,256]{2,1,0:T(8,128)S(1)}, u32[]{:S(2)}, u32[]{:S(2)}) collective-permute-start(f32[2,128,256]{2,1,0:T(8,128)S(1)} %get-tuple-element.11), channel_id=1, source_target_pairs={{0,4},{1,5},{2,6},{3,7},{4,8},{5,9},{6,10},{7,11},{8,12},{9,13},{1... | collective-permute-start | bytes 786440 | tf_op jit(solution)/shard_map/ppermute | solution.py:11
  23.1 1.9 %collective-permute-start.2 = (f32[2,128,256]{2,1,0:T(8,128)S(1)}, f32[2,128,256]{2,1,0:T(8,128)S(1)}, u32[]{:S(2)}, u32[]{:S(2)}) collective-permute-start(f32[2,128,256]{2,1,0:T(8,128)S(1)} %get-tuple-element.13), channel_id=1, source_target_pairs={{0,8},{1,9},{2,10},{3,11},{4,12},{5,13},{6,14},{7,15},{8,0},{9,1},... | collective-permute-start | bytes 786440 | tf_op jit(solution)/shard_map/ppermute | solution.py:11
  25.1 4.6 %collective-permute-start.3 = (f32[2,128,256]{2,1,0:T(8,128)S(1)}, f32[2,128,256]{2,1,0:T(8,128)S(1)}, u32[]{:S(2)}, u32[]{:S(2)}) collective-permute-start(f32[2,128,256]{2,1,0:T(8,128)S(1)} %get-tuple-element.12), channel_id=1, source_target_pairs={{0,12},{1,13},{2,14},{3,15},{4,0},{5,1},{6,2},{7,3},{8,4},{9,5},{1... | collective-permute-start | bytes 786440 | tf_op jit(solution)/shard_map/ppermute | solution.py:11
  29.7 7.7 %collective-permute-done.1 = f32[2,128,256]{2,1,0:T(8,128)S(1)} collective-permute-done((f32[2,128,256]{2,1,0:T(8,128)S(1)}, f32[2,128,256]{2,1,0:T(8,128)S(1)}, u32[]{:S(2)}, u32[]{:S(2)}) %collective-permute-start.1) | collective-permute-done | bytes 262176 | tf_op jit(solution)/shard_map/ppermute | solution.py:11
  37.4 2.2 %collective-permute-done.3 = f32[2,128,256]{2,1,0:T(8,128)S(1)} collective-permute-done((f32[2,128,256]{2,1,0:T(8,128)S(1)}, f32[2,128,256]{2,1,0:T(8,128)S(1)}, u32[]{:S(2)}, u32[]{:S(2)}) %collective-permute-start.3) | collective-permute-done | bytes 262176 | tf_op jit(solution)/shard_map/ppermute | solution.py:11
  39.7 1.0 %fusion.1 = f32[2,128,256]{2,1,0:T(8,128)S(1)} fusion(f32[2,128,256]{2,1,0:T(8,128)S(1)} %collective-permute-done.3, f32[2,128,256]{2,1,0:T(8,128)S(1)} %collective-permute-done.2, f32[2,128,256]{2,1,0:T(8,128)S(1)} %collective-permute-done.1, f32[4,2,128,256]{3,2,1,0:T(8,128)} %copy-done.1, s32[]{:T(128)S(6)} %select_n.84), kind=kLoop, calls=%fused_computation.9 | loop fusion | flops 196608 | bytes 1310724 | tf_op jit(solution)/shard_map/add | solution.py:35
  40.7 7.1 %collective-permute-start.4 = (f32[128,256]{1,0:T(8,128)S(1)}, f32[128,256]{1,0:T(8,128)S(1)}, u32[]{:S(2)}, u32[]{:S(2)}) collective-permute-start(f32[128,256]{1,0:T(8,128)S(1)} %get-tuple-element.15), channel_id=1, source_target_pairs={{0,258},{1,259},{2,256},{3,257},{4,262},{5,263},{6,260},{7,261},{8... | collective-permute-start | bytes 393224 | tf_op jit(solution)/shard_map/ppermute | solution.py:11
  47.8 0.8 gather_fusion
  48.6 10.4 %collective-permute-done.4 = f32[128,256]{1,0:T(8,128)S(1)} collective-permute-done((f32[128,256]{1,0:T(8,128)S(1)}, f32[128,256]{1,0:T(8,128)S(1)}, u32[]{:S(2)}, u32[]{:S(2)}) %collective-permute-start.4) | collective-permute-done | bytes 131104 | tf_op jit(solution)/shard_map/ppermute | solution.py:11
  59.0 0.8 gather_fusion.2
  59.9 0.7 gather_fusion.1
  60.7 0.1 copy.6
  60.8 5.9 %collective-permute-start.5 = (f32[128,256]{1,0:T(8,128)S(1)}, f32[128,256]{1,0:T(8,128)S(1)}, u32[]{:S(2)}, u32[]{:S(2)}) collective-permute-start(f32[128,256]{1,0:T(8,128)S(1)} %bitcast_add_fusion.3), channel_id=1, source_target_pairs={{0,256},{16,272},{32,288},{48,304},{64,320},{80,336},{96,352},{112... | collective-permute-start | bytes 393224 | tf_op jit(solution)/shard_map/ppermute | solution.py:11
  66.8 0.7 gather_fusion.3
  67.7 10.5 %collective-permute-done.5 = f32[128,256]{1,0:T(8,128)S(1)} collective-permute-done((f32[128,256]{1,0:T(8,128)S(1)}, f32[128,256]{1,0:T(8,128)S(1)}, u32[]{:S(2)}, u32[]{:S(2)}) %collective-permute-start.5) | collective-permute-done | bytes 131104 | tf_op jit(solution)/shard_map/ppermute | solution.py:11
  78.1 0.7 bitcast_add_fusion.2
  (22 shorter events, 0.5 us)
Async XLA Ops:
  0.0 1.0 %copy-start = (f32[256,512]{1,0:T(8,128)S(1)}, f32[256,512]{1,0:T(8,128)}, u32[]{:S(2)}) copy-start(f32[256,512]{1,0:T(8,128)} %param.8) | copy-start | bytes 1572868
  1.0 15.2 %copy-start.2 = (s32[256]{0:T(256)S(1)}, s32[256]{0:T(256)}, u32[]{:S(2)}) copy-start(s32[256]{0:T(256)} %param.10) | copy-start | bytes 3076
  6.3 23.3 %copy-start.3 = (s32[128]{0:T(128)S(1)}, s32[128]{0:T(128)}, u32[]{:S(2)}) copy-start(s32[128]{0:T(128)} %param.11) | copy-start | bytes 1540
  7.4 11.4 %collective-permute-start = (f32[4,2,128,256]{3,2,1,0:T(8,128)}, f32[4,2,128,256]{3,2,1,0:T(8,128)}, u32[]{:S(2)}, u32[]{:S(2)}) collective-permute-start(f32[4,2,128,256]{3,2,1,0:T(8,128)} %dynamic-slice_bitcast_fusion), channel_id=1, source_target_pairs={{0,1},{1,0},{2,3},{3,2},{4,5},{5,4},{6,7},{7,6},{8,9},{9,8},{10,11... | collective-permute-start | bytes 3145736 | tf_op jit(solution)/shard_map/ppermute | solution.py:11
  20.2 1.0 %copy-start.1 = (f32[4,2,128,256]{3,2,1,0:T(8,128)}, f32[4,2,128,256]{3,2,1,0:T(8,128)S(1)}, u32[]{:S(2)}) copy-start(f32[4,2,128,256]{3,2,1,0:T(8,128)S(1)} %bitcast_add_fusion) | copy-start | bytes 3145732
  21.2 16.2 %collective-permute-start.1 = (f32[2,128,256]{2,1,0:T(8,128)S(1)}, f32[2,128,256]{2,1,0:T(8,128)S(1)}, u32[]{:S(2)}, u32[]{:S(2)}) collective-permute-start(f32[2,128,256]{2,1,0:T(8,128)S(1)} %get-tuple-element.11), channel_id=1, source_target_pairs={{0,4},{1,5},{2,6},{3,7},{4,8},{5,9},{6,10},{7,11},{8,12},{9,13},{1... | collective-permute-start | bytes 786440 | tf_op jit(solution)/shard_map/ppermute | solution.py:11
  23.1 14.3 %collective-permute-start.2 = (f32[2,128,256]{2,1,0:T(8,128)S(1)}, f32[2,128,256]{2,1,0:T(8,128)S(1)}, u32[]{:S(2)}, u32[]{:S(2)}) collective-permute-start(f32[2,128,256]{2,1,0:T(8,128)S(1)} %get-tuple-element.13), channel_id=1, source_target_pairs={{0,8},{1,9},{2,10},{3,11},{4,12},{5,13},{6,14},{7,15},{8,0},{9,1},... | collective-permute-start | bytes 786440 | tf_op jit(solution)/shard_map/ppermute | solution.py:11
  25.1 14.6 %collective-permute-start.3 = (f32[2,128,256]{2,1,0:T(8,128)S(1)}, f32[2,128,256]{2,1,0:T(8,128)S(1)}, u32[]{:S(2)}, u32[]{:S(2)}) collective-permute-start(f32[2,128,256]{2,1,0:T(8,128)S(1)} %get-tuple-element.12), channel_id=1, source_target_pairs={{0,12},{1,13},{2,14},{3,15},{4,0},{5,1},{6,2},{7,3},{8,4},{9,5},{1... | collective-permute-start | bytes 786440 | tf_op jit(solution)/shard_map/ppermute | solution.py:11
  40.7 18.2 %collective-permute-start.4 = (f32[128,256]{1,0:T(8,128)S(1)}, f32[128,256]{1,0:T(8,128)S(1)}, u32[]{:S(2)}, u32[]{:S(2)}) collective-permute-start(f32[128,256]{1,0:T(8,128)S(1)} %get-tuple-element.15), channel_id=1, source_target_pairs={{0,258},{1,259},{2,256},{3,257},{4,262},{5,263},{6,260},{7,261},{8... | collective-permute-start | bytes 393224 | tf_op jit(solution)/shard_map/ppermute | solution.py:11
  60.8 17.3 %collective-permute-start.5 = (f32[128,256]{1,0:T(8,128)S(1)}, f32[128,256]{1,0:T(8,128)S(1)}, u32[]{:S(2)}, u32[]{:S(2)}) collective-permute-start(f32[128,256]{1,0:T(8,128)S(1)} %bitcast_add_fusion.3), channel_id=1, source_target_pairs={{0,256},{16,272},{32,288},{48,304},{64,320},{80,336},{96,352},{112... | collective-permute-start | bytes 393224 | tf_op jit(solution)/shard_map/ppermute | solution.py:11

commit v4 on v2

v4 whole, which is shorter than its diff:
```python
import jax
import jax.numpy as jnp
from jax import lax
from jax.sharding import Mesh, PartitionSpec as P

X, ZH, CORE = 4, 2, 2
PAIR = ("zl_hi", "zl_lo", "y")
LOOP = ("x", "zh", "core")


def moved(x, axis, target):
    count = lax.axis_size(axis)
    return lax.ppermute(x, axis, [(i, target(i)) for i in range(count)])


def local(amplitudes, integrals, pair_partner, virtual_swap):
    loop_count = lax.axis_size(LOOP)
    pair_count = lax.axis_size(PAIR)
    ab_local = integrals.shape[0] // loop_count
    ij_local = amplitudes.shape[0]
    j = lax.axis_index(LOOP)
    x, zh, c = j // (ZH * CORE), (j // CORE) % ZH, j % CORE
    partial = lax.dot_general(
        integrals,
        amplitudes,
        (((1,), (1,)), ((), ())),
        precision=lax.Precision.HIGHEST,
        preferred_element_type=jnp.float32,
    )
    part = partial.reshape(X, ZH, CORE, ab_local, ij_local)
    keep = lax.dynamic_index_in_dim(part, c, axis=2, keepdims=False)
    give = lax.dynamic_index_in_dim(part, 1 - c, axis=2, keepdims=False)
    s1 = keep + moved(give, LOOP, lambda i: i ^ 1)
    s2 = lax.all_to_all(s1, "x", 0, 0, tiled=True).reshape(X, ZH, ab_local, ij_local).sum(axis=0)
    mine = lax.dynamic_index_in_dim(s2, zh, axis=0, keepdims=False)
    other = lax.dynamic_index_in_dim(s2, 1 - zh, axis=0, keepdims=False)
    half = pair_count // 2
    from_zh = moved(other, LOOP, lambda i: i ^ 2)
    from_pair = moved(mine, PAIR, lambda i: (i + half) % pair_count)
    from_diag = moved(
        other,
        PAIR + LOOP,
        lambda i: ((i // loop_count + half) % pair_count) * loop_count + ((i % loop_count) ^ 2),
    )
    ladder = mine + from_zh
    mirror = from_pair + from_diag
    swap_local = virtual_swap - j * ab_local
    partner_local = pair_partner % ij_local
    mirror = jnp.take(jnp.take(mirror, swap_local, axis=0), partner_local, axis=1)
    return ladder + mirror


def solution(mesh):
    pair, loop = mesh.devices.shape
    fine = Mesh(mesh.devices.reshape(2, pair // (2 * 4), 4, X, ZH, CORE), PAIR + LOOP)
    in_specs = (P(PAIR, LOOP), P(None, LOOP), P(PAIR), P(LOOP))
    out_specs = P(LOOP, PAIR)
    return jax.shard_map(local, mesh=fine, in_specs=in_specs, out_specs=out_specs, check_vma=False)
```

time: 78.7 us -> 75.9 us (0.964)
  the two profiles are of different devices: /device:TPU:115 before, /device:TPU:121 now
where the time goes in v4:
time: 75.9 us; the launch traced here: 75.5 us
  waiting for transfers between devices  37.7 us (50%)
  starting transfers between devices  25.3 us (33%)
  matrix products  5.28 us (7%)
  local copies, waits for them, and re-layouts  3.9 us (5%)
  other arithmetic  3.28 us (4%)
    ppermute x4, waiting for transfers between devices, moved(): return lax.ppermute(x, axis, [(i, target(i)) for i in range(count)])  23.2 us
    ppermute x4, starting transfers between devices, moved(): return lax.ppermute(x, axis, [(i, target(i)) for i in range(count)])  21.2 us
    all_to_all x1, waiting for transfers between devices, local(): lax.all_to_all(s1, 'x', 0, 0, tiled=True).reshape(X, ZH, ab_local, ij_local)  14.5 us
    dot_general x1, matrix products, local(): lax.dot_general(integrals, amplitudes, (((1,), (1,)), ((), ())), precisio...  5.28 us
    all_to_all x1, starting transfers between devices, local(): lax.all_to_all(s1, 'x', 0, 0, tiled=True).reshape(X, ZH, ab_local, ij_local)  4.02 us
    add x1, other arithmetic, local(): s1 = keep + moved(give, LOOP, lambda i: i ^ 1)  2.38 us
  transfers between devices with their start and end apart: 5, of which 4 were waited for; matrix products, arithmetic and copies ran while one was open for 2% of the time, Pallas kernels for 0%

profile of v4, /device:TPU:121, one launch (start us, length us, event | category | flops | bytes accessed | tf_op | source)
XLA Modules:
  0.0 75.5 jit_solution(8020035801074666266)
XLA Ops:
  0.0 0.0 copy-start
  0.0 1.0 %copy-done = f32[256,512]{1,0:T(8,128)S(1)} copy-done((f32[256,512]{1,0:T(8,128)S(1)}, f32[256,512]{1,0:T(8,128)}, u32[]{:S(2)}) %copy-start) | copy-done | bytes 524312
  1.0 5.3 %fusion.1 = f32[2048,256]{1,0:T(8,128)S(1)} fusion(f32[2048,512]{1,0:T(8,128)} %param.5, f32[256,512]{1,0:T(8,128)S(1)} %copy-done), kind=kOutput, calls=%fused_computation.18 | convolution fusion | flops 3221225472 | bytes 6815744 | tf_op jit(solution)/shard_map/dot_general | solution.py:23
  6.3 0.0 copy-start.2
  6.3 0.0 copy-start.1
  6.4 1.1 %dynamic-slice_bitcast_fusion = f32[4,2,128,256]{3,2,1,0:T(8,128)} fusion(f32[4,2,2,128,256]{4,3,2,1,0:T(8,128)S(1)} %bitcast.13, s32[]{:T(128)S(6)} %select_n.55), kind=kLoop, calls=%fused_computation.3 | loop fusion | bytes 2097156 | tf_op jit(solution)/shard_map/jit(dynamic_index_in_dim)/squeeze | solution.py:32
  7.5 2.6 %collective-permute-start = (f32[4,2,128,256]{3,2,1,0:T(8,128)}, f32[4,2,128,256]{3,2,1,0:T(8,128)}, u32[]{:S(2)}, u32[]{:S(2)}) collective-permute-start(f32[4,2,128,256]{3,2,1,0:T(8,128)} %dynamic-slice_bitcast_fusion), channel_id=1, source_target_pairs={{0,1},{1,0},{2,3},{3,2},{4,5},{5,4},{6,7},{7,6},{8,9},{9,8},{10,11... | collective-permute-start | bytes 3145736 | tf_op jit(solution)/shard_map/ppermute | solution.py:13
  10.1 2.6 %collective-permute-done = f32[4,2,128,256]{3,2,1,0:T(8,128)} collective-permute-done((f32[4,2,128,256]{3,2,1,0:T(8,128)}, f32[4,2,128,256]{3,2,1,0:T(8,128)}, u32[]{:S(2)}, u32[]{:S(2)}) %collective-permute-start) | collective-permute-done | bytes 1048608 | tf_op jit(solution)/shard_map/ppermute | solution.py:13
  12.7 2.4 %bitcast_add_fusion = f32[4,2,128,256]{3,2,1,0:T(8,128)} fusion(f32[4,2,128,256]{3,2,1,0:T(8,128)} %collective-permute-done, f32[4,2,2,128,256]{4,3,2,1,0:T(8,128)S(1)} %bitcast.14, s32[]{:T(128)S(6)} %select_n.54), kind=kLoop, calls=%fused_computation.2 | loop fusion | flops 262144 | bytes 3145732 | tf_op jit(solution)/shard_map/add | solution.py:33
  15.1 4.0 %all-to-all-start = ((f32[4,2,128,256]{3,2,1,0:T(8,128)}), f32[4,2,128,256]{3,2,1,0:T(8,128)S(1)}, u32[]{:S(2)}, u32[]{:S(2)}) async-start(f32[4,2,128,256]{3,2,1,0:T(8,128)} %bitcast_add_fusion), calls=%async_computation | async-start | bytes 2097152 | tf_op jit(solution)/shard_map/all_to_all | solution.py:34
  19.1 14.5 %all-to-all-done = f32[4,2,128,256]{3,2,1,0:T(8,128)S(1)} async-done(((f32[4,2,128,256]{3,2,1,0:T(8,128)}), f32[4,2,128,256]{3,2,1,0:T(8,128)S(1)}, u32[]{:S(2)}, u32[]{:S(2)}) %all-to-all-start) | async-done | bytes 1048608 | tf_op jit(solution)/shard_map/all_to_all | solution.py:34
  33.6 0.1 reduce_sum.9
  33.7 8.8 %collective-permute-start.2 = (f32[128,256]{1,0:T(8,128)S(1)}, f32[128,256]{1,0:T(8,128)S(1)}, u32[]{:S(2)}, u32[]{:S(2)}) collective-permute-start(f32[128,256]{1,0:T(8,128)S(1)} %get-tuple-element.10), channel_id=1, source_target_pairs={{0,256},{16,272},{32,288},{48,304},{64,320},{80,336},{96,352},{112... | collective-permute-start | bytes 393224 | tf_op jit(solution)/shard_map/ppermute | solution.py:13
  42.6 6.1 %collective-permute-start.3 = (f32[128,256]{1,0:T(8,128)S(1)}, f32[128,256]{1,0:T(8,128)S(1)}, u32[]{:S(2)}, u32[]{:S(2)}) collective-permute-start(f32[128,256]{1,0:T(8,128)S(1)} %get-tuple-element.9), channel_id=1, source_target_pairs={{0,258},{1,259},{2,256},{3,257},{4,262},{5,263},{6,260},{7,261},{8... | collective-permute-start | bytes 393224 | tf_op jit(solution)/shard_map/ppermute | solution.py:13
  48.7 3.7 %collective-permute-start.1 = (f32[128,256]{1,0:T(8,128)S(1)}, f32[128,256]{1,0:T(8,128)S(1)}, u32[]{:S(2)}, u32[]{:S(2)}) collective-permute-start(f32[128,256]{1,0:T(8,128)S(1)} %get-tuple-element.9), channel_id=1, source_target_pairs={{0,2},{1,3},{2,0},{3,1},{4,6},{5,7},{6,4},{7,5},{8,10},{9,11},{10,... | collective-permute-start | bytes 393224 | tf_op jit(solution)/shard_map/ppermute | solution.py:13
  52.5 0.4 collective-permute-done.2
  52.9 20.1 %collective-permute-done.3 = f32[128,256]{1,0:T(8,128)S(1)} collective-permute-done((f32[128,256]{1,0:T(8,128)S(1)}, f32[128,256]{1,0:T(8,128)S(1)}, u32[]{:S(2)}, u32[]{:S(2)}) %collective-permute-start.3) | collective-permute-done | bytes 131104 | tf_op jit(solution)/shard_map/ppermute | solution.py:13
  73.1 0.8 gather_fusion
  73.8 0.1 broadcast_select_fusion
  73.9 0.1 copy.5
  74.0 0.7 gather_fusion.1
  74.7 0.1 copy.6
  74.8 0.0 collective-permute-done.1
  74.8 0.7 bitcast_add_fusion.1
  (8 shorter events, 0.1 us)
Async XLA Ops:
  0.0 1.0 %copy-start = (f32[256,512]{1,0:T(8,128)S(1)}, f32[256,512]{1,0:T(8,128)}, u32[]{:S(2)}) copy-start(f32[256,512]{1,0:T(8,128)} %param.4) | copy-start | bytes 1572868
  6.3 12.8 %copy-start.2 = (s32[128]{0:T(128)S(1)}, s32[128]{0:T(128)}, u32[]{:S(2)}) copy-start(s32[128]{0:T(128)} %param.7) | copy-start | bytes 1540
  6.3 12.8 %copy-start.1 = (s32[256]{0:T(256)S(1)}, s32[256]{0:T(256)}, u32[]{:S(2)}) copy-start(s32[256]{0:T(256)} %param.6) | copy-start | bytes 3076
  7.5 5.2 %collective-permute-start = (f32[4,2,128,256]{3,2,1,0:T(8,128)}, f32[4,2,128,256]{3,2,1,0:T(8,128)}, u32[]{:S(2)}, u32[]{:S(2)}) collective-permute-start(f32[4,2,128,256]{3,2,1,0:T(8,128)} %dynamic-slice_bitcast_fusion), channel_id=1, source_target_pairs={{0,1},{1,0},{2,3},{3,2},{4,5},{5,4},{6,7},{7,6},{8,9},{9,8},{10,11... | collective-permute-start | bytes 3145736 | tf_op jit(solution)/shard_map/ppermute | solution.py:13
  15.1 18.6 %all-to-all-start = ((f32[4,2,128,256]{3,2,1,0:T(8,128)}), f32[4,2,128,256]{3,2,1,0:T(8,128)S(1)}, u32[]{:S(2)}, u32[]{:S(2)}) async-start(f32[4,2,128,256]{3,2,1,0:T(8,128)} %bitcast_add_fusion), calls=%async_computation | async-start | bytes 2097152 | tf_op jit(solution)/shard_map/all_to_all | solution.py:34
  33.7 19.2 %collective-permute-start.2 = (f32[128,256]{1,0:T(8,128)S(1)}, f32[128,256]{1,0:T(8,128)S(1)}, u32[]{:S(2)}, u32[]{:S(2)}) collective-permute-start(f32[128,256]{1,0:T(8,128)S(1)} %get-tuple-element.10), channel_id=1, source_target_pairs={{0,256},{16,272},{32,288},{48,304},{64,320},{80,336},{96,352},{112... | collective-permute-start | bytes 393224 | tf_op jit(solution)/shard_map/ppermute | solution.py:13
  42.6 30.5 %collective-permute-start.3 = (f32[128,256]{1,0:T(8,128)S(1)}, f32[128,256]{1,0:T(8,128)S(1)}, u32[]{:S(2)}, u32[]{:S(2)}) collective-permute-start(f32[128,256]{1,0:T(8,128)S(1)} %get-tuple-element.9), channel_id=1, source_target_pairs={{0,258},{1,259},{2,256},{3,257},{4,262},{5,263},{6,260},{7,261},{8... | collective-permute-start | bytes 393224 | tf_op jit(solution)/shard_map/ppermute | solution.py:13
  48.7 26.1 %collective-permute-start.1 = (f32[128,256]{1,0:T(8,128)S(1)}, f32[128,256]{1,0:T(8,128)S(1)}, u32[]{:S(2)}, u32[]{:S(2)}) collective-permute-start(f32[128,256]{1,0:T(8,128)S(1)} %get-tuple-element.9), channel_id=1, source_target_pairs={{0,2},{1,3},{2,0},{3,1},{4,6},{5,7},{6,4},{7,5},{8,10},{9,11},{10,... | collective-permute-start | bytes 393224 | tf_op jit(solution)/shard_map/ppermute | solution.py:13

commit v5 on v4

--- a/solution.py
+++ b/solution.py
@@ -32,18 +32,11 @@
     give = lax.dynamic_index_in_dim(part, 1 - c, axis=2, keepdims=False)
     s1 = keep + moved(give, LOOP, lambda i: i ^ 1)
     s2 = lax.all_to_all(s1, "x", 0, 0, tiled=True).reshape(X, ZH, ab_local, ij_local).sum(axis=0)
-    mine = lax.dynamic_index_in_dim(s2, zh, axis=0, keepdims=False)
-    other = lax.dynamic_index_in_dim(s2, 1 - zh, axis=0, keepdims=False)
-    half = pair_count // 2
-    from_zh = moved(other, LOOP, lambda i: i ^ 2)
-    from_pair = moved(mine, PAIR, lambda i: (i + half) % pair_count)
-    from_diag = moved(
-        other,
-        PAIR + LOOP,
-        lambda i: ((i // loop_count + half) % pair_count) * loop_count + ((i % loop_count) ^ 2),
-    )
-    ladder = mine + from_zh
-    mirror = from_pair + from_diag
+    zl = lax.axis_index("zl_hi")
+    sent = jnp.broadcast_to(s2[None], (2,) + s2.shape).reshape(2 * ZH, ab_local, ij_local)
+    got = lax.all_to_all(sent, ("zl_hi", "zh"), 0, 0, tiled=True).reshape(2, ZH, ab_local, ij_local).sum(axis=1)
+    ladder = lax.dynamic_index_in_dim(got, zl, axis=0, keepdims=False)
+    mirror = lax.dynamic_index_in_dim(got, 1 - zl, axis=0, keepdims=False)
     swap_local = virtual_swap - j * ab_local
     partner_local = pair_partner % ij_local
     mirror = jnp.take(jnp.take(mirror, swap_local, axis=0), partner_local, axis=1)

time: 75.9 us -> 82.4 us (1.086)
  the two profiles are of different devices: /device:TPU:121 before, /device:TPU:56 now
where the time goes in v5:
time: 82.4 us; the launch traced here: 82.1 us
  waiting for transfers between devices  34 us (41%)
  blocking collectives  19.5 us (24%)
  starting transfers between devices  16.1 us (20%)
  local copies, waits for them, and re-layouts  5.43 us (7%)
  matrix products  5.28 us (6%)
  other arithmetic  1.69 us (2%)
    all_to_all x1, waiting for transfers between devices, local(): lax.all_to_all(sent, ('zl_hi', 'zh'), 0, 0, tiled=True)  31.1 us
    all_to_all x1, blocking collectives, local(): lax.all_to_all(s1, 'x', 0, 0, tiled=True).reshape(X, ZH, ab_local, ij_local)  19.5 us
    all_to_all x1, starting transfers between devices, local(): lax.all_to_all(sent, ('zl_hi', 'zh'), 0, 0, tiled=True)  14.2 us
    dot_general x1, matrix products, local(): lax.dot_general(integrals, amplitudes, (((1,), (1,)), ((), ())), precisio...  5.28 us
    ppermute x1, waiting for transfers between devices, moved(): return lax.ppermute(x, axis, [(i, target(i)) for i in range(count)])  2.94 us
    ppermute x1, starting transfers between devices, moved(): return lax.ppermute(x, axis, [(i, target(i)) for i in range(count)])  1.91 us
  transfers between devices with their start and end apart: 2, of which 2 were waited for; matrix products, arithmetic and copies ran while one was open for 0% of the time, Pallas kernels for 0%

profile of v5, /device:TPU:56, one launch (start us, length us, event | category | flops | bytes accessed | tf_op | source)
XLA Modules:
  0.0 82.1 jit_solution(7028534155148880022)
XLA Ops:
  0.0 0.0 copy-start
  0.0 1.0 %copy-done = f32[256,512]{1,0:T(8,128)S(1)} copy-done((f32[256,512]{1,0:T(8,128)S(1)}, f32[256,512]{1,0:T(8,128)}, u32[]{:S(2)}) %copy-start) | copy-done | bytes 524312
  1.0 5.3 %fusion.1 = f32[2048,256]{1,0:T(8,128)S(1)} fusion(f32[2048,512]{1,0:T(8,128)} %param.5, f32[256,512]{1,0:T(8,128)S(1)} %copy-done), kind=kOutput, calls=%fused_computation.19 | convolution fusion | flops 3221225472 | bytes 6815744 | tf_op jit(solution)/shard_map/dot_general | solution.py:23
  6.3 1.1 %dynamic-slice_bitcast_fusion = f32[4,2,128,256]{3,2,1,0:T(8,128)} fusion(f32[4,2,2,128,256]{4,3,2,1,0:T(8,128)S(1)} %bitcast.16, s32[]{:T(128)S(6)} %select_n.47), kind=kLoop, calls=%fused_computation.3 | loop fusion | bytes 2097156 | tf_op jit(solution)/shard_map/jit(dynamic_index_in_dim)/squeeze | solution.py:32
  7.4 1.9 %collective-permute-start = (f32[4,2,128,256]{3,2,1,0:T(8,128)}, f32[4,2,128,256]{3,2,1,0:T(8,128)}, u32[]{:S(2)}, u32[]{:S(2)}) collective-permute-start(f32[4,2,128,256]{3,2,1,0:T(8,128)} %dynamic-slice_bitcast_fusion), channel_id=1, source_target_pairs={{0,1},{1,0},{2,3},{3,2},{4,5},{5,4},{6,7},{7,6},{8,9},{9,8},{10,11... | collective-permute-start | bytes 3145736 | tf_op jit(solution)/shard_map/ppermute | solution.py:13
  9.3 0.0 copy-start.2
  9.4 0.0 copy-start.1
  9.4 2.9 %collective-permute-done = f32[4,2,128,256]{3,2,1,0:T(8,128)} collective-permute-done((f32[4,2,128,256]{3,2,1,0:T(8,128)}, f32[4,2,128,256]{3,2,1,0:T(8,128)}, u32[]{:S(2)}, u32[]{:S(2)}) %collective-permute-start) | collective-permute-done | bytes 1048608 | tf_op jit(solution)/shard_map/ppermute | solution.py:13
  12.3 1.4 %bitcast_add_fusion = f32[4,2,128,256]{3,2,1,0:T(8,128)S(1)} fusion(f32[4,2,128,256]{3,2,1,0:T(8,128)} %collective-permute-done, f32[4,2,2,128,256]{4,3,2,1,0:T(8,128)S(1)} %bitcast.17, s32[]{:T(128)S(6)} %select_n.46), kind=kLoop, calls=%fused_computation.2 | loop fusion | flops 262144 | bytes 3145732 | tf_op jit(solution)/shard_map/add | solution.py:33
  13.7 19.5 %all_to_all.10 = f32[4,2,128,256]{3,2,1,0:T(8,128)S(1)} all-to-all(f32[4,2,128,256]{3,2,1,0:T(8,128)S(1)} %bitcast_add_fusion), channel_id=1, replica_groups=mesh['zl_hi'=2,'zl_lo'=4,'y'=4,'x'=4,'zh'=2,'core'=2] {'x'}, dimensions={0} | all-to-all | bytes 2097152 | tf_op jit(solution)/shard_map/all_to_all | solution.py:34
  33.2 0.1 reduce_sum.18
  33.2 0.8 %broadcast_in_dim.28 = f32[2,2,128,256]{3,2,1,0:T(8,128)} broadcast(f32[2,128,256]{2,1,0:T(8,128)S(1)} %reduce_sum.18), dimensions={1,2,3} | broadcast | bytes 786432 | tf_op jit(solution)/shard_map/broadcast_in_dim | solution.py:36
  34.1 14.2 %all-to-all-start.1 = ((f32[4,128,256]{2,1,0:T(8,128)}), f32[4,128,256]{2,1,0:T(8,128)S(1)}, u32[]{:S(2)}, u32[]{:S(2)}) async-start(f32[4,128,256]{2,1,0:T(8,128)} %bitcast.3), calls=%async_computation.1 | async-start | bytes 1048576 | tf_op jit(solution)/shard_map/all_to_all | solution.py:37
  48.3 0.0 copy-done.2
  48.3 0.0 copy-done.1
  48.3 31.1 %all-to-all-done.1 = f32[4,128,256]{2,1,0:T(8,128)S(1)} async-done(((f32[4,128,256]{2,1,0:T(8,128)}), f32[4,128,256]{2,1,0:T(8,128)S(1)}, u32[]{:S(2)}, u32[]{:S(2)}) %all-to-all-start.1) | async-done | bytes 524320 | tf_op jit(solution)/shard_map/all_to_all | solution.py:37
  79.5 0.8 gather_fusion
  80.3 0.1 broadcast_select_fusion
  80.3 0.1 copy.9
  80.4 0.1 copy.8
  80.5 0.7 gather_fusion.1
  81.3 0.1 bitcast_add_fusion.1
  81.4 0.8 copy.10
  (6 shorter events, 0.1 us)
Async XLA Ops:
  0.0 1.0 %copy-start = (f32[256,512]{1,0:T(8,128)S(1)}, f32[256,512]{1,0:T(8,128)}, u32[]{:S(2)}) copy-start(f32[256,512]{1,0:T(8,128)} %param.4) | copy-start | bytes 1572868
  7.4 4.9 %collective-permute-start = (f32[4,2,128,256]{3,2,1,0:T(8,128)}, f32[4,2,128,256]{3,2,1,0:T(8,128)}, u32[]{:S(2)}, u32[]{:S(2)}) collective-permute-start(f32[4,2,128,256]{3,2,1,0:T(8,128)} %dynamic-slice_bitcast_fusion), channel_id=1, source_target_pairs={{0,1},{1,0},{2,3},{3,2},{4,5},{5,4},{6,7},{7,6},{8,9},{9,8},{10,11... | collective-permute-start | bytes 3145736 | tf_op jit(solution)/shard_map/ppermute | solution.py:13
  9.3 38.9 %copy-start.2 = (s32[128]{0:T(128)S(1)}, s32[128]{0:T(128)}, u32[]{:S(2)}) copy-start(s32[128]{0:T(128)} %param.7) | copy-start | bytes 1540
  9.4 38.9 %copy-start.1 = (s32[256]{0:T(256)S(1)}, s32[256]{0:T(256)}, u32[]{:S(2)}) copy-start(s32[256]{0:T(256)} %param.6) | copy-start | bytes 3076
  34.1 45.4 %all-to-all-start.1 = ((f32[4,128,256]{2,1,0:T(8,128)}), f32[4,128,256]{2,1,0:T(8,128)S(1)}, u32[]{:S(2)}, u32[]{:S(2)}) async-start(f32[4,128,256]{2,1,0:T(8,128)} %bitcast.3), calls=%async_computation.1 | async-start | bytes 1048576 | tf_op jit(solution)/shard_map/all_to_all | solution.py:37

commit v6 on v5

v6 whole, which is shorter than its diff:
```python
import jax
import jax.numpy as jnp
from jax import lax
from jax.sharding import Mesh, PartitionSpec as P

X, ZH, CORE = 4, 2, 2
PAIR = ("zl_hi", "zl_lo", "y")
LOOP = ("x", "zh", "core")
CHUNK = 64


def moved(x, axis, target):
    count = lax.axis_size(axis)
    return lax.ppermute(x, axis, [(i, target(i)) for i in range(count)])


def local(amplitudes, integrals, pair_partner, virtual_swap):
    loop_count = lax.axis_size(LOOP)
    pair_count = lax.axis_size(PAIR)
    ab_local = integrals.shape[0] // loop_count
    ij_local = amplitudes.shape[0]
    chunks = ab_local // CHUNK
    j = lax.axis_index(LOOP)
    x, zh, c = j // (ZH * CORE), (j // CORE) % ZH, j % CORE
    half = pair_count // 2
    swap_local = virtual_swap - j * ab_local
    partner_local = pair_partner % ij_local
    rows = integrals.reshape(loop_count, chunks, CHUNK, integrals.shape[1])
    outs = []
    for h in range(chunks):
        partial = lax.dot_general(
            rows[:, h].reshape(loop_count * CHUNK, integrals.shape[1]),
            amplitudes,
            (((1,), (1,)), ((), ())),
            precision=lax.Precision.HIGHEST,
            preferred_element_type=jnp.float32,
        )
        part = partial.reshape(X, ZH, CORE, CHUNK, ij_local)
        keep = lax.dynamic_index_in_dim(part, c, axis=2, keepdims=False)
        give = lax.dynamic_index_in_dim(part, 1 - c, axis=2, keepdims=False)
        s1 = keep + moved(give, LOOP, lambda i: i ^ 1)
        s2 = lax.all_to_all(s1, "x", 0, 0, tiled=True).reshape(X, ZH, CHUNK, ij_local).sum(axis=0)
        mine = lax.dynamic_index_in_dim(s2, zh, axis=0, keepdims=False)
        other = lax.dynamic_index_in_dim(s2, 1 - zh, axis=0, keepdims=False)
        from_zh = moved(other, LOOP, lambda i: i ^ 2)
        from_pair = moved(mine, PAIR, lambda i: (i + half) % pair_count)
        from_diag = moved(
            other,
            PAIR + LOOP,
            lambda i: ((i // loop_count + half) % pair_count) * loop_count + ((i % loop_count) ^ 2),
        )
        ladder = mine + from_zh
        mirror = from_pair + from_diag
        swap_chunk = swap_local[h * CHUNK:(h + 1) * CHUNK] - h * CHUNK
        mirror = jnp.take(jnp.take(mirror, swap_chunk, axis=0), partner_local, axis=1)
        outs.append(ladder + mirror)
    return jnp.concatenate(outs, axis=0)


def solution(mesh):
    pair, loop = mesh.devices.shape
    fine = Mesh(mesh.devices.reshape(2, pair // (2 * 4), 4, X, ZH, CORE), PAIR + LOOP)
    in_specs = (P(PAIR, LOOP), P(None, LOOP), P(PAIR), P(LOOP))
    out_specs = P(LOOP, PAIR)
    return jax.shard_map(local, mesh=fine, in_specs=in_specs, out_specs=out_specs, check_vma=False)
```

time: 82.4 us -> 92.6 us (1.12)
  the two profiles are of different devices: /device:TPU:56 before, /device:TPU:42 now
where the time goes in v6:
time: 92.6 us; the launch traced here: 92 us
  starting transfers between devices  53.4 us (58%)
  waiting for transfers between devices  17.2 us (19%)
  local copies, waits for them, and re-layouts  11.2 us (12%)
  matrix products  6.22 us (7%)
  other arithmetic  3.82 us (4%)
    ppermute x8, starting transfers between devices, moved(): return lax.ppermute(x, axis, [(i, target(i)) for i in range(count)])  43.5 us
    ppermute x8, waiting for transfers between devices, moved(): return lax.ppermute(x, axis, [(i, target(i)) for i in range(count)])  9.98 us
    all_to_all x2, starting transfers between devices, local(): lax.all_to_all(s1, 'x', 0, 0, tiled=True).reshape(X, ZH, CHUNK, ij_local)  9.86 us
    all_to_all x2, waiting for transfers between devices, local(): lax.all_to_all(s1, 'x', 0, 0, tiled=True).reshape(X, ZH, CHUNK, ij_local)  7.2 us
    dot_general x2, matrix products, local(): lax.dot_general(rows[:, h].reshape(loop_count * CHUNK, integrals.shape[1]...  6.22 us
    slice x1, local copies, waits for them, and re-layouts, local(): rows[:, h].reshape(loop_count * CHUNK, integrals.shape[1])  4.26 us
    add x2, other arithmetic, local(): s1 = keep + moved(give, LOOP, lambda i: i ^ 1)  2.84 us
    squeeze x2, local copies, waits for them, and re-layouts, local(): give = lax.dynamic_index_in_dim(part, 1 - c, axis=2, keepdims=False)  2.76 us
  transfers between devices with their start and end apart: 10, of which 2 were waited for; matrix products, arithmetic and copies ran while one was open for 10% of the time, Pallas kernels for 0%

profile of v6, /device:TPU:42, one launch (start us, length us, event | category | flops | bytes accessed | tf_op | source)
XLA Modules:
  0.0 92.0 jit_solution(1760193774064583350)
XLA Ops:
  0.0 4.3 %fusion.5 = (f32[16,1,64,512]{3,2,1,0:T(8,128)S(1)}, f32[16,1,64,512]{3,2,1,0:T(8,128)}) fusion(f32[16,2,64,512]{3,2,1,0:T(8,128)} %bitcast.38), kind=kLoop, calls=%fused_computation.35 | loop fusion | bytes 8388608 | tf_op jit(solution)/shard_map/slice | solution.py:32
  4.3 4.4 %fusion = f32[4,2,2,64,256]{4,3,2,1,0:T(8,128)} fusion(f32[4,2,2,64,512]{4,3,2,1,0:T(8,128)} %bitcast.37, f32[256,512]{1,0:T(8,128)S(1)} %copy-done), kind=kOutput, calls=%fused_computation.5 | convolution fusion | flops 1610612736 | bytes 3670016 | tf_op jit(solution)/shard_map/dot_general | solution.py:31
  8.7 1.9 %dynamic-slice_bitcast_fusion = f32[4,2,64,256]{3,2,1,0:T(8,128)} fusion(f32[4,2,2,64,256]{4,3,2,1,0:T(8,128)} %fusion, s32[]{:T(128)S(6)} %select_n.55), kind=kLoop, calls=%fused_computation.10 | loop fusion | bytes 1048580 | tf_op jit(solution)/shard_map/jit(dynamic_index_in_dim)/squeeze | solution.py:40
  10.6 1.9 %collective-permute-start.4 = (f32[4,2,64,256]{3,2,1,0:T(8,128)}, f32[4,2,64,256]{3,2,1,0:T(8,128)S(1)}, u32[]{:S(2)}, u32[]{:S(2)}) collective-permute-start(f32[4,2,64,256]{3,2,1,0:T(8,128)} %dynamic-slice_bitcast_fusion), channel_id=1, source_target_pairs={{0,1},{1,0},{2,3},{3,2},{4,5},{5,4},{6,7},{7,6},{8,9},{9,8},{10,11... | collective-permute-start | bytes 1572872 | tf_op jit(solution)/shard_map/ppermute | solution.py:14
  12.5 1.8 %fusion.2 = f32[4,2,2,64,256]{4,3,2,1,0:T(8,128)S(1)} fusion(f32[4,2,2,64,512]{4,3,2,1,0:T(8,128)S(1)} %bitcast.36, f32[256,512]{1,0:T(8,128)S(1)} %copy-done), kind=kOutput, calls=%fused_computation.7 | convolution fusion | flops 1610612736 | bytes 3670016 | tf_op jit(solution)/shard_map/dot_general | solution.py:31
  14.3 1.0 %copy-done.1 = f32[4,2,2,64,256]{4,3,2,1,0:T(8,128)} copy-done((f32[4,2,2,64,256]{4,3,2,1,0:T(8,128)}, f32[4,2,2,64,256]{4,3,2,1,0:T(8,128)S(1)}, u32[]{:S(2)}) %copy-start.1) | copy-done | bytes 1048600
  15.3 0.9 dynamic-slice_bitcast_fusion.1
  16.2 2.5 %collective-permute-start = (f32[4,2,64,256]{3,2,1,0:T(8,128)}, f32[4,2,64,256]{3,2,1,0:T(8,128)S(1)}, u32[]{:S(2)}, u32[]{:S(2)}) collective-permute-start(f32[4,2,64,256]{3,2,1,0:T(8,128)} %dynamic-slice_bitcast_fusion.1), channel_id=1, source_target_pairs={{0,1},{1,0},{2,3},{3,2},{4,5},{5,4},{6,7},{7,6},{8,9},{9,8},{10,11... | collective-permute-start | bytes 1572872 | tf_op jit(solution)/shard_map/ppermute | solution.py:14
  18.8 1.9 %bitcast_add_fusion = f32[4,2,64,256]{3,2,1,0:T(8,128)} fusion(f32[4,2,64,256]{3,2,1,0:T(8,128)S(1)} %collective-permute-done.4, f32[4,2,2,64,256]{4,3,2,1,0:T(8,128)} %fusion, s32[]{:T(128)S(6)} %select_n.54), kind=kLoop, calls=%fused_computation.4 | loop fusion | flops 131072 | bytes 1572868 | tf_op jit(solution)/shard_map/add | solution.py:41
  20.7 5.0 %all-to-all-start.1 = ((f32[4,2,64,256]{3,2,1,0:T(8,128)}), f32[4,2,64,256]{3,2,1,0:T(8,128)S(1)}, u32[]{:S(2)}, u32[]{:S(2)}) async-start(f32[4,2,64,256]{3,2,1,0:T(8,128)} %bitcast_add_fusion), calls=%async_computation.1 | async-start | bytes 1048576 | tf_op jit(solution)/shard_map/all_to_all | solution.py:42
  25.8 0.9 bitcast_add_fusion.1
  26.7 7.2 %all-to-all-done.1 = f32[4,2,64,256]{3,2,1,0:T(8,128)S(1)} async-done(((f32[4,2,64,256]{3,2,1,0:T(8,128)}), f32[4,2,64,256]{3,2,1,0:T(8,128)S(1)}, u32[]{:S(2)}, u32[]{:S(2)}) %all-to-all-start.1) | async-done | bytes 524320 | tf_op jit(solution)/shard_map/all_to_all | solution.py:42
  33.9 4.9 %all-to-all-start = ((f32[4,2,64,256]{3,2,1,0:T(8,128)}), f32[4,2,64,256]{3,2,1,0:T(8,128)S(1)}, u32[]{:S(2)}, u32[]{:S(2)}) async-start(f32[4,2,64,256]{3,2,1,0:T(8,128)} %bitcast_add_fusion.1), calls=%async_computation | async-start | bytes 1048576 | tf_op jit(solution)/shard_map/all_to_all | solution.py:42
  38.9 9.1 %collective-permute-start.6 = (f32[64,256]{1,0:T(8,128)S(1)}, f32[64,256]{1,0:T(8,128)S(1)}, u32[]{:S(2)}, u32[]{:S(2)}) collective-permute-start(f32[64,256]{1,0:T(8,128)S(1)} %get-tuple-element.18), channel_id=1, source_target_pairs={{0,256},{16,272},{32,288},{48,304},{64,320},{80,336},{96,352},{112... | collective-permute-start | bytes 196616 | tf_op jit(solution)/shard_map/ppermute | solution.py:14
  48.0 8.2 %collective-permute-start.7 = (f32[64,256]{1,0:T(8,128)S(1)}, f32[64,256]{1,0:T(8,128)S(1)}, u32[]{:S(2)}, u32[]{:S(2)}) collective-permute-start(f32[64,256]{1,0:T(8,128)S(1)} %get-tuple-element.17), channel_id=1, source_target_pairs={{0,258},{1,259},{2,256},{3,257},{4,262},{5,263},{6,260},{7,261},{8... | collective-permute-start | bytes 196616 | tf_op jit(solution)/shard_map/ppermute | solution.py:14
  56.2 4.3 %collective-permute-start.2 = (f32[64,256]{1,0:T(8,128)S(1)}, f32[64,256]{1,0:T(8,128)S(1)}, u32[]{:S(2)}, u32[]{:S(2)}) collective-permute-start(f32[64,256]{1,0:T(8,128)S(1)} %get-tuple-element.16), channel_id=1, source_target_pairs={{0,256},{16,272},{32,288},{48,304},{64,320},{80,336},{96,352},{112... | collective-permute-start | bytes 196616 | tf_op jit(solution)/shard_map/ppermute | solution.py:14
  60.5 2.9 %collective-permute-start.3 = (f32[64,256]{1,0:T(8,128)S(1)}, f32[64,256]{1,0:T(8,128)S(1)}, u32[]{:S(2)}, u32[]{:S(2)}) collective-permute-start(f32[64,256]{1,0:T(8,128)S(1)} %get-tuple-element.15), channel_id=1, source_target_pairs={{0,258},{1,259},{2,256},{3,257},{4,262},{5,263},{6,260},{7,261},{8... | collective-permute-start | bytes 196616 | tf_op jit(solution)/shard_map/ppermute | solution.py:14
  63.5 9.8 %collective-permute-start.1 = (f32[64,256]{1,0:T(8,128)S(1)}, f32[64,256]{1,0:T(8,128)S(1)}, u32[]{:S(2)}, u32[]{:S(2)}) collective-permute-start(f32[64,256]{1,0:T(8,128)S(1)} %get-tuple-element.15), channel_id=1, source_target_pairs={{0,2},{1,3},{2,0},{3,1},{4,6},{5,7},{6,4},{7,5},{8,10},{9,11},{10,... | collective-permute-start | bytes 196616 | tf_op jit(solution)/shard_map/ppermute | solution.py:14
  73.3 4.7 %collective-permute-start.5 = (f32[64,256]{1,0:T(8,128)S(1)}, f32[64,256]{1,0:T(8,128)S(1)}, u32[]{:S(2)}, u32[]{:S(2)}) collective-permute-start(f32[64,256]{1,0:T(8,128)S(1)} %get-tuple-element.17), channel_id=1, source_target_pairs={{0,2},{1,3},{2,0},{3,1},{4,6},{5,7},{6,4},{7,5},{8,10},{9,11},{10,... | collective-permute-start | bytes 196616 | tf_op jit(solution)/shard_map/ppermute | solution.py:14
  78.1 0.7 gather_fusion.2
  79.6 0.7 gather_fusion.1
  80.6 0.7 gather_fusion.3
  81.4 10.0 %collective-permute-done.5 = f32[64,256]{1,0:T(8,128)S(1)} collective-permute-done((f32[64,256]{1,0:T(8,128)S(1)}, f32[64,256]{1,0:T(8,128)S(1)}, u32[]{:S(2)}, u32[]{:S(2)}) %collective-permute-start.5) | collective-permute-done | bytes 65568 | tf_op jit(solution)/shard_map/ppermute | solution.py:14
  91.4 0.7 pad_maximum_fusion
  (36 shorter events, 1.4 us)
Async XLA Ops:
  0.0 4.3 %copy-start = (f32[256,512]{1,0:T(8,128)S(1)}, f32[256,512]{1,0:T(8,128)}, u32[]{:S(2)}) copy-start(f32[256,512]{1,0:T(8,128)} %param.8) | copy-start | bytes 1572868
  10.6 8.2 %collective-permute-start.4 = (f32[4,2,64,256]{3,2,1,0:T(8,128)}, f32[4,2,64,256]{3,2,1,0:T(8,128)S(1)}, u32[]{:S(2)}, u32[]{:S(2)}) collective-permute-start(f32[4,2,64,256]{3,2,1,0:T(8,128)} %dynamic-slice_bitcast_fusion), channel_id=1, source_target_pairs={{0,1},{1,0},{2,3},{3,2},{4,5},{5,4},{6,7},{7,6},{8,9},{9,8},{10,11... | collective-permute-start | bytes 1572872 | tf_op jit(solution)/shard_map/ppermute | solution.py:14
  12.5 6.3 %copy-start.4 = (s32[128]{0:T(128)S(1)}, s32[128]{0:T(128)}, u32[]{:S(2)}) copy-start(s32[128]{0:T(128)} %param.11) | copy-start | bytes 1540
  14.3 1.0 %copy-start.1 = (f32[4,2,2,64,256]{4,3,2,1,0:T(8,128)}, f32[4,2,2,64,256]{4,3,2,1,0:T(8,128)S(1)}, u32[]{:S(2)}) copy-start(f32[4,2,2,64,256]{4,3,2,1,0:T(8,128)S(1)} %fusion.2) | copy-start | bytes 3145732
  16.2 9.6 %copy-start.2 = (f32[4,2,2,64,256]{4,3,2,1,0:T(8,128)S(1)}, f32[4,2,2,64,256]{4,3,2,1,0:T(8,128)}, u32[]{:S(2)}) copy-start(f32[4,2,2,64,256]{4,3,2,1,0:T(8,128)} %copy-done.1) | copy-start | bytes 3145732
  16.2 9.6 %collective-permute-start = (f32[4,2,64,256]{3,2,1,0:T(8,128)}, f32[4,2,64,256]{3,2,1,0:T(8,128)S(1)}, u32[]{:S(2)}, u32[]{:S(2)}) collective-permute-start(f32[4,2,64,256]{3,2,1,0:T(8,128)} %dynamic-slice_bitcast_fusion.1), channel_id=1, source_target_pairs={{0,1},{1,0},{2,3},{3,2},{4,5},{5,4},{6,7},{7,6},{8,9},{9,8},{10,11... | collective-permute-start | bytes 1572872 | tf_op jit(solution)/shard_map/ppermute | solution.py:14
  20.7 18.1 %copy-start.3 = (s32[256]{0:T(256)S(1)}, s32[256]{0:T(256)}, u32[]{:S(2)}) copy-start(s32[256]{0:T(256)} %param.10) | copy-start | bytes 3076
  20.7 13.2 %all-to-all-start.1 = ((f32[4,2,64,256]{3,2,1,0:T(8,128)}), f32[4,2,64,256]{3,2,1,0:T(8,128)S(1)}, u32[]{:S(2)}, u32[]{:S(2)}) async-start(f32[4,2,64,256]{3,2,1,0:T(8,128)} %bitcast_add_fusion), calls=%async_computation.1 | async-start | bytes 1048576 | tf_op jit(solution)/shard_map/all_to_all | solution.py:42
  33.9 22.3 %all-to-all-start = ((f32[4,2,64,256]{3,2,1,0:T(8,128)}), f32[4,2,64,256]{3,2,1,0:T(8,128)S(1)}, u32[]{:S(2)}, u32[]{:S(2)}) async-start(f32[4,2,64,256]{3,2,1,0:T(8,128)} %bitcast_add_fusion.1), calls=%async_computation | async-start | bytes 1048576 | tf_op jit(solution)/shard_map/all_to_all | solution.py:42
  38.9 34.5 %collective-permute-start.6 = (f32[64,256]{1,0:T(8,128)S(1)}, f32[64,256]{1,0:T(8,128)S(1)}, u32[]{:S(2)}, u32[]{:S(2)}) collective-permute-start(f32[64,256]{1,0:T(8,128)S(1)} %get-tuple-element.18), channel_id=1, source_target_pairs={{0,256},{16,272},{32,288},{48,304},{64,320},{80,336},{96,352},{112... | collective-permute-start | bytes 196616 | tf_op jit(solution)/shard_map/ppermute | solution.py:14
  48.0 30.1 %collective-permute-start.7 = (f32[64,256]{1,0:T(8,128)S(1)}, f32[64,256]{1,0:T(8,128)S(1)}, u32[]{:S(2)}, u32[]{:S(2)}) collective-permute-start(f32[64,256]{1,0:T(8,128)S(1)} %get-tuple-element.17), channel_id=1, source_target_pairs={{0,258},{1,259},{2,256},{3,257},{4,262},{5,263},{6,260},{7,261},{8... | collective-permute-start | bytes 196616 | tf_op jit(solution)/shard_map/ppermute | solution.py:14
  56.2 22.5 %collective-permute-start.2 = (f32[64,256]{1,0:T(8,128)S(1)}, f32[64,256]{1,0:T(8,128)S(1)}, u32[]{:S(2)}, u32[]{:S(2)}) collective-permute-start(f32[64,256]{1,0:T(8,128)S(1)} %get-tuple-element.16), channel_id=1, source_target_pairs={{0,256},{16,272},{32,288},{48,304},{64,320},{80,336},{96,352},{112... | collective-permute-start | bytes 196616 | tf_op jit(solution)/shard_map/ppermute | solution.py:14
  60.5 18.2 %collective-permute-start.3 = (f32[64,256]{1,0:T(8,128)S(1)}, f32[64,256]{1,0:T(8,128)S(1)}, u32[]{:S(2)}, u32[]{:S(2)}) collective-permute-start(f32[64,256]{1,0:T(8,128)S(1)} %get-tuple-element.15), channel_id=1, source_target_pairs={{0,258},{1,259},{2,256},{3,257},{4,262},{5,263},{6,260},{7,261},{8... | collective-permute-start | bytes 196616 | tf_op jit(solution)/shard_map/ppermute | solution.py:14
  63.5 17.9 %collective-permute-start.1 = (f32[64,256]{1,0:T(8,128)S(1)}, f32[64,256]{1,0:T(8,128)S(1)}, u32[]{:S(2)}, u32[]{:S(2)}) collective-permute-start(f32[64,256]{1,0:T(8,128)S(1)} %get-tuple-element.15), channel_id=1, source_target_pairs={{0,2},{1,3},{2,0},{3,1},{4,6},{5,7},{6,4},{7,5},{8,10},{9,11},{10,... | collective-permute-start | bytes 196616 | tf_op jit(solution)/shard_map/ppermute | solution.py:14
  73.3 18.0 %collective-permute-start.5 = (f32[64,256]{1,0:T(8,128)S(1)}, f32[64,256]{1,0:T(8,128)S(1)}, u32[]{:S(2)}, u32[]{:S(2)}) collective-permute-start(f32[64,256]{1,0:T(8,128)S(1)} %get-tuple-element.17), channel_id=1, source_target_pairs={{0,2},{1,3},{2,0},{3,1},{4,6},{5,7},{6,4},{7,5},{8,10},{9,11},{10,... | collective-permute-start | bytes 196616 | tf_op jit(solution)/shard_map/ppermute | solution.py:14

commit v7 on v4

--- a/solution.py
+++ b/solution.py
@@ -20,17 +20,20 @@
     ij_local = amplitudes.shape[0]
     j = lax.axis_index(LOOP)
     x, zh, c = j // (ZH * CORE), (j // CORE) % ZH, j % CORE
-    partial = lax.dot_general(
-        integrals,
-        amplitudes,
-        (((1,), (1,)), ((), ())),
-        precision=lax.Precision.HIGHEST,
-        preferred_element_type=jnp.float32,
-    )
-    part = partial.reshape(X, ZH, CORE, ab_local, ij_local)
-    keep = lax.dynamic_index_in_dim(part, c, axis=2, keepdims=False)
-    give = lax.dynamic_index_in_dim(part, 1 - c, axis=2, keepdims=False)
-    s1 = keep + moved(give, LOOP, lambda i: i ^ 1)
+    blocks = integrals.reshape(X, ZH, CORE, ab_local, integrals.shape[1])
+
+    def product(core):
+        rows = lax.dynamic_index_in_dim(blocks, core, axis=2, keepdims=False)
+        return lax.dot_general(
+            rows.reshape(X * ZH * ab_local, integrals.shape[1]),
+            amplitudes,
+            (((1,), (1,)), ((), ())),
+            precision=lax.Precision.HIGHEST,
+            preferred_element_type=jnp.float32,
+        ).reshape(X, ZH, ab_local, ij_local)
+
+    give = moved(product(1 - c), LOOP, lambda i: i ^ 1)
+    s1 = lax.optimization_barrier(product(c)) + give
     s2 = lax.all_to_all(s1, "x", 0, 0, tiled=True).reshape(X, ZH, ab_local, ij_local).sum(axis=0)
     mine = lax.dynamic_index_in_dim(s2, zh, axis=0, keepdims=False)
     other = lax.dynamic_index_in_dim(s2, 1 - zh, axis=0, keepdims=False)

time: 75.9 us -> 72.9 us (0.960)
  the two profiles are of different devices: /device:TPU:121 before, /device:TPU:105 now
where the time goes in v7:
time: 72.9 us; the launch traced here: 72.5 us
  waiting for transfers between devices  35.4 us (49%)
  starting transfers between devices  25.3 us (35%)
  matrix products  6.84 us (9%)
  local copies, waits for them, and re-layouts  2.75 us (4%)
  other arithmetic  2.03 us (3%)
    ppermute x4, starting transfers between devices, moved(): return lax.ppermute(x, axis, [(i, target(i)) for i in range(count)])  21.3 us
    ppermute x4, waiting for transfers between devices, moved(): return lax.ppermute(x, axis, [(i, target(i)) for i in range(count)])  20.6 us
    all_to_all x1, waiting for transfers between devices, local(): lax.all_to_all(s1, 'x', 0, 0, tiled=True).reshape(X, ZH, ab_local, ij_local)  14.9 us
    dot_general x2, matrix products, product(): lax.dot_general(rows.reshape(X * ZH * ab_local, integrals.shape[1]), ampl...  6.84 us
    all_to_all x1, starting transfers between devices, local(): lax.all_to_all(s1, 'x', 0, 0, tiled=True).reshape(X, ZH, ab_local, ij_local)  4.01 us
  transfers between devices with their start and end apart: 5, of which 3 were waited for; matrix products, arithmetic and copies ran while one was open for 7% of the time, Pallas kernels for 0%

profile of v7, /device:TPU:105, one launch (start us, length us, event | category | flops | bytes accessed | tf_op | source)
XLA Modules:
  0.0 72.5 jit_solution(13543477614209400853)
XLA Ops:
  0.0 0.0 copy-start
  0.0 1.0 %copy-done = f32[256,512]{1,0:T(8,128)S(1)} copy-done((f32[256,512]{1,0:T(8,128)S(1)}, f32[256,512]{1,0:T(8,128)}, u32[]{:S(2)}) %copy-start) | copy-done | bytes 524312
  1.0 3.4 %fusion = f32[4,2,128,256]{3,2,1,0:T(8,128)S(1)} fusion(f32[4,2,2,128,512]{4,3,2,1,0:T(8,128)} %bitcast.24, s32[]{:T(128)S(6)} %select_n.55, f32[256,512]{1,0:T(8,128)S(1)} %copy-done), kind=kOutput, calls=%fused_computation.2 | convolution fusion | flops 1610612736 | bytes 3670020 | tf_op jit(solution)/shard_map/dot_general | solution.py:27
  4.5 2.6 %collective-permute-start = (f32[4,2,128,256]{3,2,1,0:T(8,128)S(1)}, f32[4,2,128,256]{3,2,1,0:T(8,128)S(1)}, u32[]{:S(2)}, u32[]{:S(2)}) collective-permute-start(f32[4,2,128,256]{3,2,1,0:T(8,128)S(1)} %fusion), channel_id=1, source_target_pairs={{0,1},{1,0},{2,3},{3,2},{4,5},{5,4},{6,7},{7,6},{8,9},{9,8},{10,11... | collective-permute-start | bytes 3145736 | tf_op jit(solution)/shard_map/ppermute | solution.py:13
  7.1 0.0 copy-start.2
  7.1 0.0 copy-start.1
  7.1 3.4 %fusion.2 = f32[4,2,128,256]{3,2,1,0:T(8,128)S(1)} fusion(f32[4,2,2,128,512]{4,3,2,1,0:T(8,128)} %bitcast.25, s32[]{:T(128)S(6)} %select_n.54, f32[256,512]{1,0:T(8,128)S(1)} %copy-done), kind=kOutput, calls=%fused_computation.4 | convolution fusion | flops 1610612736 | bytes 3670020 | tf_op jit(solution)/shard_map/dot_general | solution.py:27
  10.5 0.0 collective-permute-done
  10.5 1.1 %add.67 = f32[4,2,128,256]{3,2,1,0:T(8,128)} add(f32[4,2,128,256]{3,2,1,0:T(8,128)S(1)} %fusion.2, f32[4,2,128,256]{3,2,1,0:T(8,128)S(1)} %collective-permute-done) | non-fusion elementwise | flops 262144 | bytes 3145728 | tf_op jit(solution)/shard_map/add | solution.py:36
  11.7 4.0 %all-to-all-start = ((f32[4,2,128,256]{3,2,1,0:T(8,128)}), f32[4,2,128,256]{3,2,1,0:T(8,128)S(1)}, u32[]{:S(2)}, u32[]{:S(2)}) async-start(f32[4,2,128,256]{3,2,1,0:T(8,128)} %add.67), calls=%async_computation | async-start | bytes 2097152 | tf_op jit(solution)/shard_map/all_to_all | solution.py:37
  15.7 14.9 %all-to-all-done = f32[4,2,128,256]{3,2,1,0:T(8,128)S(1)} async-done(((f32[4,2,128,256]{3,2,1,0:T(8,128)}), f32[4,2,128,256]{3,2,1,0:T(8,128)S(1)}, u32[]{:S(2)}, u32[]{:S(2)}) %all-to-all-start) | async-done | bytes 1048608 | tf_op jit(solution)/shard_map/all_to_all | solution.py:37
  30.6 0.1 reduce_sum.9
  30.7 8.8 %collective-permute-start.2 = (f32[128,256]{1,0:T(8,128)S(1)}, f32[128,256]{1,0:T(8,128)S(1)}, u32[]{:S(2)}, u32[]{:S(2)}) collective-permute-start(f32[128,256]{1,0:T(8,128)S(1)} %get-tuple-element.10), channel_id=1, source_target_pairs={{0,256},{16,272},{32,288},{48,304},{64,320},{80,336},{96,352},{112... | collective-permute-start | bytes 393224 | tf_op jit(solution)/shard_map/ppermute | solution.py:13
  39.5 6.1 %collective-permute-start.3 = (f32[128,256]{1,0:T(8,128)S(1)}, f32[128,256]{1,0:T(8,128)S(1)}, u32[]{:S(2)}, u32[]{:S(2)}) collective-permute-start(f32[128,256]{1,0:T(8,128)S(1)} %get-tuple-element.9), channel_id=1, source_target_pairs={{0,258},{1,259},{2,256},{3,257},{4,262},{5,263},{6,260},{7,261},{8... | collective-permute-start | bytes 393224 | tf_op jit(solution)/shard_map/ppermute | solution.py:13
  45.7 3.7 %collective-permute-start.1 = (f32[128,256]{1,0:T(8,128)S(1)}, f32[128,256]{1,0:T(8,128)S(1)}, u32[]{:S(2)}, u32[]{:S(2)}) collective-permute-start(f32[128,256]{1,0:T(8,128)S(1)} %get-tuple-element.9), channel_id=1, source_target_pairs={{0,2},{1,3},{2,0},{3,1},{4,6},{5,7},{6,4},{7,5},{8,10},{9,11},{10,... | collective-permute-start | bytes 393224 | tf_op jit(solution)/shard_map/ppermute | solution.py:13
  49.4 0.4 collective-permute-done.2
  49.9 20.1 %collective-permute-done.3 = f32[128,256]{1,0:T(8,128)S(1)} collective-permute-done((f32[128,256]{1,0:T(8,128)S(1)}, f32[128,256]{1,0:T(8,128)S(1)}, u32[]{:S(2)}, u32[]{:S(2)}) %collective-permute-start.3) | collective-permute-done | bytes 131104 | tf_op jit(solution)/shard_map/ppermute | solution.py:13
  70.0 0.8 %gather_fusion = f32[128,256]{1,0:T(8,128)S(1)} fusion(f32[128,256]{1,0:T(8,128)S(1)} %add.76, s32[1024]{0:T(1024)S(1)} %pad_clamp_fusion.1), kind=kCustom, calls=%fused_computation | custom fusion | bytes 262656 | tf_op jit(solution)/shard_map/jit(_take)/gather | solution.py:52
  70.8 0.1 broadcast_select_fusion
  70.9 0.1 copy.7
  71.0 0.7 %gather_fusion.1 = f32[256,128]{1,0:T(8,128)S(1)} fusion(f32[128,256]{0,1:T(8,128)S(1)} %copy.7, s32[1024]{0:T(1024)S(1)} %pad_clamp_fusion), kind=kCustom, calls=%fused_computation.1 | custom fusion | bytes 263168 | tf_op jit(solution)/shard_map/jit(_take)/gather | solution.py:52
  71.7 0.1 copy.8
  71.8 0.0 collective-permute-done.1
  71.8 0.7 bitcast_add_fusion
  (8 shorter events, 0.1 us)
Async XLA Ops:
  0.0 1.0 %copy-start = (f32[256,512]{1,0:T(8,128)S(1)}, f32[256,512]{1,0:T(8,128)}, u32[]{:S(2)}) copy-start(f32[256,512]{1,0:T(8,128)} %param.4) | copy-start | bytes 1572868
  4.5 6.1 %collective-permute-start = (f32[4,2,128,256]{3,2,1,0:T(8,128)S(1)}, f32[4,2,128,256]{3,2,1,0:T(8,128)S(1)}, u32[]{:S(2)}, u32[]{:S(2)}) collective-permute-start(f32[4,2,128,256]{3,2,1,0:T(8,128)S(1)} %fusion), channel_id=1, source_target_pairs={{0,1},{1,0},{2,3},{3,2},{4,5},{5,4},{6,7},{7,6},{8,9},{9,8},{10,11... | collective-permute-start | bytes 3145736 | tf_op jit(solution)/shard_map/ppermute | solution.py:13
  7.1 8.6 %copy-start.2 = (s32[128]{0:T(128)S(1)}, s32[128]{0:T(128)}, u32[]{:S(2)}) copy-start(s32[128]{0:T(128)} %param.7) | copy-start | bytes 1540
  7.1 8.6 %copy-start.1 = (s32[256]{0:T(256)S(1)}, s32[256]{0:T(256)}, u32[]{:S(2)}) copy-start(s32[256]{0:T(256)} %param.6) | copy-start | bytes 3076
  11.7 18.9 %all-to-all-start = ((f32[4,2,128,256]{3,2,1,0:T(8,128)}), f32[4,2,128,256]{3,2,1,0:T(8,128)S(1)}, u32[]{:S(2)}, u32[]{:S(2)}) async-start(f32[4,2,128,256]{3,2,1,0:T(8,128)} %add.67), calls=%async_computation | async-start | bytes 2097152 | tf_op jit(solution)/shard_map/all_to_all | solution.py:37
  30.7 19.2 %collective-permute-start.2 = (f32[128,256]{1,0:T(8,128)S(1)}, f32[128,256]{1,0:T(8,128)S(1)}, u32[]{:S(2)}, u32[]{:S(2)}) collective-permute-start(f32[128,256]{1,0:T(8,128)S(1)} %get-tuple-element.10), channel_id=1, source_target_pairs={{0,256},{16,272},{32,288},{48,304},{64,320},{80,336},{96,352},{112... | collective-permute-start | bytes 393224 | tf_op jit(solution)/shard_map/ppermute | solution.py:13
  39.5 30.5 %collective-permute-start.3 = (f32[128,256]{1,0:T(8,128)S(1)}, f32[128,256]{1,0:T(8,128)S(1)}, u32[]{:S(2)}, u32[]{:S(2)}) collective-permute-start(f32[128,256]{1,0:T(8,128)S(1)} %get-tuple-element.9), channel_id=1, source_target_pairs={{0,258},{1,259},{2,256},{3,257},{4,262},{5,263},{6,260},{7,261},{8... | collective-permute-start | bytes 393224 | tf_op jit(solution)/shard_map/ppermute | solution.py:13
  45.7 26.1 %collective-permute-start.1 = (f32[128,256]{1,0:T(8,128)S(1)}, f32[128,256]{1,0:T(8,128)S(1)}, u32[]{:S(2)}, u32[]{:S(2)}) collective-permute-start(f32[128,256]{1,0:T(8,128)S(1)} %get-tuple-element.9), channel_id=1, source_target_pairs={{0,2},{1,3},{2,0},{3,1},{4,6},{5,7},{6,4},{7,5},{8,10},{9,11},{10,... | collective-permute-start | bytes 393224 | tf_op jit(solution)/shard_map/ppermute | solution.py:13

commit v8 on v7

--- a/solution.py
+++ b/solution.py
@@ -38,18 +38,18 @@
     mine = lax.dynamic_index_in_dim(s2, zh, axis=0, keepdims=False)
     other = lax.dynamic_index_in_dim(s2, 1 - zh, axis=0, keepdims=False)
     half = pair_count // 2
-    from_zh = moved(other, LOOP, lambda i: i ^ 2)
-    from_pair = moved(mine, PAIR, lambda i: (i + half) % pair_count)
     from_diag = moved(
         other,
         PAIR + LOOP,
         lambda i: ((i // loop_count + half) % pair_count) * loop_count + ((i % loop_count) ^ 2),
     )
-    ladder = mine + from_zh
-    mirror = from_pair + from_diag
     swap_local = virtual_swap - j * ab_local
     partner_local = pair_partner % ij_local
-    mirror = jnp.take(jnp.take(mirror, swap_local, axis=0), partner_local, axis=1)
+    inverse = jnp.zeros((ij_local,), jnp.int32).at[partner_local].set(jnp.arange(ij_local, dtype=jnp.int32))
+    to_pair = jnp.take(jnp.take(mine, swap_local, axis=0), inverse, axis=1) + from_diag
+    from_pair = moved(to_pair, PAIR, lambda i: (i + half) % pair_count)
+    ladder = mine + from_pair
+    mirror = jnp.take(jnp.take(from_diag, swap_local, axis=0), partner_local, axis=1)
     return ladder + mirror
 
 

time: 72.9 us -> 76.3 us (1.047)
  the two profiles are of different devices: /device:TPU:105 before, /device:TPU:1 now
where the time goes in v8:
time: 76.3 us; the launch traced here: 76 us
  waiting for transfers between devices  34.5 us (45%)
  starting transfers between devices  25.5 us (33%)
  matrix products  7.82 us (10%)
  local copies, waits for them, and re-layouts  5.82 us (8%)
  other arithmetic  2.06 us (3%)
    ppermute x3, starting transfers between devices, moved(): return lax.ppermute(x, axis, [(i, target(i)) for i in range(count)])  22 us
    ppermute x3, waiting for transfers between devices, moved(): return lax.ppermute(x, axis, [(i, target(i)) for i in range(count)])  20.8 us
    all_to_all x1, waiting for transfers between devices, local(): lax.all_to_all(s1, 'x', 0, 0, tiled=True).reshape(X, ZH, ab_local, ij_local)  13.7 us
    dot_general x2, matrix products, product(): lax.dot_general(rows.reshape(X * ZH * ab_local, integrals.shape[1]), ampl...  7.82 us
    all_to_all x1, starting transfers between devices, local(): lax.all_to_all(s1, 'x', 0, 0, tiled=True).reshape(X, ZH, ab_local, ij_local)  3.51 us
  transfers between devices with their start and end apart: 4, of which 3 were waited for; matrix products, arithmetic and copies ran while one was open for 9% of the time, Pallas kernels for 0%

profile of v8, /device:TPU:1, one launch (start us, length us, event | category | flops | bytes accessed | tf_op | source)
XLA Modules:
  0.0 76.0 jit_solution(12272544593754305843)
XLA Ops:
  0.0 1.0 %copy-done = f32[256,512]{1,0:T(8,128)S(1)} copy-done((f32[256,512]{1,0:T(8,128)S(1)}, f32[256,512]{1,0:T(8,128)}, u32[]{:S(2)}) %copy-start) | copy-done | bytes 524312
  1.0 4.4 %fusion = f32[4,2,128,256]{3,2,1,0:T(8,128)} fusion(f32[4,2,2,128,512]{4,3,2,1,0:T(8,128)} %bitcast.26, s32[]{:T(128)S(6)} %select_n.54, f32[256,512]{1,0:T(8,128)S(1)} %copy-done), kind=kOutput, calls=%fused_computation.5 | convolution fusion | flops 1610612736 | bytes 3670020 | tf_op jit(solution)/shard_map/dot_general | solution.py:27
  5.4 8.7 %collective-permute-start = (f32[4,2,128,256]{3,2,1,0:T(8,128)}, f32[4,2,128,256]{3,2,1,0:T(8,128)S(1)}, u32[]{:S(2)}, u32[]{:S(2)}) collective-permute-start(f32[4,2,128,256]{3,2,1,0:T(8,128)} %fusion), channel_id=1, source_target_pairs={{0,1},{1,0},{2,3},{3,2},{4,5},{5,4},{6,7},{7,6},{8,9},{9,8},{10,11... | collective-permute-start | bytes 3145736 | tf_op jit(solution)/shard_map/ppermute | solution.py:13
  14.2 0.0 copy-start.1
  14.2 3.4 %fusion.2 = f32[4,2,128,256]{3,2,1,0:T(8,128)S(1)} fusion(f32[4,2,2,128,512]{4,3,2,1,0:T(8,128)} %bitcast.27, s32[]{:T(128)S(6)} %select_n.53, f32[256,512]{1,0:T(8,128)S(1)} %copy-done), kind=kOutput, calls=%fused_computation.7 | convolution fusion | flops 1610612736 | bytes 3670020 | tf_op jit(solution)/shard_map/dot_general | solution.py:27
  17.7 1.1 %add.69 = f32[4,2,128,256]{3,2,1,0:T(8,128)} add(f32[4,2,128,256]{3,2,1,0:T(8,128)S(1)} %fusion.2, f32[4,2,128,256]{3,2,1,0:T(8,128)S(1)} %collective-permute-done) | non-fusion elementwise | flops 262144 | bytes 3145728 | tf_op jit(solution)/shard_map/add | solution.py:36
  18.8 3.5 %all-to-all-start = ((f32[4,2,128,256]{3,2,1,0:T(8,128)}), f32[4,2,128,256]{3,2,1,0:T(8,128)S(1)}, u32[]{:S(2)}, u32[]{:S(2)}) async-start(f32[4,2,128,256]{3,2,1,0:T(8,128)} %add.69), calls=%async_computation | async-start | bytes 2097152 | tf_op jit(solution)/shard_map/all_to_all | solution.py:37
  22.4 1.4 %scatter_custom_fusion = s32[256]{0:T(256)S(1)} fusion(s32[256]{0:T(256)S(1)} %get-tuple-element.8, s32[256]{0:T(256)S(1)} %iota.3, s32[]{:T(128)} %constant.84.clone.1), kind=kCustom, calls=%fused_computation.34 | custom fusion | bytes 1028 | tf_op jit(solution)/shard_map/scatter | solution.py:48
  23.9 13.7 %all-to-all-done = f32[4,2,128,256]{3,2,1,0:T(8,128)S(1)} async-done(((f32[4,2,128,256]{3,2,1,0:T(8,128)}), f32[4,2,128,256]{3,2,1,0:T(8,128)S(1)}, u32[]{:S(2)}, u32[]{:S(2)}) %all-to-all-start) | async-done | bytes 1048608 | tf_op jit(solution)/shard_map/all_to_all | solution.py:37
  37.5 0.1 reduce_sum.9
  37.6 7.4 %collective-permute-start.1 = (f32[128,256]{1,0:T(8,128)S(1)}, f32[128,256]{1,0:T(8,128)S(1)}, u32[]{:S(2)}, u32[]{:S(2)}) collective-permute-start(f32[128,256]{1,0:T(8,128)S(1)} %get-tuple-element.12), channel_id=1, source_target_pairs={{0,258},{1,259},{2,256},{3,257},{4,262},{5,263},{6,260},{7,261},{8... | collective-permute-start | bytes 393224 | tf_op jit(solution)/shard_map/ppermute | solution.py:13
  45.0 0.8 gather_fusion
  45.8 10.4 %collective-permute-done.1 = f32[128,256]{1,0:T(8,128)S(1)} collective-permute-done((f32[128,256]{1,0:T(8,128)S(1)}, f32[128,256]{1,0:T(8,128)S(1)}, u32[]{:S(2)}, u32[]{:S(2)}) %collective-permute-start.1) | collective-permute-done | bytes 131104 | tf_op jit(solution)/shard_map/ppermute | solution.py:13
  56.2 0.8 gather_fusion.2
  56.9 0.1 broadcast_select_fusion.1
  57.0 0.1 copy.7
  57.1 0.7 gather_fusion.1
  57.8 0.1 copy.8
  58.0 5.9 %collective-permute-start.2 = (f32[128,256]{1,0:T(8,128)S(1)}, f32[128,256]{1,0:T(8,128)S(1)}, u32[]{:S(2)}, u32[]{:S(2)}) collective-permute-start(f32[128,256]{1,0:T(8,128)S(1)} %bitcast_add_fusion.1), channel_id=1, source_target_pairs={{0,256},{16,272},{32,288},{48,304},{64,320},{80,336},{96,352},{112... | collective-permute-start | bytes 393224 | tf_op jit(solution)/shard_map/ppermute | solution.py:13
  63.9 0.1 copy.9
  64.0 0.7 gather_fusion.3
  64.7 0.1 copy.10
  64.8 10.4 %collective-permute-done.2 = f32[128,256]{1,0:T(8,128)S(1)} collective-permute-done((f32[128,256]{1,0:T(8,128)S(1)}, f32[128,256]{1,0:T(8,128)S(1)}, u32[]{:S(2)}, u32[]{:S(2)}) %collective-permute-start.2) | collective-permute-done | bytes 131104 | tf_op jit(solution)/shard_map/ppermute | solution.py:13
  75.3 0.7 bitcast_add_fusion
  (15 shorter events, 0.1 us)
Async XLA Ops:
  0.0 1.0 %copy-start = (f32[256,512]{1,0:T(8,128)S(1)}, f32[256,512]{1,0:T(8,128)}, u32[]{:S(2)}) copy-start(f32[256,512]{1,0:T(8,128)} %param.8) | copy-start | bytes 1572868
  5.4 12.3 %collective-permute-start = (f32[4,2,128,256]{3,2,1,0:T(8,128)}, f32[4,2,128,256]{3,2,1,0:T(8,128)S(1)}, u32[]{:S(2)}, u32[]{:S(2)}) collective-permute-start(f32[4,2,128,256]{3,2,1,0:T(8,128)} %fusion), channel_id=1, source_target_pairs={{0,1},{1,0},{2,3},{3,2},{4,5},{5,4},{6,7},{7,6},{8,9},{9,8},{10,11... | collective-permute-start | bytes 3145736 | tf_op jit(solution)/shard_map/ppermute | solution.py:13
  14.2 8.2 %copy-start.1 = (s32[256]{0:T(256)S(1)}, s32[256]{0:T(256)}, u32[]{:S(2)}) copy-start(s32[256]{0:T(256)} %param.10) | copy-start | bytes 3076
  14.2 9.6 %copy-start.2 = (s32[128]{0:T(128)S(1)}, s32[128]{0:T(128)}, u32[]{:S(2)}) copy-start(s32[128]{0:T(128)} %param.11) | copy-start | bytes 1540
  18.8 18.7 %all-to-all-start = ((f32[4,2,128,256]{3,2,1,0:T(8,128)}), f32[4,2,128,256]{3,2,1,0:T(8,128)S(1)}, u32[]{:S(2)}, u32[]{:S(2)}) async-start(f32[4,2,128,256]{3,2,1,0:T(8,128)} %add.69), calls=%async_computation | async-start | bytes 2097152 | tf_op jit(solution)/shard_map/all_to_all | solution.py:37
  37.6 18.5 %collective-permute-start.1 = (f32[128,256]{1,0:T(8,128)S(1)}, f32[128,256]{1,0:T(8,128)S(1)}, u32[]{:S(2)}, u32[]{:S(2)}) collective-permute-start(f32[128,256]{1,0:T(8,128)S(1)} %get-tuple-element.12), channel_id=1, source_target_pairs={{0,258},{1,259},{2,256},{3,257},{4,262},{5,263},{6,260},{7,261},{8... | collective-permute-start | bytes 393224 | tf_op jit(solution)/shard_map/ppermute | solution.py:13
  58.0 17.3 %collective-permute-start.2 = (f32[128,256]{1,0:T(8,128)S(1)}, f32[128,256]{1,0:T(8,128)S(1)}, u32[]{:S(2)}, u32[]{:S(2)}) collective-permute-start(f32[128,256]{1,0:T(8,128)S(1)} %bitcast_add_fusion.1), channel_id=1, source_target_pairs={{0,256},{16,272},{32,288},{48,304},{64,320},{80,336},{96,352},{112... | collective-permute-start | bytes 393224 | tf_op jit(solution)/shard_map/ppermute | solution.py:13

commit v9 on v7

--- a/solution.py
+++ b/solution.py
@@ -2,6 +2,7 @@
 import jax.numpy as jnp
 from jax import lax
 from jax.sharding import Mesh, PartitionSpec as P
+
 
 X, ZH, CORE = 4, 2, 2
 PAIR = ("zl_hi", "zl_lo", "y")
@@ -13,13 +14,13 @@
     return lax.ppermute(x, axis, [(i, target(i)) for i in range(count)])
 
 
-def local(amplitudes, integrals, pair_partner, virtual_swap):
+def body(amplitudes, integrals, pair_partner, virtual_swap):
     loop_count = lax.axis_size(LOOP)
     pair_count = lax.axis_size(PAIR)
     ab_local = integrals.shape[0] // loop_count
     ij_local = amplitudes.shape[0]
     j = lax.axis_index(LOOP)
-    x, zh, c = j // (ZH * CORE), (j // CORE) % ZH, j % CORE
+    zh, c = (j // CORE) % ZH, j % CORE
     blocks = integrals.reshape(X, ZH, CORE, ab_local, integrals.shape[1])
 
     def product(core):
@@ -54,8 +55,8 @@
 
 
 def solution(mesh):
-    pair, loop = mesh.devices.shape
+    pair, _ = mesh.devices.shape
     fine = Mesh(mesh.devices.reshape(2, pair // (2 * 4), 4, X, ZH, CORE), PAIR + LOOP)
     in_specs = (P(PAIR, LOOP), P(None, LOOP), P(PAIR), P(LOOP))
     out_specs = P(LOOP, PAIR)
-    return jax.shard_map(local, mesh=fine, in_specs=in_specs, out_specs=out_specs, check_vma=False)
+    return jax.shard_map(body, mesh=fine, in_specs=in_specs, out_specs=out_specs, check_vma=False)

time: 72.9 us -> 72.9 us (level)
  the two profiles are of different devices: /device:TPU:105 before, /device:TPU:97 now
where the time goes in v9:
time: 72.9 us; the launch traced here: 72.5 us
  waiting for transfers between devices  35.4 us (49%)
  starting transfers between devices  25.3 us (35%)
  matrix products  6.85 us (9%)
  local copies, waits for them, and re-layouts  2.75 us (4%)
  other arithmetic  2.03 us (3%)
    ppermute x4, starting transfers between devices, moved(): return lax.ppermute(x, axis, [(i, target(i)) for i in range(count)])  21.3 us
    ppermute x4, waiting for transfers between devices, moved(): return lax.ppermute(x, axis, [(i, target(i)) for i in range(count)])  20.6 us
    all_to_all x1, waiting for transfers between devices, body(): lax.all_to_all(s1, 'x', 0, 0, tiled=True).reshape(X, ZH, ab_local, ij_local)  14.9 us
    dot_general x2, matrix products, product(): lax.dot_general(rows.reshape(X * ZH * ab_local, integrals.shape[1]), ampl...  6.85 us
    all_to_all x1, starting transfers between devices, body(): lax.all_to_all(s1, 'x', 0, 0, tiled=True).reshape(X, ZH, ab_local, ij_local)  4.01 us
  transfers between devices with their start and end apart: 5, of which 3 were waited for; matrix products, arithmetic and copies ran while one was open for 7% of the time, Pallas kernels for 0%

profile of v9, /device:TPU:97, one launch (start us, length us, event | category | flops | bytes accessed | tf_op | source)
XLA Modules:
  0.0 72.5 jit_solution(13543477614209400853)
XLA Ops:
  0.0 0.0 copy-start
  0.0 1.0 %copy-done = f32[256,512]{1,0:T(8,128)S(1)} copy-done((f32[256,512]{1,0:T(8,128)S(1)}, f32[256,512]{1,0:T(8,128)}, u32[]{:S(2)}) %copy-start) | copy-done | bytes 524312
  1.0 3.4 %fusion = f32[4,2,128,256]{3,2,1,0:T(8,128)S(1)} fusion(f32[4,2,2,128,512]{4,3,2,1,0:T(8,128)} %bitcast.24, s32[]{:T(128)S(6)} %select_n.55, f32[256,512]{1,0:T(8,128)S(1)} %copy-done), kind=kOutput, calls=%fused_computation.2 | convolution fusion | flops 1610612736 | bytes 3670020 | tf_op jit(solution)/shard_map/dot_general | solution.py:28
  4.5 2.6 %collective-permute-start = (f32[4,2,128,256]{3,2,1,0:T(8,128)S(1)}, f32[4,2,128,256]{3,2,1,0:T(8,128)S(1)}, u32[]{:S(2)}, u32[]{:S(2)}) collective-permute-start(f32[4,2,128,256]{3,2,1,0:T(8,128)S(1)} %fusion), channel_id=1, source_target_pairs={{0,1},{1,0},{2,3},{3,2},{4,5},{5,4},{6,7},{7,6},{8,9},{9,8},{10,11... | collective-permute-start | bytes 3145736 | tf_op jit(solution)/shard_map/ppermute | solution.py:14
  7.1 0.0 copy-start.2
  7.1 0.0 copy-start.1
  7.1 3.4 %fusion.2 = f32[4,2,128,256]{3,2,1,0:T(8,128)S(1)} fusion(f32[4,2,2,128,512]{4,3,2,1,0:T(8,128)} %bitcast.25, s32[]{:T(128)S(6)} %select_n.54, f32[256,512]{1,0:T(8,128)S(1)} %copy-done), kind=kOutput, calls=%fused_computation.4 | convolution fusion | flops 1610612736 | bytes 3670020 | tf_op jit(solution)/shard_map/dot_general | solution.py:28
  10.5 0.0 collective-permute-done
  10.5 1.1 %add.67 = f32[4,2,128,256]{3,2,1,0:T(8,128)} add(f32[4,2,128,256]{3,2,1,0:T(8,128)S(1)} %fusion.2, f32[4,2,128,256]{3,2,1,0:T(8,128)S(1)} %collective-permute-done) | non-fusion elementwise | flops 262144 | bytes 3145728 | tf_op jit(solution)/shard_map/add | solution.py:37
  11.7 4.0 %all-to-all-start = ((f32[4,2,128,256]{3,2,1,0:T(8,128)}), f32[4,2,128,256]{3,2,1,0:T(8,128)S(1)}, u32[]{:S(2)}, u32[]{:S(2)}) async-start(f32[4,2,128,256]{3,2,1,0:T(8,128)} %add.67), calls=%async_computation | async-start | bytes 2097152 | tf_op jit(solution)/shard_map/all_to_all | solution.py:38
  15.7 14.9 %all-to-all-done = f32[4,2,128,256]{3,2,1,0:T(8,128)S(1)} async-done(((f32[4,2,128,256]{3,2,1,0:T(8,128)}), f32[4,2,128,256]{3,2,1,0:T(8,128)S(1)}, u32[]{:S(2)}, u32[]{:S(2)}) %all-to-all-start) | async-done | bytes 1048608 | tf_op jit(solution)/shard_map/all_to_all | solution.py:38
  30.6 0.1 reduce_sum.9
  30.7 8.8 %collective-permute-start.2 = (f32[128,256]{1,0:T(8,128)S(1)}, f32[128,256]{1,0:T(8,128)S(1)}, u32[]{:S(2)}, u32[]{:S(2)}) collective-permute-start(f32[128,256]{1,0:T(8,128)S(1)} %get-tuple-element.10), channel_id=1, source_target_pairs={{0,256},{16,272},{32,288},{48,304},{64,320},{80,336},{96,352},{112... | collective-permute-start | bytes 393224 | tf_op jit(solution)/shard_map/ppermute | solution.py:14
  39.5 6.1 %collective-permute-start.3 = (f32[128,256]{1,0:T(8,128)S(1)}, f32[128,256]{1,0:T(8,128)S(1)}, u32[]{:S(2)}, u32[]{:S(2)}) collective-permute-start(f32[128,256]{1,0:T(8,128)S(1)} %get-tuple-element.9), channel_id=1, source_target_pairs={{0,258},{1,259},{2,256},{3,257},{4,262},{5,263},{6,260},{7,261},{8... | collective-permute-start | bytes 393224 | tf_op jit(solution)/shard_map/ppermute | solution.py:14
  45.7 3.7 %collective-permute-start.1 = (f32[128,256]{1,0:T(8,128)S(1)}, f32[128,256]{1,0:T(8,128)S(1)}, u32[]{:S(2)}, u32[]{:S(2)}) collective-permute-start(f32[128,256]{1,0:T(8,128)S(1)} %get-tuple-element.9), channel_id=1, source_target_pairs={{0,2},{1,3},{2,0},{3,1},{4,6},{5,7},{6,4},{7,5},{8,10},{9,11},{10,... | collective-permute-start | bytes 393224 | tf_op jit(solution)/shard_map/ppermute | solution.py:14
  49.4 0.4 collective-permute-done.2
  49.9 20.1 %collective-permute-done.3 = f32[128,256]{1,0:T(8,128)S(1)} collective-permute-done((f32[128,256]{1,0:T(8,128)S(1)}, f32[128,256]{1,0:T(8,128)S(1)}, u32[]{:S(2)}, u32[]{:S(2)}) %collective-permute-start.3) | collective-permute-done | bytes 131104 | tf_op jit(solution)/shard_map/ppermute | solution.py:14
  70.0 0.8 %gather_fusion = f32[128,256]{1,0:T(8,128)S(1)} fusion(f32[128,256]{1,0:T(8,128)S(1)} %add.76, s32[1024]{0:T(1024)S(1)} %pad_clamp_fusion.1), kind=kCustom, calls=%fused_computation | custom fusion | bytes 262656 | tf_op jit(solution)/shard_map/jit(_take)/gather | solution.py:53
  70.8 0.1 broadcast_select_fusion
  70.9 0.1 copy.7
  71.0 0.7 %gather_fusion.1 = f32[256,128]{1,0:T(8,128)S(1)} fusion(f32[128,256]{0,1:T(8,128)S(1)} %copy.7, s32[1024]{0:T(1024)S(1)} %pad_clamp_fusion), kind=kCustom, calls=%fused_computation.1 | custom fusion | bytes 263168 | tf_op jit(solution)/shard_map/jit(_take)/gather | solution.py:53
  71.7 0.1 copy.8
  71.8 0.0 collective-permute-done.1
  71.8 0.7 bitcast_add_fusion
  (8 shorter events, 0.1 us)
Async XLA Ops:
  0.0 1.0 %copy-start = (f32[256,512]{1,0:T(8,128)S(1)}, f32[256,512]{1,0:T(8,128)}, u32[]{:S(2)}) copy-start(f32[256,512]{1,0:T(8,128)} %param.4) | copy-start | bytes 1572868
  4.5 6.1 %collective-permute-start = (f32[4,2,128,256]{3,2,1,0:T(8,128)S(1)}, f32[4,2,128,256]{3,2,1,0:T(8,128)S(1)}, u32[]{:S(2)}, u32[]{:S(2)}) collective-permute-start(f32[4,2,128,256]{3,2,1,0:T(8,128)S(1)} %fusion), channel_id=1, source_target_pairs={{0,1},{1,0},{2,3},{3,2},{4,5},{5,4},{6,7},{7,6},{8,9},{9,8},{10,11... | collective-permute-start | bytes 3145736 | tf_op jit(solution)/shard_map/ppermute | solution.py:14
  7.1 8.6 %copy-start.2 = (s32[128]{0:T(128)S(1)}, s32[128]{0:T(128)}, u32[]{:S(2)}) copy-start(s32[128]{0:T(128)} %param.7) | copy-start | bytes 1540
  7.1 8.6 %copy-start.1 = (s32[256]{0:T(256)S(1)}, s32[256]{0:T(256)}, u32[]{:S(2)}) copy-start(s32[256]{0:T(256)} %param.6) | copy-start | bytes 3076
  11.7 18.9 %all-to-all-start = ((f32[4,2,128,256]{3,2,1,0:T(8,128)}), f32[4,2,128,256]{3,2,1,0:T(8,128)S(1)}, u32[]{:S(2)}, u32[]{:S(2)}) async-start(f32[4,2,128,256]{3,2,1,0:T(8,128)} %add.67), calls=%async_computation | async-start | bytes 2097152 | tf_op jit(solution)/shard_map/all_to_all | solution.py:38
  30.7 19.2 %collective-permute-start.2 = (f32[128,256]{1,0:T(8,128)S(1)}, f32[128,256]{1,0:T(8,128)S(1)}, u32[]{:S(2)}, u32[]{:S(2)}) collective-permute-start(f32[128,256]{1,0:T(8,128)S(1)} %get-tuple-element.10), channel_id=1, source_target_pairs={{0,256},{16,272},{32,288},{48,304},{64,320},{80,336},{96,352},{112... | collective-permute-start | bytes 393224 | tf_op jit(solution)/shard_map/ppermute | solution.py:14
  39.5 30.5 %collective-permute-start.3 = (f32[128,256]{1,0:T(8,128)S(1)}, f32[128,256]{1,0:T(8,128)S(1)}, u32[]{:S(2)}, u32[]{:S(2)}) collective-permute-start(f32[128,256]{1,0:T(8,128)S(1)} %get-tuple-element.9), channel_id=1, source_target_pairs={{0,258},{1,259},{2,256},{3,257},{4,262},{5,263},{6,260},{7,261},{8... | collective-permute-start | bytes 393224 | tf_op jit(solution)/shard_map/ppermute | solution.py:14
  45.7 26.1 %collective-permute-start.1 = (f32[128,256]{1,0:T(8,128)S(1)}, f32[128,256]{1,0:T(8,128)S(1)}, u32[]{:S(2)}, u32[]{:S(2)}) collective-permute-start(f32[128,256]{1,0:T(8,128)S(1)} %get-tuple-element.9), channel_id=1, source_target_pairs={{0,2},{1,3},{2,0},{3,1},{4,6},{5,7},{6,4},{7,5},{8,10},{9,11},{10,... | collective-permute-start | bytes 393224 | tf_op jit(solution)/shard_map/ppermute | solution.py:14

commit v10 on v7

--- a/solution.py
+++ b/solution.py
@@ -28,7 +28,7 @@
             rows.reshape(X * ZH * ab_local, integrals.shape[1]),
             amplitudes,
             (((1,), (1,)), ((), ())),
-            precision=lax.Precision.HIGHEST,
+            precision=lax.Precision.HIGH,
             preferred_element_type=jnp.float32,
         ).reshape(X, ZH, ab_local, ij_local)
 

time: 72.9 us -> 71.3 us (0.978)
  the two profiles are of different devices: /device:TPU:105 before, /device:TPU:121 now
where the time goes in v10:
time: 71.3 us; the launch traced here: 70.9 us
  waiting for transfers between devices  35.4 us (50%)
  starting transfers between devices  25.3 us (35%)
  matrix products  5.25 us (7%)
  local copies, waits for them, and re-layouts  2.75 us (4%)
  other arithmetic  2.03 us (3%)
    ppermute x4, starting transfers between devices, moved(): return lax.ppermute(x, axis, [(i, target(i)) for i in range(count)])  21.3 us
    ppermute x4, waiting for transfers between devices, moved(): return lax.ppermute(x, axis, [(i, target(i)) for i in range(count)])  20.6 us
    all_to_all x1, waiting for transfers between devices, local(): lax.all_to_all(s1, 'x', 0, 0, tiled=True).reshape(X, ZH, ab_local, ij_local)  14.9 us
    dot_general x2, matrix products, product(): lax.dot_general(rows.reshape(X * ZH * ab_local, integrals.shape[1]), ampl...  5.25 us
    all_to_all x1, starting transfers between devices, local(): lax.all_to_all(s1, 'x', 0, 0, tiled=True).reshape(X, ZH, ab_local, ij_local)  4.01 us
  transfers between devices with their start and end apart: 5, of which 3 were waited for; matrix products, arithmetic and copies ran while one was open for 6% of the time, Pallas kernels for 0%

profile of v10, /device:TPU:121, one launch (start us, length us, event | category | flops | bytes accessed | tf_op | source)
XLA Modules:
  0.0 70.9 jit_solution(16658697561674839572)
XLA Ops:
  0.0 0.0 copy-start
  0.0 1.0 %copy-done = f32[256,512]{1,0:T(8,128)S(1)} copy-done((f32[256,512]{1,0:T(8,128)S(1)}, f32[256,512]{1,0:T(8,128)}, u32[]{:S(2)}) %copy-start) | copy-done | bytes 524312
  1.0 2.6 %fusion = f32[4,2,128,256]{3,2,1,0:T(8,128)S(1)} fusion(f32[4,2,2,128,512]{4,3,2,1,0:T(8,128)} %bitcast.24, s32[]{:T(128)S(6)} %select_n.55, f32[256,512]{1,0:T(8,128)S(1)} %copy-done), kind=kOutput, calls=%fused_computation.2 | convolution fusion | flops 805306368 | bytes 3670020 | tf_op jit(solution)/shard_map/dot_general | solution.py:27
  3.7 2.6 %collective-permute-start = (f32[4,2,128,256]{3,2,1,0:T(8,128)S(1)}, f32[4,2,128,256]{3,2,1,0:T(8,128)S(1)}, u32[]{:S(2)}, u32[]{:S(2)}) collective-permute-start(f32[4,2,128,256]{3,2,1,0:T(8,128)S(1)} %fusion), channel_id=1, source_target_pairs={{0,1},{1,0},{2,3},{3,2},{4,5},{5,4},{6,7},{7,6},{8,9},{9,8},{10,11... | collective-permute-start | bytes 3145736 | tf_op jit(solution)/shard_map/ppermute | solution.py:13
  6.3 0.0 copy-start.2
  6.3 0.0 copy-start.1
  6.3 2.6 %fusion.2 = f32[4,2,128,256]{3,2,1,0:T(8,128)S(1)} fusion(f32[4,2,2,128,512]{4,3,2,1,0:T(8,128)} %bitcast.25, s32[]{:T(128)S(6)} %select_n.54, f32[256,512]{1,0:T(8,128)S(1)} %copy-done), kind=kOutput, calls=%fused_computation.4 | convolution fusion | flops 805306368 | bytes 3670020 | tf_op jit(solution)/shard_map/dot_general | solution.py:27
  8.9 0.0 collective-permute-done
  8.9 1.1 %add.67 = f32[4,2,128,256]{3,2,1,0:T(8,128)} add(f32[4,2,128,256]{3,2,1,0:T(8,128)S(1)} %fusion.2, f32[4,2,128,256]{3,2,1,0:T(8,128)S(1)} %collective-permute-done) | non-fusion elementwise | flops 262144 | bytes 3145728 | tf_op jit(solution)/shard_map/add | solution.py:36
  10.1 4.0 %all-to-all-start = ((f32[4,2,128,256]{3,2,1,0:T(8,128)}), f32[4,2,128,256]{3,2,1,0:T(8,128)S(1)}, u32[]{:S(2)}, u32[]{:S(2)}) async-start(f32[4,2,128,256]{3,2,1,0:T(8,128)} %add.67), calls=%async_computation | async-start | bytes 2097152 | tf_op jit(solution)/shard_map/all_to_all | solution.py:37
  14.1 14.9 %all-to-all-done = f32[4,2,128,256]{3,2,1,0:T(8,128)S(1)} async-done(((f32[4,2,128,256]{3,2,1,0:T(8,128)}), f32[4,2,128,256]{3,2,1,0:T(8,128)S(1)}, u32[]{:S(2)}, u32[]{:S(2)}) %all-to-all-start) | async-done | bytes 1048608 | tf_op jit(solution)/shard_map/all_to_all | solution.py:37
  29.0 0.1 reduce_sum.9
  29.1 8.8 %collective-permute-start.2 = (f32[128,256]{1,0:T(8,128)S(1)}, f32[128,256]{1,0:T(8,128)S(1)}, u32[]{:S(2)}, u32[]{:S(2)}) collective-permute-start(f32[128,256]{1,0:T(8,128)S(1)} %get-tuple-element.10), channel_id=1, source_target_pairs={{0,256},{16,272},{32,288},{48,304},{64,320},{80,336},{96,352},{112... | collective-permute-start | bytes 393224 | tf_op jit(solution)/shard_map/ppermute | solution.py:13
  37.9 6.1 %collective-permute-start.3 = (f32[128,256]{1,0:T(8,128)S(1)}, f32[128,256]{1,0:T(8,128)S(1)}, u32[]{:S(2)}, u32[]{:S(2)}) collective-permute-start(f32[128,256]{1,0:T(8,128)S(1)} %get-tuple-element.9), channel_id=1, source_target_pairs={{0,258},{1,259},{2,256},{3,257},{4,262},{5,263},{6,260},{7,261},{8... | collective-permute-start | bytes 393224 | tf_op jit(solution)/shard_map/ppermute | solution.py:13
  44.1 3.7 %collective-permute-start.1 = (f32[128,256]{1,0:T(8,128)S(1)}, f32[128,256]{1,0:T(8,128)S(1)}, u32[]{:S(2)}, u32[]{:S(2)}) collective-permute-start(f32[128,256]{1,0:T(8,128)S(1)} %get-tuple-element.9), channel_id=1, source_target_pairs={{0,2},{1,3},{2,0},{3,1},{4,6},{5,7},{6,4},{7,5},{8,10},{9,11},{10,... | collective-permute-start | bytes 393224 | tf_op jit(solution)/shard_map/ppermute | solution.py:13
  47.8 0.4 collective-permute-done.2
  48.3 20.1 %collective-permute-done.3 = f32[128,256]{1,0:T(8,128)S(1)} collective-permute-done((f32[128,256]{1,0:T(8,128)S(1)}, f32[128,256]{1,0:T(8,128)S(1)}, u32[]{:S(2)}, u32[]{:S(2)}) %collective-permute-start.3) | collective-permute-done | bytes 131104 | tf_op jit(solution)/shard_map/ppermute | solution.py:13
  68.4 0.8 %gather_fusion = f32[128,256]{1,0:T(8,128)S(1)} fusion(f32[128,256]{1,0:T(8,128)S(1)} %add.76, s32[1024]{0:T(1024)S(1)} %pad_clamp_fusion.1), kind=kCustom, calls=%fused_computation | custom fusion | bytes 262656 | tf_op jit(solution)/shard_map/jit(_take)/gather | solution.py:52
  69.2 0.1 broadcast_select_fusion
  69.3 0.1 copy.7
  69.4 0.7 %gather_fusion.1 = f32[256,128]{1,0:T(8,128)S(1)} fusion(f32[128,256]{0,1:T(8,128)S(1)} %copy.7, s32[1024]{0:T(1024)S(1)} %pad_clamp_fusion), kind=kCustom, calls=%fused_computation.1 | custom fusion | bytes 263168 | tf_op jit(solution)/shard_map/jit(_take)/gather | solution.py:52
  70.1 0.1 copy.8
  70.2 0.0 collective-permute-done.1
  70.2 0.7 bitcast_add_fusion
  (8 shorter events, 0.1 us)
Async XLA Ops:
  0.0 1.0 %copy-start = (f32[256,512]{1,0:T(8,128)S(1)}, f32[256,512]{1,0:T(8,128)}, u32[]{:S(2)}) copy-start(f32[256,512]{1,0:T(8,128)} %param.4) | copy-start | bytes 1572868
  3.7 5.3 %collective-permute-start = (f32[4,2,128,256]{3,2,1,0:T(8,128)S(1)}, f32[4,2,128,256]{3,2,1,0:T(8,128)S(1)}, u32[]{:S(2)}, u32[]{:S(2)}) collective-permute-start(f32[4,2,128,256]{3,2,1,0:T(8,128)S(1)} %fusion), channel_id=1, source_target_pairs={{0,1},{1,0},{2,3},{3,2},{4,5},{5,4},{6,7},{7,6},{8,9},{9,8},{10,11... | collective-permute-start | bytes 3145736 | tf_op jit(solution)/shard_map/ppermute | solution.py:13
  6.3 7.8 %copy-start.2 = (s32[128]{0:T(128)S(1)}, s32[128]{0:T(128)}, u32[]{:S(2)}) copy-start(s32[128]{0:T(128)} %param.7) | copy-start | bytes 1540
  6.3 7.8 %copy-start.1 = (s32[256]{0:T(256)S(1)}, s32[256]{0:T(256)}, u32[]{:S(2)}) copy-start(s32[256]{0:T(256)} %param.6) | copy-start | bytes 3076
  10.1 18.9 %all-to-all-start = ((f32[4,2,128,256]{3,2,1,0:T(8,128)}), f32[4,2,128,256]{3,2,1,0:T(8,128)S(1)}, u32[]{:S(2)}, u32[]{:S(2)}) async-start(f32[4,2,128,256]{3,2,1,0:T(8,128)} %add.67), calls=%async_computation | async-start | bytes 2097152 | tf_op jit(solution)/shard_map/all_to_all | solution.py:37
  29.1 19.2 %collective-permute-start.2 = (f32[128,256]{1,0:T(8,128)S(1)}, f32[128,256]{1,0:T(8,128)S(1)}, u32[]{:S(2)}, u32[]{:S(2)}) collective-permute-start(f32[128,256]{1,0:T(8,128)S(1)} %get-tuple-element.10), channel_id=1, source_target_pairs={{0,256},{16,272},{32,288},{48,304},{64,320},{80,336},{96,352},{112... | collective-permute-start | bytes 393224 | tf_op jit(solution)/shard_map/ppermute | solution.py:13
  37.9 30.5 %collective-permute-start.3 = (f32[128,256]{1,0:T(8,128)S(1)}, f32[128,256]{1,0:T(8,128)S(1)}, u32[]{:S(2)}, u32[]{:S(2)}) collective-permute-start(f32[128,256]{1,0:T(8,128)S(1)} %get-tuple-element.9), channel_id=1, source_target_pairs={{0,258},{1,259},{2,256},{3,257},{4,262},{5,263},{6,260},{7,261},{8... | collective-permute-start | bytes 393224 | tf_op jit(solution)/shard_map/ppermute | solution.py:13
  44.1 26.1 %collective-permute-start.1 = (f32[128,256]{1,0:T(8,128)S(1)}, f32[128,256]{1,0:T(8,128)S(1)}, u32[]{:S(2)}, u32[]{:S(2)}) collective-permute-start(f32[128,256]{1,0:T(8,128)S(1)} %get-tuple-element.9), channel_id=1, source_target_pairs={{0,2},{1,3},{2,0},{3,1},{4,6},{5,7},{6,4},{7,5},{8,10},{9,11},{10,... | collective-permute-start | bytes 393224 | tf_op jit(solution)/shard_map/ppermute | solution.py:13

commit v11 on v9

--- a/solution.py
+++ b/solution.py
@@ -35,17 +35,20 @@
 
     give = moved(product(1 - c), LOOP, lambda i: i ^ 1)
     s1 = lax.optimization_barrier(product(c)) + give
-    s2 = lax.all_to_all(s1, "x", 0, 0, tiled=True).reshape(X, ZH, ab_local, ij_local).sum(axis=0)
-    mine = lax.dynamic_index_in_dim(s2, zh, axis=0, keepdims=False)
-    other = lax.dynamic_index_in_dim(s2, 1 - zh, axis=0, keepdims=False)
+
+    def along_x(rows):
+        return lax.all_to_all(rows, "x", 0, 0, tiled=True).reshape(X, ab_local, ij_local).sum(axis=0)
+
+    other = along_x(lax.dynamic_index_in_dim(s1, 1 - zh, axis=1, keepdims=False))
     half = pair_count // 2
     from_zh = moved(other, LOOP, lambda i: i ^ 2)
-    from_pair = moved(mine, PAIR, lambda i: (i + half) % pair_count)
     from_diag = moved(
         other,
         PAIR + LOOP,
         lambda i: ((i // loop_count + half) % pair_count) * loop_count + ((i % loop_count) ^ 2),
     )
+    mine = along_x(lax.dynamic_index_in_dim(s1, zh, axis=1, keepdims=False))
+    from_pair = moved(mine, PAIR, lambda i: (i + half) % pair_count)
     ladder = mine + from_zh
     mirror = from_pair + from_diag
     swap_local = virtual_swap - j * ab_local

time: 72.9 us -> 77.7 us (1.066)
  the two profiles are of different devices: /device:TPU:97 before, /device:TPU:33 now
where the time goes in v11:
time: 77.7 us; the launch traced here: 77.3 us
  starting transfers between devices  34.5 us (44%)
  waiting for transfers between devices  29.9 us (38%)
  matrix products  7.82 us (10%)
  local copies, waits for them, and re-layouts  3.81 us (5%)
  other arithmetic  1.03 us (1%)
    ppermute x4, starting transfers between devices, moved(): return lax.ppermute(x, axis, [(i, target(i)) for i in range(count)])  27 us
    ppermute x4, waiting for transfers between devices, moved(): return lax.ppermute(x, axis, [(i, target(i)) for i in range(count)])  20.6 us
    all_to_all x2, waiting for transfers between devices, along_x(): lax.all_to_all(rows, 'x', 0, 0, tiled=True).reshape(X, ab_local, ij_local)  9.28 us
    dot_general x2, matrix products, product(): lax.dot_general(rows.reshape(X * ZH * ab_local, integrals.shape[1]), ampl...  7.82 us
    all_to_all x2, starting transfers between devices, along_x(): lax.all_to_all(rows, 'x', 0, 0, tiled=True).reshape(X, ab_local, ij_local)  7.49 us
  transfers between devices with their start and end apart: 6, of which 3 were waited for; matrix products, arithmetic and copies ran while one was open for 7% of the time, Pallas kernels for 0%

profile of v11, /device:TPU:33, one launch (start us, length us, event | category | flops | bytes accessed | tf_op | source)
XLA Modules:
  0.0 77.3 jit_solution(3369887046186163076)
XLA Ops:
  0.0 1.0 %copy-done = f32[256,512]{1,0:T(8,128)S(1)} copy-done((f32[256,512]{1,0:T(8,128)S(1)}, f32[256,512]{1,0:T(8,128)}, u32[]{:S(2)}) %copy-start) | copy-done | bytes 524312
  1.0 4.4 %fusion = f32[4,2,128,256]{3,2,1,0:T(8,128)} fusion(f32[4,2,2,128,512]{4,3,2,1,0:T(8,128)} %bitcast.24, s32[]{:T(128)S(6)} %select_n.55, f32[256,512]{1,0:T(8,128)S(1)} %copy-done), kind=kOutput, calls=%fused_computation.2 | convolution fusion | flops 1610612736 | bytes 3670020 | tf_op jit(solution)/shard_map/dot_general | solution.py:28
  5.4 2.6 %collective-permute-start = (f32[4,2,128,256]{3,2,1,0:T(8,128)}, f32[4,2,128,256]{3,2,1,0:T(8,128)S(1)}, u32[]{:S(2)}, u32[]{:S(2)}) collective-permute-start(f32[4,2,128,256]{3,2,1,0:T(8,128)} %fusion), channel_id=1, source_target_pairs={{0,1},{1,0},{2,3},{3,2},{4,5},{5,4},{6,7},{7,6},{8,9},{9,8},{10,11... | collective-permute-start | bytes 3145736 | tf_op jit(solution)/shard_map/ppermute | solution.py:14
  8.1 3.4 %fusion.2 = f32[4,2,128,256]{3,2,1,0:T(8,128)S(1)} fusion(f32[4,2,2,128,512]{4,3,2,1,0:T(8,128)} %bitcast.25, s32[]{:T(128)S(6)} %select_n.54, f32[256,512]{1,0:T(8,128)S(1)} %copy-done), kind=kOutput, calls=%fused_computation.4 | convolution fusion | flops 1610612736 | bytes 3670020 | tf_op jit(solution)/shard_map/dot_general | solution.py:28
  11.5 0.0 copy-start.2
  11.5 0.0 copy-start.1
  11.5 0.0 collective-permute-done
  11.5 0.1 add.67
  11.7 1.1 %dynamic-slice_bitcast_fusion = (f32[4,128,256]{2,1,0:T(8,128)}, f32[4,128,256]{2,1,0:T(8,128)}) fusion(f32[4,2,128,256]{3,2,1,0:T(8,128)S(1)} %add.67, s32[]{:T(128)S(6)} %select_n.59, s32[]{:T(128)S(6)} %select_n.58), kind=kLoop, calls=%fused_computation.10 | loop fusion | bytes 2097160 | tf_op jit(solution)/shard_map/jit(dynamic_index_in_dim)/squeeze | solution.py:42
  12.8 4.0 %all-to-all-start = ((f32[4,128,256]{2,1,0:T(8,128)}), f32[4,128,256]{2,1,0:T(8,128)S(1)}, u32[]{:S(2)}, u32[]{:S(2)}) async-start(f32[4,128,256]{2,1,0:T(8,128)} %get-tuple-element.10), calls=%async_computation | async-start | bytes 1048576 | tf_op jit(solution)/shard_map/all_to_all | solution.py:40
  16.8 9.3 %all-to-all-done = f32[4,128,256]{2,1,0:T(8,128)S(1)} async-done(((f32[4,128,256]{2,1,0:T(8,128)}), f32[4,128,256]{2,1,0:T(8,128)S(1)}, u32[]{:S(2)}, u32[]{:S(2)}) %all-to-all-start) | async-done | bytes 524320 | tf_op jit(solution)/shard_map/all_to_all | solution.py:40
  26.1 3.5 %all-to-all-start.1 = ((f32[4,128,256]{2,1,0:T(8,128)}), f32[4,128,256]{2,1,0:T(8,128)S(1)}, u32[]{:S(2)}, u32[]{:S(2)}) async-start(f32[4,128,256]{2,1,0:T(8,128)} %get-tuple-element.9), calls=%async_computation.1 | async-start | bytes 1048576 | tf_op jit(solution)/shard_map/all_to_all | solution.py:40
  29.6 8.8 %collective-permute-start.2 = (f32[128,256]{1,0:T(8,128)S(1)}, f32[128,256]{1,0:T(8,128)S(1)}, u32[]{:S(2)}, u32[]{:S(2)}) collective-permute-start(f32[128,256]{1,0:T(8,128)S(1)} %reduce_sum.18), channel_id=1, source_target_pairs={{0,256},{16,272},{32,288},{48,304},{64,320},{80,336},{96,352},{112... | collective-permute-start | bytes 393224 | tf_op jit(solution)/shard_map/ppermute | solution.py:14
  38.5 10.7 %collective-permute-start.3 = (f32[128,256]{1,0:T(8,128)S(1)}, f32[128,256]{1,0:T(8,128)S(1)}, u32[]{:S(2)}, u32[]{:S(2)}) collective-permute-start(f32[128,256]{1,0:T(8,128)S(1)} %reduce_sum.19), channel_id=1, source_target_pairs={{0,258},{1,259},{2,256},{3,257},{4,262},{5,263},{6,260},{7,261},{8... | collective-permute-start | bytes 393224 | tf_op jit(solution)/shard_map/ppermute | solution.py:14
  49.3 4.9 %collective-permute-start.1 = (f32[128,256]{1,0:T(8,128)S(1)}, f32[128,256]{1,0:T(8,128)S(1)}, u32[]{:S(2)}, u32[]{:S(2)}) collective-permute-start(f32[128,256]{1,0:T(8,128)S(1)} %reduce_sum.19), channel_id=1, source_target_pairs={{0,2},{1,3},{2,0},{3,1},{4,6},{5,7},{6,4},{7,5},{8,10},{9,11},{10,... | collective-permute-start | bytes 393224 | tf_op jit(solution)/shard_map/ppermute | solution.py:14
  54.2 0.0 collective-permute-done.2
  54.2 12.2 %collective-permute-done.3 = f32[128,256]{1,0:T(8,128)S(1)} collective-permute-done((f32[128,256]{1,0:T(8,128)S(1)}, f32[128,256]{1,0:T(8,128)S(1)}, u32[]{:S(2)}, u32[]{:S(2)}) %collective-permute-start.3) | collective-permute-done | bytes 131104 | tf_op jit(solution)/shard_map/ppermute | solution.py:14
  66.4 0.8 gather_fusion
  67.2 0.1 broadcast_select_fusion
  67.3 0.1 copy.7
  67.4 0.7 gather_fusion.1
  68.1 0.1 copy.8
  68.2 8.4 %collective-permute-done.1 = f32[128,256]{1,0:T(8,128)S(1)} collective-permute-done((f32[128,256]{1,0:T(8,128)S(1)}, f32[128,256]{1,0:T(8,128)S(1)}, u32[]{:S(2)}, u32[]{:S(2)}) %collective-permute-start.1) | collective-permute-done | bytes 131104 | tf_op jit(solution)/shard_map/ppermute | solution.py:14
  76.6 0.7 bitcast_add_fusion
  (11 shorter events, 0.1 us)
Async XLA Ops:
  0.0 1.0 %copy-start = (f32[256,512]{1,0:T(8,128)S(1)}, f32[256,512]{1,0:T(8,128)}, u32[]{:S(2)}) copy-start(f32[256,512]{1,0:T(8,128)} %param.4) | copy-start | bytes 1572868
  5.4 6.1 %collective-permute-start = (f32[4,2,128,256]{3,2,1,0:T(8,128)}, f32[4,2,128,256]{3,2,1,0:T(8,128)S(1)}, u32[]{:S(2)}, u32[]{:S(2)}) collective-permute-start(f32[4,2,128,256]{3,2,1,0:T(8,128)} %fusion), channel_id=1, source_target_pairs={{0,1},{1,0},{2,3},{3,2},{4,5},{5,4},{6,7},{7,6},{8,9},{9,8},{10,11... | collective-permute-start | bytes 3145736 | tf_op jit(solution)/shard_map/ppermute | solution.py:14
  11.5 18.1 %copy-start.2 = (s32[128]{0:T(128)S(1)}, s32[128]{0:T(128)}, u32[]{:S(2)}) copy-start(s32[128]{0:T(128)} %param.7) | copy-start | bytes 1540
  11.5 18.1 %copy-start.1 = (s32[256]{0:T(256)S(1)}, s32[256]{0:T(256)}, u32[]{:S(2)}) copy-start(s32[256]{0:T(256)} %param.6) | copy-start | bytes 3076
  12.8 13.3 %all-to-all-start = ((f32[4,128,256]{2,1,0:T(8,128)}), f32[4,128,256]{2,1,0:T(8,128)S(1)}, u32[]{:S(2)}, u32[]{:S(2)}) async-start(f32[4,128,256]{2,1,0:T(8,128)} %get-tuple-element.10), calls=%async_computation | async-start | bytes 1048576 | tf_op jit(solution)/shard_map/all_to_all | solution.py:40
  26.1 12.4 %all-to-all-start.1 = ((f32[4,128,256]{2,1,0:T(8,128)}), f32[4,128,256]{2,1,0:T(8,128)S(1)}, u32[]{:S(2)}, u32[]{:S(2)}) async-start(f32[4,128,256]{2,1,0:T(8,128)} %get-tuple-element.9), calls=%async_computation.1 | async-start | bytes 1048576 | tf_op jit(solution)/shard_map/all_to_all | solution.py:40
  29.6 24.5 %collective-permute-start.2 = (f32[128,256]{1,0:T(8,128)S(1)}, f32[128,256]{1,0:T(8,128)S(1)}, u32[]{:S(2)}, u32[]{:S(2)}) collective-permute-start(f32[128,256]{1,0:T(8,128)S(1)} %reduce_sum.18), channel_id=1, source_target_pairs={{0,256},{16,272},{32,288},{48,304},{64,320},{80,336},{96,352},{112... | collective-permute-start | bytes 393224 | tf_op jit(solution)/shard_map/ppermute | solution.py:14
  38.5 27.9 %collective-permute-start.3 = (f32[128,256]{1,0:T(8,128)S(1)}, f32[128,256]{1,0:T(8,128)S(1)}, u32[]{:S(2)}, u32[]{:S(2)}) collective-permute-start(f32[128,256]{1,0:T(8,128)S(1)} %reduce_sum.19), channel_id=1, source_target_pairs={{0,258},{1,259},{2,256},{3,257},{4,262},{5,263},{6,260},{7,261},{8... | collective-permute-start | bytes 393224 | tf_op jit(solution)/shard_map/ppermute | solution.py:14
  49.3 27.4 %collective-permute-start.1 = (f32[128,256]{1,0:T(8,128)S(1)}, f32[128,256]{1,0:T(8,128)S(1)}, u32[]{:S(2)}, u32[]{:S(2)}) collective-permute-start(f32[128,256]{1,0:T(8,128)S(1)} %reduce_sum.19), channel_id=1, source_target_pairs={{0,2},{1,3},{2,0},{3,1},{4,6},{5,7},{6,4},{7,5},{8,10},{9,11},{10,... | collective-permute-start | bytes 393224 | tf_op jit(solution)/shard_map/ppermute | solution.py:14

commit v12 on v10

--- a/solution.py
+++ b/solution.py
@@ -22,18 +22,18 @@
     x, zh, c = j // (ZH * CORE), (j // CORE) % ZH, j % CORE
     blocks = integrals.reshape(X, ZH, CORE, ab_local, integrals.shape[1])
 
-    def product(core):
+    def product(core, precision):
         rows = lax.dynamic_index_in_dim(blocks, core, axis=2, keepdims=False)
         return lax.dot_general(
             rows.reshape(X * ZH * ab_local, integrals.shape[1]),
             amplitudes,
             (((1,), (1,)), ((), ())),
-            precision=lax.Precision.HIGH,
+            precision=precision,
             preferred_element_type=jnp.float32,
         ).reshape(X, ZH, ab_local, ij_local)
 
-    give = moved(product(1 - c), LOOP, lambda i: i ^ 1)
-    s1 = lax.optimization_barrier(product(c)) + give
+    give = moved(product(1 - c, lax.Precision.HIGH), LOOP, lambda i: i ^ 1)
+    s1 = lax.optimization_barrier(product(c, lax.Precision.HIGHEST)) + give
     s2 = lax.all_to_all(s1, "x", 0, 0, tiled=True).reshape(X, ZH, ab_local, ij_local).sum(axis=0)
     mine = lax.dynamic_index_in_dim(s2, zh, axis=0, keepdims=False)
     other = lax.dynamic_index_in_dim(s2, 1 - zh, axis=0, keepdims=False)

time: 71.3 us -> 72.1 us (1.011)
  the two profiles are of different devices: /device:TPU:121 before, /device:TPU:105 now
where the time goes in v12:
time: 72.1 us; the launch traced here: 71.7 us
  waiting for transfers between devices  35.4 us (49%)
  starting transfers between devices  25.3 us (35%)
  matrix products  6.05 us (8%)
  local copies, waits for them, and re-layouts  2.75 us (4%)
  other arithmetic  2.03 us (3%)
    ppermute x4, starting transfers between devices, moved(): return lax.ppermute(x, axis, [(i, target(i)) for i in range(count)])  21.3 us
    ppermute x4, waiting for transfers between devices, moved(): return lax.ppermute(x, axis, [(i, target(i)) for i in range(count)])  20.6 us
    all_to_all x1, waiting for transfers between devices, local(): lax.all_to_all(s1, 'x', 0, 0, tiled=True).reshape(X, ZH, ab_local, ij_local)  14.9 us
    dot_general x2, matrix products, product(): lax.dot_general(rows.reshape(X * ZH * ab_local, integrals.shape[1]), ampl...  6.05 us
    all_to_all x1, starting transfers between devices, local(): lax.all_to_all(s1, 'x', 0, 0, tiled=True).reshape(X, ZH, ab_local, ij_local)  4.02 us
  transfers between devices with their start and end apart: 5, of which 3 were waited for; matrix products, arithmetic and copies ran while one was open for 7% of the time, Pallas kernels for 0%

profile of v12, /device:TPU:105, one launch (start us, length us, event | category | flops | bytes accessed | tf_op | source)
XLA Modules:
  0.0 71.7 jit_solution(14845497723100452077)
XLA Ops:
  0.0 0.0 copy-start
  0.0 1.0 %copy-done = f32[256,512]{1,0:T(8,128)S(1)} copy-done((f32[256,512]{1,0:T(8,128)S(1)}, f32[256,512]{1,0:T(8,128)}, u32[]{:S(2)}) %copy-start) | copy-done | bytes 524312
  1.0 2.6 %fusion = f32[4,2,128,256]{3,2,1,0:T(8,128)S(1)} fusion(f32[4,2,2,128,512]{4,3,2,1,0:T(8,128)} %bitcast.24, s32[]{:T(128)S(6)} %select_n.55, f32[256,512]{1,0:T(8,128)S(1)} %copy-done), kind=kOutput, calls=%fused_computation.2 | convolution fusion | flops 805306368 | bytes 3670020 | tf_op jit(solution)/shard_map/dot_general | solution.py:27
  3.7 2.6 %collective-permute-start = (f32[4,2,128,256]{3,2,1,0:T(8,128)S(1)}, f32[4,2,128,256]{3,2,1,0:T(8,128)S(1)}, u32[]{:S(2)}, u32[]{:S(2)}) collective-permute-start(f32[4,2,128,256]{3,2,1,0:T(8,128)S(1)} %fusion), channel_id=1, source_target_pairs={{0,1},{1,0},{2,3},{3,2},{4,5},{5,4},{6,7},{7,6},{8,9},{9,8},{10,11... | collective-permute-start | bytes 3145736 | tf_op jit(solution)/shard_map/ppermute | solution.py:13
  6.3 0.0 copy-start.2
  6.3 0.0 copy-start.1
  6.3 3.4 %fusion.2 = f32[4,2,128,256]{3,2,1,0:T(8,128)S(1)} fusion(f32[4,2,2,128,512]{4,3,2,1,0:T(8,128)} %bitcast.25, s32[]{:T(128)S(6)} %select_n.54, f32[256,512]{1,0:T(8,128)S(1)} %copy-done), kind=kOutput, calls=%fused_computation.4 | convolution fusion | flops 1610612736 | bytes 3670020 | tf_op jit(solution)/shard_map/dot_general | solution.py:27
  9.7 0.0 collective-permute-done
  9.7 1.1 %add.67 = f32[4,2,128,256]{3,2,1,0:T(8,128)} add(f32[4,2,128,256]{3,2,1,0:T(8,128)S(1)} %fusion.2, f32[4,2,128,256]{3,2,1,0:T(8,128)S(1)} %collective-permute-done) | non-fusion elementwise | flops 262144 | bytes 3145728 | tf_op jit(solution)/shard_map/add | solution.py:36
  10.9 4.0 %all-to-all-start = ((f32[4,2,128,256]{3,2,1,0:T(8,128)}), f32[4,2,128,256]{3,2,1,0:T(8,128)S(1)}, u32[]{:S(2)}, u32[]{:S(2)}) async-start(f32[4,2,128,256]{3,2,1,0:T(8,128)} %add.67), calls=%async_computation | async-start | bytes 2097152 | tf_op jit(solution)/shard_map/all_to_all | solution.py:37
  14.9 14.9 %all-to-all-done = f32[4,2,128,256]{3,2,1,0:T(8,128)S(1)} async-done(((f32[4,2,128,256]{3,2,1,0:T(8,128)}), f32[4,2,128,256]{3,2,1,0:T(8,128)S(1)}, u32[]{:S(2)}, u32[]{:S(2)}) %all-to-all-start) | async-done | bytes 1048608 | tf_op jit(solution)/shard_map/all_to_all | solution.py:37
  29.8 0.1 reduce_sum.9
  29.9 8.8 %collective-permute-start.2 = (f32[128,256]{1,0:T(8,128)S(1)}, f32[128,256]{1,0:T(8,128)S(1)}, u32[]{:S(2)}, u32[]{:S(2)}) collective-permute-start(f32[128,256]{1,0:T(8,128)S(1)} %get-tuple-element.10), channel_id=1, source_target_pairs={{0,256},{16,272},{32,288},{48,304},{64,320},{80,336},{96,352},{112... | collective-permute-start | bytes 393224 | tf_op jit(solution)/shard_map/ppermute | solution.py:13
  38.7 6.1 %collective-permute-start.3 = (f32[128,256]{1,0:T(8,128)S(1)}, f32[128,256]{1,0:T(8,128)S(1)}, u32[]{:S(2)}, u32[]{:S(2)}) collective-permute-start(f32[128,256]{1,0:T(8,128)S(1)} %get-tuple-element.9), channel_id=1, source_target_pairs={{0,258},{1,259},{2,256},{3,257},{4,262},{5,263},{6,260},{7,261},{8... | collective-permute-start | bytes 393224 | tf_op jit(solution)/shard_map/ppermute | solution.py:13
  44.9 3.8 %collective-permute-start.1 = (f32[128,256]{1,0:T(8,128)S(1)}, f32[128,256]{1,0:T(8,128)S(1)}, u32[]{:S(2)}, u32[]{:S(2)}) collective-permute-start(f32[128,256]{1,0:T(8,128)S(1)} %get-tuple-element.9), channel_id=1, source_target_pairs={{0,2},{1,3},{2,0},{3,1},{4,6},{5,7},{6,4},{7,5},{8,10},{9,11},{10,... | collective-permute-start | bytes 393224 | tf_op jit(solution)/shard_map/ppermute | solution.py:13
  48.6 0.4 collective-permute-done.2
  49.1 20.1 %collective-permute-done.3 = f32[128,256]{1,0:T(8,128)S(1)} collective-permute-done((f32[128,256]{1,0:T(8,128)S(1)}, f32[128,256]{1,0:T(8,128)S(1)}, u32[]{:S(2)}, u32[]{:S(2)}) %collective-permute-start.3) | collective-permute-done | bytes 131104 | tf_op jit(solution)/shard_map/ppermute | solution.py:13
  69.2 0.8 %gather_fusion = f32[128,256]{1,0:T(8,128)S(1)} fusion(f32[128,256]{1,0:T(8,128)S(1)} %add.76, s32[1024]{0:T(1024)S(1)} %pad_clamp_fusion.1), kind=kCustom, calls=%fused_computation | custom fusion | bytes 262656 | tf_op jit(solution)/shard_map/jit(_take)/gather | solution.py:52
  70.0 0.1 broadcast_select_fusion
  70.1 0.1 copy.7
  70.2 0.7 %gather_fusion.1 = f32[256,128]{1,0:T(8,128)S(1)} fusion(f32[128,256]{0,1:T(8,128)S(1)} %copy.7, s32[1024]{0:T(1024)S(1)} %pad_clamp_fusion), kind=kCustom, calls=%fused_computation.1 | custom fusion | bytes 263168 | tf_op jit(solution)/shard_map/jit(_take)/gather | solution.py:52
  70.9 0.1 copy.8
  71.0 0.0 collective-permute-done.1
  71.0 0.7 bitcast_add_fusion
  (8 shorter events, 0.1 us)
Async XLA Ops:
  0.0 1.0 %copy-start = (f32[256,512]{1,0:T(8,128)S(1)}, f32[256,512]{1,0:T(8,128)}, u32[]{:S(2)}) copy-start(f32[256,512]{1,0:T(8,128)} %param.4) | copy-start | bytes 1572868
  3.7 6.1 %collective-permute-start = (f32[4,2,128,256]{3,2,1,0:T(8,128)S(1)}, f32[4,2,128,256]{3,2,1,0:T(8,128)S(1)}, u32[]{:S(2)}, u32[]{:S(2)}) collective-permute-start(f32[4,2,128,256]{3,2,1,0:T(8,128)S(1)} %fusion), channel_id=1, source_target_pairs={{0,1},{1,0},{2,3},{3,2},{4,5},{5,4},{6,7},{7,6},{8,9},{9,8},{10,11... | collective-permute-start | bytes 3145736 | tf_op jit(solution)/shard_map/ppermute | solution.py:13
  6.3 8.6 %copy-start.2 = (s32[128]{0:T(128)S(1)}, s32[128]{0:T(128)}, u32[]{:S(2)}) copy-start(s32[128]{0:T(128)} %param.7) | copy-start | bytes 1540
  6.3 8.6 %copy-start.1 = (s32[256]{0:T(256)S(1)}, s32[256]{0:T(256)}, u32[]{:S(2)}) copy-start(s32[256]{0:T(256)} %param.6) | copy-start | bytes 3076
  10.9 18.9 %all-to-all-start = ((f32[4,2,128,256]{3,2,1,0:T(8,128)}), f32[4,2,128,256]{3,2,1,0:T(8,128)S(1)}, u32[]{:S(2)}, u32[]{:S(2)}) async-start(f32[4,2,128,256]{3,2,1,0:T(8,128)} %add.67), calls=%async_computation | async-start | bytes 2097152 | tf_op jit(solution)/shard_map/all_to_all | solution.py:37
  29.9 19.2 %collective-permute-start.2 = (f32[128,256]{1,0:T(8,128)S(1)}, f32[128,256]{1,0:T(8,128)S(1)}, u32[]{:S(2)}, u32[]{:S(2)}) collective-permute-start(f32[128,256]{1,0:T(8,128)S(1)} %get-tuple-element.10), channel_id=1, source_target_pairs={{0,256},{16,272},{32,288},{48,304},{64,320},{80,336},{96,352},{112... | collective-permute-start | bytes 393224 | tf_op jit(solution)/shard_map/ppermute | solution.py:13
  38.7 30.5 %collective-permute-start.3 = (f32[128,256]{1,0:T(8,128)S(1)}, f32[128,256]{1,0:T(8,128)S(1)}, u32[]{:S(2)}, u32[]{:S(2)}) collective-permute-start(f32[128,256]{1,0:T(8,128)S(1)} %get-tuple-element.9), channel_id=1, source_target_pairs={{0,258},{1,259},{2,256},{3,257},{4,262},{5,263},{6,260},{7,261},{8... | collective-permute-start | bytes 393224 | tf_op jit(solution)/shard_map/ppermute | solution.py:13
  44.9 26.1 %collective-permute-start.1 = (f32[128,256]{1,0:T(8,128)S(1)}, f32[128,256]{1,0:T(8,128)S(1)}, u32[]{:S(2)}, u32[]{:S(2)}) collective-permute-start(f32[128,256]{1,0:T(8,128)S(1)} %get-tuple-element.9), channel_id=1, source_target_pairs={{0,2},{1,3},{2,0},{3,1},{4,6},{5,7},{6,4},{7,5},{8,10},{9,11},{10,... | collective-permute-start | bytes 393224 | tf_op jit(solution)/shard_map/ppermute | solution.py:13

commit v13 on v7

--- a/solution.py
+++ b/solution.py
@@ -38,7 +38,7 @@
     mine = lax.dynamic_index_in_dim(s2, zh, axis=0, keepdims=False)
     other = lax.dynamic_index_in_dim(s2, 1 - zh, axis=0, keepdims=False)
     half = pair_count // 2
-    from_zh = moved(other, LOOP, lambda i: i ^ 2)
+    from_zh = lax.dynamic_index_in_dim(lax.all_to_all(s2, "zh", 0, 0, tiled=True), 1 - zh, axis=0, keepdims=False)
     from_pair = moved(mine, PAIR, lambda i: (i + half) % pair_count)
     from_diag = moved(
         other,

time: 72.9 us -> 79.4 us (1.089)
  the two profiles are of different devices: /device:TPU:105 before, /device:TPU:8 now
where the time goes in v13:
time: 79.4 us; the launch traced here: 79 us
  starting transfers between devices  36.4 us (46%)
  waiting for transfers between devices  29.1 us (37%)
  matrix products  6.85 us (9%)
  local copies, waits for them, and re-layouts  3.71 us (5%)
  other arithmetic  2.76 us (3%)
    ppermute x3, starting transfers between devices, moved(): return lax.ppermute(x, axis, [(i, target(i)) for i in range(count)])  17 us
    all_to_all x1, waiting for transfers between devices, local(): lax.all_to_all(s1, 'x', 0, 0, tiled=True).reshape(X, ZH, ab_local, ij_local)  15.7 us
    all_to_all x1, starting transfers between devices, local(): lax.all_to_all(s2, 'zh', 0, 0, tiled=True)  15.1 us
    ppermute x3, waiting for transfers between devices, moved(): return lax.ppermute(x, axis, [(i, target(i)) for i in range(count)])  13.4 us
    dot_general x2, matrix products, product(): lax.dot_general(rows.reshape(X * ZH * ab_local, integrals.shape[1]), ampl...  6.85 us
    all_to_all x1, starting transfers between devices, local(): lax.all_to_all(s1, 'x', 0, 0, tiled=True).reshape(X, ZH, ab_local, ij_local)  4.29 us
  transfers between devices with their start and end apart: 5, of which 3 were waited for; matrix products, arithmetic and copies ran while one was open for 8% of the time, Pallas kernels for 0%

profile of v13, /device:TPU:8, one launch (start us, length us, event | category | flops | bytes accessed | tf_op | source)
XLA Modules:
  0.0 79.0 jit_solution(2911623677126461536)
XLA Ops:
  0.0 1.0 %copy-done = f32[256,512]{1,0:T(8,128)S(1)} copy-done((f32[256,512]{1,0:T(8,128)S(1)}, f32[256,512]{1,0:T(8,128)}, u32[]{:S(2)}) %copy-start) | copy-done | bytes 524312
  1.0 3.4 %fusion = f32[4,2,128,256]{3,2,1,0:T(8,128)S(1)} fusion(f32[4,2,2,128,512]{4,3,2,1,0:T(8,128)} %bitcast.28, s32[]{:T(128)S(6)} %select_n.56, f32[256,512]{1,0:T(8,128)S(1)} %copy-done), kind=kOutput, calls=%fused_computation.2 | convolution fusion | flops 1610612736 | bytes 3670020 | tf_op jit(solution)/shard_map/dot_general | solution.py:27
  4.5 1.9 %collective-permute-start = (f32[4,2,128,256]{3,2,1,0:T(8,128)S(1)}, f32[4,2,128,256]{3,2,1,0:T(8,128)S(1)}, u32[]{:S(2)}, u32[]{:S(2)}) collective-permute-start(f32[4,2,128,256]{3,2,1,0:T(8,128)S(1)} %fusion), channel_id=1, source_target_pairs={{0,1},{1,0},{2,3},{3,2},{4,5},{5,4},{6,7},{7,6},{8,9},{9,8},{10,11... | collective-permute-start | bytes 3145736 | tf_op jit(solution)/shard_map/ppermute | solution.py:13
  6.4 0.0 copy-start.2
  6.4 0.0 copy-start.1
  6.4 3.4 %fusion.2 = f32[4,2,128,256]{3,2,1,0:T(8,128)S(1)} fusion(f32[4,2,2,128,512]{4,3,2,1,0:T(8,128)} %bitcast.29, s32[]{:T(128)S(6)} %select_n.55, f32[256,512]{1,0:T(8,128)S(1)} %copy-done), kind=kOutput, calls=%fused_computation.4 | convolution fusion | flops 1610612736 | bytes 3670020 | tf_op jit(solution)/shard_map/dot_general | solution.py:27
  9.9 0.0 collective-permute-done
  9.9 1.1 %add.68 = f32[4,2,128,256]{3,2,1,0:T(8,128)} add(f32[4,2,128,256]{3,2,1,0:T(8,128)S(1)} %fusion.2, f32[4,2,128,256]{3,2,1,0:T(8,128)S(1)} %collective-permute-done) | non-fusion elementwise | flops 262144 | bytes 3145728 | tf_op jit(solution)/shard_map/add | solution.py:36
  11.0 4.3 %all-to-all-start = ((f32[4,2,128,256]{3,2,1,0:T(8,128)}), f32[4,2,128,256]{3,2,1,0:T(8,128)S(1)}, u32[]{:S(2)}, u32[]{:S(2)}) async-start(f32[4,2,128,256]{3,2,1,0:T(8,128)} %add.68), calls=%async_computation | async-start | bytes 2097152 | tf_op jit(solution)/shard_map/all_to_all | solution.py:37
  15.4 15.7 %all-to-all-done = f32[4,2,128,256]{3,2,1,0:T(8,128)S(1)} async-done(((f32[4,2,128,256]{3,2,1,0:T(8,128)}), f32[4,2,128,256]{3,2,1,0:T(8,128)S(1)}, u32[]{:S(2)}, u32[]{:S(2)}) %all-to-all-start) | async-done | bytes 1048608 | tf_op jit(solution)/shard_map/all_to_all | solution.py:37
  31.1 0.8 reduce_sum.9
  31.9 15.1 %all-to-all-start.1 = ((f32[2,128,256]{2,1,0:T(8,128)}), f32[2,128,256]{2,1,0:T(8,128)S(1)}, u32[]{:S(2)}, u32[]{:S(2)}) async-start(f32[2,128,256]{2,1,0:T(8,128)} %reduce_sum.9), calls=%async_computation.1 | async-start | bytes 524288 | tf_op jit(solution)/shard_map/all_to_all | solution.py:41
  46.9 1.0 %dynamic-slice_bitcast_fusion = (f32[128,256]{1,0:T(8,128)S(1)}, f32[128,256]{1,0:T(8,128)S(1)}) fusion(f32[2,128,256]{2,1,0:T(8,128)} %reduce_sum.9, s32[]{:T(128)S(6)} %select_n.60, s32[]{:T(128)S(6)} %select_n.59), kind=kLoop, calls=%fused_computation.12 | loop fusion | bytes 524296 | tf_op jit(solution)/shard_map/jit(dynamic_index_in_dim)/squeeze | solution.py:39
  47.9 4.3 %collective-permute-start.1 = (f32[128,256]{1,0:T(8,128)S(1)}, f32[128,256]{1,0:T(8,128)S(1)}, u32[]{:S(2)}, u32[]{:S(2)}) collective-permute-start(f32[128,256]{1,0:T(8,128)S(1)} %get-tuple-element.10), channel_id=1, source_target_pairs={{0,256},{16,272},{32,288},{48,304},{64,320},{80,336},{96,352},{112... | collective-permute-start | bytes 393224 | tf_op jit(solution)/shard_map/ppermute | solution.py:13
  52.2 10.8 %collective-permute-start.2 = (f32[128,256]{1,0:T(8,128)S(1)}, f32[128,256]{1,0:T(8,128)S(1)}, u32[]{:S(2)}, u32[]{:S(2)}) collective-permute-start(f32[128,256]{1,0:T(8,128)S(1)} %get-tuple-element.9), channel_id=1, source_target_pairs={{0,258},{1,259},{2,256},{3,257},{4,262},{5,263},{6,260},{7,261},{8... | collective-permute-start | bytes 393224 | tf_op jit(solution)/shard_map/ppermute | solution.py:13
  63.1 8.9 %collective-permute-done.1 = f32[128,256]{1,0:T(8,128)S(1)} collective-permute-done((f32[128,256]{1,0:T(8,128)S(1)}, f32[128,256]{1,0:T(8,128)S(1)}, u32[]{:S(2)}, u32[]{:S(2)}) %collective-permute-start.1) | collective-permute-done | bytes 131104 | tf_op jit(solution)/shard_map/ppermute | solution.py:13
  72.0 4.5 %collective-permute-done.2 = f32[128,256]{1,0:T(8,128)S(1)} collective-permute-done((f32[128,256]{1,0:T(8,128)S(1)}, f32[128,256]{1,0:T(8,128)S(1)}, u32[]{:S(2)}, u32[]{:S(2)}) %collective-permute-start.2) | collective-permute-done | bytes 131104 | tf_op jit(solution)/shard_map/ppermute | solution.py:13
  76.5 0.8 gather_fusion
  77.3 0.1 broadcast_select_fusion
  77.4 0.1 copy.7
  77.4 0.7 gather_fusion.1
  78.2 0.1 copy.8
  78.3 0.0 all-to-all-done.1
  78.3 0.7 bitcast_add_fusion
  (8 shorter events, 0.1 us)
Async XLA Ops:
  0.0 1.0 %copy-start = (f32[256,512]{1,0:T(8,128)S(1)}, f32[256,512]{1,0:T(8,128)}, u32[]{:S(2)}) copy-start(f32[256,512]{1,0:T(8,128)} %param.4) | copy-start | bytes 1572868
  4.5 5.4 %collective-permute-start = (f32[4,2,128,256]{3,2,1,0:T(8,128)S(1)}, f32[4,2,128,256]{3,2,1,0:T(8,128)S(1)}, u32[]{:S(2)}, u32[]{:S(2)}) collective-permute-start(f32[4,2,128,256]{3,2,1,0:T(8,128)S(1)} %fusion), channel_id=1, source_target_pairs={{0,1},{1,0},{2,3},{3,2},{4,5},{5,4},{6,7},{7,6},{8,9},{9,8},{10,11... | collective-permute-start | bytes 3145736 | tf_op jit(solution)/shard_map/ppermute | solution.py:13
  6.4 8.9 %copy-start.2 = (s32[128]{0:T(128)S(1)}, s32[128]{0:T(128)}, u32[]{:S(2)}) copy-start(s32[128]{0:T(128)} %param.7) | copy-start | bytes 1540
  6.4 8.9 %copy-start.1 = (s32[256]{0:T(256)S(1)}, s32[256]{0:T(256)}, u32[]{:S(2)}) copy-start(s32[256]{0:T(256)} %param.6) | copy-start | bytes 3076
  11.0 20.0 %all-to-all-start = ((f32[4,2,128,256]{3,2,1,0:T(8,128)}), f32[4,2,128,256]{3,2,1,0:T(8,128)S(1)}, u32[]{:S(2)}, u32[]{:S(2)}) async-start(f32[4,2,128,256]{3,2,1,0:T(8,128)} %add.68), calls=%async_computation | async-start | bytes 2097152 | tf_op jit(solution)/shard_map/all_to_all | solution.py:37
  31.9 46.4 %all-to-all-start.1 = ((f32[2,128,256]{2,1,0:T(8,128)}), f32[2,128,256]{2,1,0:T(8,128)S(1)}, u32[]{:S(2)}, u32[]{:S(2)}) async-start(f32[2,128,256]{2,1,0:T(8,128)} %reduce_sum.9), calls=%async_computation.1 | async-start | bytes 524288 | tf_op jit(solution)/shard_map/all_to_all | solution.py:41
  47.9 24.1 %collective-permute-start.1 = (f32[128,256]{1,0:T(8,128)S(1)}, f32[128,256]{1,0:T(8,128)S(1)}, u32[]{:S(2)}, u32[]{:S(2)}) collective-permute-start(f32[128,256]{1,0:T(8,128)S(1)} %get-tuple-element.10), channel_id=1, source_target_pairs={{0,256},{16,272},{32,288},{48,304},{64,320},{80,336},{96,352},{112... | collective-permute-start | bytes 393224 | tf_op jit(solution)/shard_map/ppermute | solution.py:13
  52.2 24.2 %collective-permute-start.2 = (f32[128,256]{1,0:T(8,128)S(1)}, f32[128,256]{1,0:T(8,128)S(1)}, u32[]{:S(2)}, u32[]{:S(2)}) collective-permute-start(f32[128,256]{1,0:T(8,128)S(1)} %get-tuple-element.9), channel_id=1, source_target_pairs={{0,258},{1,259},{2,256},{3,257},{4,262},{5,263},{6,260},{7,261},{8... | collective-permute-start | bytes 393224 | tf_op jit(solution)/shard_map/ppermute | solution.py:13

commit v14 on v7

--- a/solution.py
+++ b/solution.py
@@ -34,7 +34,10 @@
 
     give = moved(product(1 - c), LOOP, lambda i: i ^ 1)
     s1 = lax.optimization_barrier(product(c)) + give
-    s2 = lax.all_to_all(s1, "x", 0, 0, tiled=True).reshape(X, ZH, ab_local, ij_local).sum(axis=0)
+    s2 = lax.dynamic_index_in_dim(s1, x, axis=0, keepdims=False)
+    for shift in (2, 1, 3):
+        out = lax.dynamic_index_in_dim(s1, (x + shift) % X, axis=0, keepdims=False)
+        s2 = s2 + moved(out, LOOP, lambda i, s=shift: (((i // 4) + s) % X) * 4 + i % 4)
     mine = lax.dynamic_index_in_dim(s2, zh, axis=0, keepdims=False)
     other = lax.dynamic_index_in_dim(s2, 1 - zh, axis=0, keepdims=False)
     half = pair_count // 2

time: 72.9 us -> 71.7 us (0.984)
  the two profiles are of different devices: /device:TPU:105 before, /device:TPU:109 now
where the time goes in v14:
time: 71.7 us; the launch traced here: 71.3 us
  waiting for transfers between devices  29.9 us (42%)
  starting transfers between devices  29.1 us (41%)
  matrix products  6.85 us (10%)
  local copies, waits for them, and re-layouts  2.83 us (4%)
  other arithmetic  2.25 us (3%)
    ppermute x7, waiting for transfers between devices, moved(): return lax.ppermute(x, axis, [(i, target(i)) for i in range(count)])  29.9 us
    ppermute x7, starting transfers between devices, moved(): return lax.ppermute(x, axis, [(i, target(i)) for i in range(count)])  29.1 us
    dot_general x2, matrix products, product(): lax.dot_general(rows.reshape(X * ZH * ab_local, integrals.shape[1]), ampl...  6.85 us
  transfers between devices with their start and end apart: 7, of which 4 were waited for; matrix products, arithmetic and copies ran while one was open for 7% of the time, Pallas kernels for 0%

profile of v14, /device:TPU:109, one launch (start us, length us, event | category | flops | bytes accessed | tf_op | source)
XLA Modules:
  0.0 71.3 jit_solution(10348852841063105036)
XLA Ops:
  0.0 1.0 %copy-done = f32[256,512]{1,0:T(8,128)S(1)} copy-done((f32[256,512]{1,0:T(8,128)S(1)}, f32[256,512]{1,0:T(8,128)}, u32[]{:S(2)}) %copy-start) | copy-done | bytes 524312
  1.0 3.4 %fusion = f32[4,2,128,256]{3,2,1,0:T(8,128)S(1)} fusion(f32[4,2,2,128,512]{4,3,2,1,0:T(8,128)} %bitcast.36, s32[]{:T(128)S(6)} %select_n.83, f32[256,512]{1,0:T(8,128)S(1)} %copy-done), kind=kOutput, calls=%fused_computation.2 | convolution fusion | flops 1610612736 | bytes 3670020 | tf_op jit(solution)/shard_map/dot_general | solution.py:27
  4.5 2.6 %collective-permute-start = (f32[4,2,128,256]{3,2,1,0:T(8,128)S(1)}, f32[4,2,128,256]{3,2,1,0:T(8,128)}, u32[]{:S(2)}, u32[]{:S(2)}) collective-permute-start(f32[4,2,128,256]{3,2,1,0:T(8,128)S(1)} %fusion), channel_id=1, source_target_pairs={{0,1},{1,0},{2,3},{3,2},{4,5},{5,4},{6,7},{7,6},{8,9},{9,8},{10,11... | collective-permute-start | bytes 3145736 | tf_op jit(solution)/shard_map/ppermute | solution.py:13
  7.1 0.0 copy-start.2
  7.2 3.4 %fusion.2 = f32[4,2,128,256]{3,2,1,0:T(8,128)S(1)} fusion(f32[4,2,2,128,512]{4,3,2,1,0:T(8,128)} %bitcast.37, s32[]{:T(128)S(6)} %select_n.82, f32[256,512]{1,0:T(8,128)S(1)} %copy-done), kind=kOutput, calls=%fused_computation.4 | convolution fusion | flops 1610612736 | bytes 3670020 | tf_op jit(solution)/shard_map/dot_general | solution.py:27
  10.6 1.4 %add.108 = f32[4,2,128,256]{3,2,1,0:T(8,128)S(1)} add(f32[4,2,128,256]{3,2,1,0:T(8,128)S(1)} %fusion.2, f32[4,2,128,256]{3,2,1,0:T(8,128)} %collective-permute-done) | non-fusion elementwise | flops 262144 | bytes 3145728 | tf_op jit(solution)/shard_map/add | solution.py:36
  12.0 0.1 dynamic-slice_bitcast_fusion.2
  12.1 2.1 %collective-permute-start.1 = (f32[2,128,256]{2,1,0:T(8,128)S(1)}, f32[2,128,256]{2,1,0:T(8,128)S(1)}, u32[]{:S(2)}, u32[]{:S(2)}) collective-permute-start(f32[2,128,256]{2,1,0:T(8,128)S(1)} %get-tuple-element.9), channel_id=1, source_target_pairs={{0,8},{1,9},{2,10},{3,11},{4,12},{5,13},{6,14},{7,15},{8,0},{9,1},... | collective-permute-start | bytes 786440 | tf_op jit(solution)/shard_map/ppermute | solution.py:13
  14.2 3.7 %collective-permute-start.2 = (f32[2,128,256]{2,1,0:T(8,128)S(1)}, f32[2,128,256]{2,1,0:T(8,128)S(1)}, u32[]{:S(2)}, u32[]{:S(2)}) collective-permute-start(f32[2,128,256]{2,1,0:T(8,128)S(1)} %get-tuple-element.11), channel_id=1, source_target_pairs={{0,4},{1,5},{2,6},{3,7},{4,8},{5,9},{6,10},{7,11},{8,12},{9,13},{1... | collective-permute-start | bytes 786440 | tf_op jit(solution)/shard_map/ppermute | solution.py:13
  18.0 2.0 %collective-permute-start.3 = (f32[2,128,256]{2,1,0:T(8,128)S(1)}, f32[2,128,256]{2,1,0:T(8,128)S(1)}, u32[]{:S(2)}, u32[]{:S(2)}) collective-permute-start(f32[2,128,256]{2,1,0:T(8,128)S(1)} %get-tuple-element.10), channel_id=1, source_target_pairs={{0,12},{1,13},{2,14},{3,15},{4,0},{5,1},{6,2},{7,3},{8,4},{9,5},{1... | collective-permute-start | bytes 786440 | tf_op jit(solution)/shard_map/ppermute | solution.py:13
  20.0 3.3 %collective-permute-done.1 = f32[2,128,256]{2,1,0:T(8,128)S(1)} collective-permute-done((f32[2,128,256]{2,1,0:T(8,128)S(1)}, f32[2,128,256]{2,1,0:T(8,128)S(1)}, u32[]{:S(2)}, u32[]{:S(2)}) %collective-permute-start.1) | collective-permute-done | bytes 262176 | tf_op jit(solution)/shard_map/ppermute | solution.py:13
  23.4 6.0 %collective-permute-done.2 = f32[2,128,256]{2,1,0:T(8,128)S(1)} collective-permute-done((f32[2,128,256]{2,1,0:T(8,128)S(1)}, f32[2,128,256]{2,1,0:T(8,128)S(1)}, u32[]{:S(2)}, u32[]{:S(2)}) %collective-permute-start.2) | collective-permute-done | bytes 262176 | tf_op jit(solution)/shard_map/ppermute | solution.py:13
  29.4 0.1 fusion.9
  29.5 8.8 %collective-permute-start.5 = (f32[128,256]{1,0:T(8,128)S(1)}, f32[128,256]{1,0:T(8,128)S(1)}, u32[]{:S(2)}, u32[]{:S(2)}) collective-permute-start(f32[128,256]{1,0:T(8,128)S(1)} %get-tuple-element.13), channel_id=1, source_target_pairs={{0,256},{16,272},{32,288},{48,304},{64,320},{80,336},{96,352},{112... | collective-permute-start | bytes 393224 | tf_op jit(solution)/shard_map/ppermute | solution.py:13
  38.3 6.1 %collective-permute-start.6 = (f32[128,256]{1,0:T(8,128)S(1)}, f32[128,256]{1,0:T(8,128)S(1)}, u32[]{:S(2)}, u32[]{:S(2)}) collective-permute-start(f32[128,256]{1,0:T(8,128)S(1)} %get-tuple-element.12), channel_id=1, source_target_pairs={{0,258},{1,259},{2,256},{3,257},{4,262},{5,263},{6,260},{7,261},{8... | collective-permute-start | bytes 393224 | tf_op jit(solution)/shard_map/ppermute | solution.py:13
  44.5 3.7 %collective-permute-start.4 = (f32[128,256]{1,0:T(8,128)S(1)}, f32[128,256]{1,0:T(8,128)S(1)}, u32[]{:S(2)}, u32[]{:S(2)}) collective-permute-start(f32[128,256]{1,0:T(8,128)S(1)} %get-tuple-element.12), channel_id=1, source_target_pairs={{0,2},{1,3},{2,0},{3,1},{4,6},{5,7},{6,4},{7,5},{8,10},{9,11},{10,... | collective-permute-start | bytes 393224 | tf_op jit(solution)/shard_map/ppermute | solution.py:13
  48.2 0.5 collective-permute-done.5
  48.7 20.1 %collective-permute-done.6 = f32[128,256]{1,0:T(8,128)S(1)} collective-permute-done((f32[128,256]{1,0:T(8,128)S(1)}, f32[128,256]{1,0:T(8,128)S(1)}, u32[]{:S(2)}, u32[]{:S(2)}) %collective-permute-start.6) | collective-permute-done | bytes 131104 | tf_op jit(solution)/shard_map/ppermute | solution.py:13
  68.8 0.8 %gather_fusion = f32[128,256]{1,0:T(8,128)S(1)} fusion(f32[128,256]{1,0:T(8,128)S(1)} %add.130, s32[1024]{0:T(1024)S(1)} %pad_clamp_fusion.1), kind=kCustom, calls=%fused_computation | custom fusion | bytes 262656 | tf_op jit(solution)/shard_map/jit(_take)/gather | solution.py:55
  69.6 0.1 broadcast_select_fusion
  69.7 0.1 copy.7
  69.7 0.7 %gather_fusion.1 = f32[256,128]{1,0:T(8,128)S(1)} fusion(f32[128,256]{0,1:T(8,128)S(1)} %copy.7, s32[1024]{0:T(1024)S(1)} %pad_clamp_fusion), kind=kCustom, calls=%fused_computation.1 | custom fusion | bytes 263168 | tf_op jit(solution)/shard_map/jit(_take)/gather | solution.py:55
  70.5 0.1 copy.8
  70.6 0.7 bitcast_add_fusion.1
  (13 shorter events, 0.1 us)
Async XLA Ops:
  0.0 1.0 %copy-start = (f32[256,512]{1,0:T(8,128)S(1)}, f32[256,512]{1,0:T(8,128)}, u32[]{:S(2)}) copy-start(f32[256,512]{1,0:T(8,128)} %param.4) | copy-start | bytes 1572868
  4.5 6.2 %collective-permute-start = (f32[4,2,128,256]{3,2,1,0:T(8,128)S(1)}, f32[4,2,128,256]{3,2,1,0:T(8,128)}, u32[]{:S(2)}, u32[]{:S(2)}) collective-permute-start(f32[4,2,128,256]{3,2,1,0:T(8,128)S(1)} %fusion), channel_id=1, source_target_pairs={{0,1},{1,0},{2,3},{3,2},{4,5},{5,4},{6,7},{7,6},{8,9},{9,8},{10,11... | collective-permute-start | bytes 3145736 | tf_op jit(solution)/shard_map/ppermute | solution.py:13
  7.1 12.8 %copy-start.2 = (s32[128]{0:T(128)S(1)}, s32[128]{0:T(128)}, u32[]{:S(2)}) copy-start(s32[128]{0:T(128)} %param.7) | copy-start | bytes 1540
  7.2 12.9 %copy-start.1 = (s32[256]{0:T(256)S(1)}, s32[256]{0:T(256)}, u32[]{:S(2)}) copy-start(s32[256]{0:T(256)} %param.6) | copy-start | bytes 3076
  12.1 11.3 %collective-permute-start.1 = (f32[2,128,256]{2,1,0:T(8,128)S(1)}, f32[2,128,256]{2,1,0:T(8,128)S(1)}, u32[]{:S(2)}, u32[]{:S(2)}) collective-permute-start(f32[2,128,256]{2,1,0:T(8,128)S(1)} %get-tuple-element.9), channel_id=1, source_target_pairs={{0,8},{1,9},{2,10},{3,11},{4,12},{5,13},{6,14},{7,15},{8,0},{9,1},... | collective-permute-start | bytes 786440 | tf_op jit(solution)/shard_map/ppermute | solution.py:13
  14.2 15.2 %collective-permute-start.2 = (f32[2,128,256]{2,1,0:T(8,128)S(1)}, f32[2,128,256]{2,1,0:T(8,128)S(1)}, u32[]{:S(2)}, u32[]{:S(2)}) collective-permute-start(f32[2,128,256]{2,1,0:T(8,128)S(1)} %get-tuple-element.11), channel_id=1, source_target_pairs={{0,4},{1,5},{2,6},{3,7},{4,8},{5,9},{6,10},{7,11},{8,12},{9,13},{1... | collective-permute-start | bytes 786440 | tf_op jit(solution)/shard_map/ppermute | solution.py:13
  18.0 11.4 %collective-permute-start.3 = (f32[2,128,256]{2,1,0:T(8,128)S(1)}, f32[2,128,256]{2,1,0:T(8,128)S(1)}, u32[]{:S(2)}, u32[]{:S(2)}) collective-permute-start(f32[2,128,256]{2,1,0:T(8,128)S(1)} %get-tuple-element.10), channel_id=1, source_target_pairs={{0,12},{1,13},{2,14},{3,15},{4,0},{5,1},{6,2},{7,3},{8,4},{9,5},{1... | collective-permute-start | bytes 786440 | tf_op jit(solution)/shard_map/ppermute | solution.py:13
  29.5 19.2 %collective-permute-start.5 = (f32[128,256]{1,0:T(8,128)S(1)}, f32[128,256]{1,0:T(8,128)S(1)}, u32[]{:S(2)}, u32[]{:S(2)}) collective-permute-start(f32[128,256]{1,0:T(8,128)S(1)} %get-tuple-element.13), channel_id=1, source_target_pairs={{0,256},{16,272},{32,288},{48,304},{64,320},{80,336},{96,352},{112... | collective-permute-start | bytes 393224 | tf_op jit(solution)/shard_map/ppermute | solution.py:13
  38.3 30.5 %collective-permute-start.6 = (f32[128,256]{1,0:T(8,128)S(1)}, f32[128,256]{1,0:T(8,128)S(1)}, u32[]{:S(2)}, u32[]{:S(2)}) collective-permute-start(f32[128,256]{1,0:T(8,128)S(1)} %get-tuple-element.12), channel_id=1, source_target_pairs={{0,258},{1,259},{2,256},{3,257},{4,262},{5,263},{6,260},{7,261},{8... | collective-permute-start | bytes 393224 | tf_op jit(solution)/shard_map/ppermute | solution.py:13
  44.5 26.1 %collective-permute-start.4 = (f32[128,256]{1,0:T(8,128)S(1)}, f32[128,256]{1,0:T(8,128)S(1)}, u32[]{:S(2)}, u32[]{:S(2)}) collective-permute-start(f32[128,256]{1,0:T(8,128)S(1)} %get-tuple-element.12), channel_id=1, source_target_pairs={{0,2},{1,3},{2,0},{3,1},{4,6},{5,7},{6,4},{7,5},{8,10},{9,11},{10,... | collective-permute-start | bytes 393224 | tf_op jit(solution)/shard_map/ppermute | solution.py:13

commit v15 on v14

--- a/solution.py
+++ b/solution.py
@@ -35,7 +35,7 @@
     give = moved(product(1 - c), LOOP, lambda i: i ^ 1)
     s1 = lax.optimization_barrier(product(c)) + give
     s2 = lax.dynamic_index_in_dim(s1, x, axis=0, keepdims=False)
-    for shift in (2, 1, 3):
+    for shift in (2, 3, 1):
         out = lax.dynamic_index_in_dim(s1, (x + shift) % X, axis=0, keepdims=False)
         s2 = s2 + moved(out, LOOP, lambda i, s=shift: (((i // 4) + s) % X) * 4 + i % 4)
     mine = lax.dynamic_index_in_dim(s2, zh, axis=0, keepdims=False)

time: 71.7 us -> 72.2 us (level)
  the two profiles are of different devices: /device:TPU:109 before, /device:TPU:97 now
where the time goes in v15:
time: 72.2 us; the launch traced here: 71.8 us
  starting transfers between devices  31.2 us (43%)
  waiting for transfers between devices  28.3 us (39%)
  matrix products  6.85 us (9%)
  local copies, waits for them, and re-layouts  2.83 us (4%)
  other arithmetic  2.25 us (3%)
    ppermute x7, starting transfers between devices, moved(): return lax.ppermute(x, axis, [(i, target(i)) for i in range(count)])  31.2 us
    ppermute x7, waiting for transfers between devices, moved(): return lax.ppermute(x, axis, [(i, target(i)) for i in range(count)])  28.3 us
    dot_general x2, matrix products, product(): lax.dot_general(rows.reshape(X * ZH * ab_local, integrals.shape[1]), ampl...  6.85 us
  transfers between devices with their start and end apart: 7, of which 5 were waited for; matrix products, arithmetic and copies ran while one was open for 7% of the time, Pallas kernels for 0%

profile of v15, /device:TPU:97, one launch (start us, length us, event | category | flops | bytes accessed | tf_op | source)
XLA Modules:
  0.0 71.8 jit_solution(3890395705059167292)
XLA Ops:
  0.0 1.0 %copy-done = f32[256,512]{1,0:T(8,128)S(1)} copy-done((f32[256,512]{1,0:T(8,128)S(1)}, f32[256,512]{1,0:T(8,128)}, u32[]{:S(2)}) %copy-start) | copy-done | bytes 524312
  1.0 3.4 %fusion = f32[4,2,128,256]{3,2,1,0:T(8,128)S(1)} fusion(f32[4,2,2,128,512]{4,3,2,1,0:T(8,128)} %bitcast.36, s32[]{:T(128)S(6)} %select_n.83, f32[256,512]{1,0:T(8,128)S(1)} %copy-done), kind=kOutput, calls=%fused_computation.2 | convolution fusion | flops 1610612736 | bytes 3670020 | tf_op jit(solution)/shard_map/dot_general | solution.py:27
  4.5 2.6 %collective-permute-start = (f32[4,2,128,256]{3,2,1,0:T(8,128)S(1)}, f32[4,2,128,256]{3,2,1,0:T(8,128)}, u32[]{:S(2)}, u32[]{:S(2)}) collective-permute-start(f32[4,2,128,256]{3,2,1,0:T(8,128)S(1)} %fusion), channel_id=1, source_target_pairs={{0,1},{1,0},{2,3},{3,2},{4,5},{5,4},{6,7},{7,6},{8,9},{9,8},{10,11... | collective-permute-start | bytes 3145736 | tf_op jit(solution)/shard_map/ppermute | solution.py:13
  7.2 3.4 %fusion.2 = f32[4,2,128,256]{3,2,1,0:T(8,128)S(1)} fusion(f32[4,2,2,128,512]{4,3,2,1,0:T(8,128)} %bitcast.37, s32[]{:T(128)S(6)} %select_n.82, f32[256,512]{1,0:T(8,128)S(1)} %copy-done), kind=kOutput, calls=%fused_computation.4 | convolution fusion | flops 1610612736 | bytes 3670020 | tf_op jit(solution)/shard_map/dot_general | solution.py:27
  10.6 1.4 %add.108 = f32[4,2,128,256]{3,2,1,0:T(8,128)S(1)} add(f32[4,2,128,256]{3,2,1,0:T(8,128)S(1)} %fusion.2, f32[4,2,128,256]{3,2,1,0:T(8,128)} %collective-permute-done) | non-fusion elementwise | flops 262144 | bytes 3145728 | tf_op jit(solution)/shard_map/add | solution.py:36
  12.0 0.1 dynamic-slice_bitcast_fusion.2
  12.1 4.6 %collective-permute-start.1 = (f32[2,128,256]{2,1,0:T(8,128)S(1)}, f32[2,128,256]{2,1,0:T(8,128)S(1)}, u32[]{:S(2)}, u32[]{:S(2)}) collective-permute-start(f32[2,128,256]{2,1,0:T(8,128)S(1)} %get-tuple-element.9), channel_id=1, source_target_pairs={{0,8},{1,9},{2,10},{3,11},{4,12},{5,13},{6,14},{7,15},{8,0},{9,1},... | collective-permute-start | bytes 786440 | tf_op jit(solution)/shard_map/ppermute | solution.py:13
  16.7 2.8 %collective-permute-start.2 = (f32[2,128,256]{2,1,0:T(8,128)S(1)}, f32[2,128,256]{2,1,0:T(8,128)S(1)}, u32[]{:S(2)}, u32[]{:S(2)}) collective-permute-start(f32[2,128,256]{2,1,0:T(8,128)S(1)} %get-tuple-element.11), channel_id=1, source_target_pairs={{0,12},{1,13},{2,14},{3,15},{4,0},{5,1},{6,2},{7,3},{8,4},{9,5},{1... | collective-permute-start | bytes 786440 | tf_op jit(solution)/shard_map/ppermute | solution.py:13
  19.5 2.5 %collective-permute-start.3 = (f32[2,128,256]{2,1,0:T(8,128)S(1)}, f32[2,128,256]{2,1,0:T(8,128)S(1)}, u32[]{:S(2)}, u32[]{:S(2)}) collective-permute-start(f32[2,128,256]{2,1,0:T(8,128)S(1)} %get-tuple-element.10), channel_id=1, source_target_pairs={{0,4},{1,5},{2,6},{3,7},{4,8},{5,9},{6,10},{7,11},{8,12},{9,13},{1... | collective-permute-start | bytes 786440 | tf_op jit(solution)/shard_map/ppermute | solution.py:13
  22.1 1.2 %collective-permute-done.1 = f32[2,128,256]{2,1,0:T(8,128)S(1)} collective-permute-done((f32[2,128,256]{2,1,0:T(8,128)S(1)}, f32[2,128,256]{2,1,0:T(8,128)S(1)}, u32[]{:S(2)}, u32[]{:S(2)}) %collective-permute-start.1) | collective-permute-done | bytes 262176 | tf_op jit(solution)/shard_map/ppermute | solution.py:13
  23.3 5.8 %collective-permute-done.2 = f32[2,128,256]{2,1,0:T(8,128)S(1)} collective-permute-done((f32[2,128,256]{2,1,0:T(8,128)S(1)}, f32[2,128,256]{2,1,0:T(8,128)S(1)}, u32[]{:S(2)}, u32[]{:S(2)}) %collective-permute-start.2) | collective-permute-done | bytes 262176 | tf_op jit(solution)/shard_map/ppermute | solution.py:13
  29.1 0.8 %collective-permute-done.3 = f32[2,128,256]{2,1,0:T(8,128)S(1)} collective-permute-done((f32[2,128,256]{2,1,0:T(8,128)S(1)}, f32[2,128,256]{2,1,0:T(8,128)S(1)}, u32[]{:S(2)}, u32[]{:S(2)}) %collective-permute-start.3) | collective-permute-done | bytes 262176 | tf_op jit(solution)/shard_map/ppermute | solution.py:13
  29.9 0.1 fusion.9
  30.0 8.8 %collective-permute-start.5 = (f32[128,256]{1,0:T(8,128)S(1)}, f32[128,256]{1,0:T(8,128)S(1)}, u32[]{:S(2)}, u32[]{:S(2)}) collective-permute-start(f32[128,256]{1,0:T(8,128)S(1)} %get-tuple-element.13), channel_id=1, source_target_pairs={{0,256},{16,272},{32,288},{48,304},{64,320},{80,336},{96,352},{112... | collective-permute-start | bytes 393224 | tf_op jit(solution)/shard_map/ppermute | solution.py:13
  38.8 6.1 %collective-permute-start.6 = (f32[128,256]{1,0:T(8,128)S(1)}, f32[128,256]{1,0:T(8,128)S(1)}, u32[]{:S(2)}, u32[]{:S(2)}) collective-permute-start(f32[128,256]{1,0:T(8,128)S(1)} %get-tuple-element.12), channel_id=1, source_target_pairs={{0,258},{1,259},{2,256},{3,257},{4,262},{5,263},{6,260},{7,261},{8... | collective-permute-start | bytes 393224 | tf_op jit(solution)/shard_map/ppermute | solution.py:13
  45.0 3.7 %collective-permute-start.4 = (f32[128,256]{1,0:T(8,128)S(1)}, f32[128,256]{1,0:T(8,128)S(1)}, u32[]{:S(2)}, u32[]{:S(2)}) collective-permute-start(f32[128,256]{1,0:T(8,128)S(1)} %get-tuple-element.12), channel_id=1, source_target_pairs={{0,2},{1,3},{2,0},{3,1},{4,6},{5,7},{6,4},{7,5},{8,10},{9,11},{10,... | collective-permute-start | bytes 393224 | tf_op jit(solution)/shard_map/ppermute | solution.py:13
  48.7 0.4 collective-permute-done.5
  49.2 20.1 %collective-permute-done.6 = f32[128,256]{1,0:T(8,128)S(1)} collective-permute-done((f32[128,256]{1,0:T(8,128)S(1)}, f32[128,256]{1,0:T(8,128)S(1)}, u32[]{:S(2)}, u32[]{:S(2)}) %collective-permute-start.6) | collective-permute-done | bytes 131104 | tf_op jit(solution)/shard_map/ppermute | solution.py:13
  69.3 0.8 %gather_fusion = f32[128,256]{1,0:T(8,128)S(1)} fusion(f32[128,256]{1,0:T(8,128)S(1)} %add.130, s32[1024]{0:T(1024)S(1)} %pad_clamp_fusion.1), kind=kCustom, calls=%fused_computation | custom fusion | bytes 262656 | tf_op jit(solution)/shard_map/jit(_take)/gather | solution.py:55
  70.1 0.1 broadcast_select_fusion
  70.2 0.1 copy.7
  70.3 0.7 %gather_fusion.1 = f32[256,128]{1,0:T(8,128)S(1)} fusion(f32[128,256]{0,1:T(8,128)S(1)} %copy.7, s32[1024]{0:T(1024)S(1)} %pad_clamp_fusion), kind=kCustom, calls=%fused_computation.1 | custom fusion | bytes 263168 | tf_op jit(solution)/shard_map/jit(_take)/gather | solution.py:55
  71.0 0.1 copy.8
  71.1 0.7 bitcast_add_fusion.1
  (13 shorter events, 0.1 us)
Async XLA Ops:
  0.0 1.0 %copy-start = (f32[256,512]{1,0:T(8,128)S(1)}, f32[256,512]{1,0:T(8,128)}, u32[]{:S(2)}) copy-start(f32[256,512]{1,0:T(8,128)} %param.4) | copy-start | bytes 1572868
  4.5 6.2 %collective-permute-start = (f32[4,2,128,256]{3,2,1,0:T(8,128)S(1)}, f32[4,2,128,256]{3,2,1,0:T(8,128)}, u32[]{:S(2)}, u32[]{:S(2)}) collective-permute-start(f32[4,2,128,256]{3,2,1,0:T(8,128)S(1)} %fusion), channel_id=1, source_target_pairs={{0,1},{1,0},{2,3},{3,2},{4,5},{5,4},{6,7},{7,6},{8,9},{9,8},{10,11... | collective-permute-start | bytes 3145736 | tf_op jit(solution)/shard_map/ppermute | solution.py:13
  7.1 14.9 %copy-start.2 = (s32[128]{0:T(128)S(1)}, s32[128]{0:T(128)}, u32[]{:S(2)}) copy-start(s32[128]{0:T(128)} %param.7) | copy-start | bytes 1540
  7.2 15.0 %copy-start.1 = (s32[256]{0:T(256)S(1)}, s32[256]{0:T(256)}, u32[]{:S(2)}) copy-start(s32[256]{0:T(256)} %param.6) | copy-start | bytes 3076
  12.1 11.2 %collective-permute-start.1 = (f32[2,128,256]{2,1,0:T(8,128)S(1)}, f32[2,128,256]{2,1,0:T(8,128)S(1)}, u32[]{:S(2)}, u32[]{:S(2)}) collective-permute-start(f32[2,128,256]{2,1,0:T(8,128)S(1)} %get-tuple-element.9), channel_id=1, source_target_pairs={{0,8},{1,9},{2,10},{3,11},{4,12},{5,13},{6,14},{7,15},{8,0},{9,1},... | collective-permute-start | bytes 786440 | tf_op jit(solution)/shard_map/ppermute | solution.py:13
  16.7 12.3 %collective-permute-start.2 = (f32[2,128,256]{2,1,0:T(8,128)S(1)}, f32[2,128,256]{2,1,0:T(8,128)S(1)}, u32[]{:S(2)}, u32[]{:S(2)}) collective-permute-start(f32[2,128,256]{2,1,0:T(8,128)S(1)} %get-tuple-element.11), channel_id=1, source_target_pairs={{0,12},{1,13},{2,14},{3,15},{4,0},{5,1},{6,2},{7,3},{8,4},{9,5},{1... | collective-permute-start | bytes 786440 | tf_op jit(solution)/shard_map/ppermute | solution.py:13
  19.5 10.4 %collective-permute-start.3 = (f32[2,128,256]{2,1,0:T(8,128)S(1)}, f32[2,128,256]{2,1,0:T(8,128)S(1)}, u32[]{:S(2)}, u32[]{:S(2)}) collective-permute-start(f32[2,128,256]{2,1,0:T(8,128)S(1)} %get-tuple-element.10), channel_id=1, source_target_pairs={{0,4},{1,5},{2,6},{3,7},{4,8},{5,9},{6,10},{7,11},{8,12},{9,13},{1... | collective-permute-start | bytes 786440 | tf_op jit(solution)/shard_map/ppermute | solution.py:13
  30.0 19.2 %collective-permute-start.5 = (f32[128,256]{1,0:T(8,128)S(1)}, f32[128,256]{1,0:T(8,128)S(1)}, u32[]{:S(2)}, u32[]{:S(2)}) collective-permute-start(f32[128,256]{1,0:T(8,128)S(1)} %get-tuple-element.13), channel_id=1, source_target_pairs={{0,256},{16,272},{32,288},{48,304},{64,320},{80,336},{96,352},{112... | collective-permute-start | bytes 393224 | tf_op jit(solution)/shard_map/ppermute | solution.py:13
  38.8 30.5 %collective-permute-start.6 = (f32[128,256]{1,0:T(8,128)S(1)}, f32[128,256]{1,0:T(8,128)S(1)}, u32[]{:S(2)}, u32[]{:S(2)}) collective-permute-start(f32[128,256]{1,0:T(8,128)S(1)} %get-tuple-element.12), channel_id=1, source_target_pairs={{0,258},{1,259},{2,256},{3,257},{4,262},{5,263},{6,260},{7,261},{8... | collective-permute-start | bytes 393224 | tf_op jit(solution)/shard_map/ppermute | solution.py:13
  45.0 26.1 %collective-permute-start.4 = (f32[128,256]{1,0:T(8,128)S(1)}, f32[128,256]{1,0:T(8,128)S(1)}, u32[]{:S(2)}, u32[]{:S(2)}) collective-permute-start(f32[128,256]{1,0:T(8,128)S(1)} %get-tuple-element.12), channel_id=1, source_target_pairs={{0,2},{1,3},{2,0},{3,1},{4,6},{5,7},{6,4},{7,5},{8,10},{9,11},{10,... | collective-permute-start | bytes 393224 | tf_op jit(solution)/shard_map/ppermute | solution.py:13
